TPU v7x, 256 devices: a whole 4x4x8 slice. The times are simulated.
256 devices in a mesh: sub: 128 (over x_lo, y, z, core), depth: 2 (over x_hi).
Axes of the slice: x: 4 (x_hi: 2, x_lo: 2; x = x_hi * 2 + x_lo), y: 4, z: 8, core: 2. Of those that a mesh axis runs over, the one named last changes fastest.
Arguments:
- recharge: float32 [128, 2, 40, 128], P('sub', 'depth'), may hold values from -6 to 6
- inv_diag: float32 [128, 2, 40, 128, 128], P('sub', 'depth')
- couple: bfloat16 [128, 2, 40, 6, 128, 128], P('sub', 'depth'), may hold values from -0.09716797 to 0.09716797
- col_index: int32 [128, 2, 40, 6], P('sub', 'depth'), may hold values from 0 to 41, as said below
- soil_id: int32 [128, 2, 40], P('sub', 'depth'), may hold values from 0 to 11
- field_id: int32 [128, 2, 40], P('sub', 'depth'), may hold values from 0 to 4999
- robin_table: float32 [12], replicated, may hold values from 0.05 to 0.2
- field_rate: float32 [5000], replicated, may hold values from 0.1 to 2
- matching: int32 [4, 128], replicated, may hold values from 0 to 127, as said below
- lambda_in: float32 [128, 2, 4, 2, 128], P('sub', 'depth'), may hold values from -6 to 6
Outputs:
- state: float32 [128, 2, 40, 128], P('sub', 'depth')
- robin_data: float32 [128, 2, 4, 2, 128], P('sub', 'depth')
Inputs may be any that keep to these rules, and one draw needn't show every extreme that they name: Each row c pairs every subdomain s with another one, matching[c, s] != s, and matching[c, matching[c, s]] = s. `col_index`: A block row never names its own block; indices from 40 on name the other half's last 2 blocks in order.
All inputs are finite; a program needn't handle non-finite values.
Results may differ from a plain program's by a relative error of at most 0.0003.
Values sent between devices are 32-bit elements; how exact they have to be, the bound alone decides.
No kernel may reach another device: no remote copies, remote signals or barrier semaphores. Data moves between devices by JAX's collectives and lax.ppermute only.
A program may use at most 64 MiB of HBM per device.

v0:
```python
import functools

import jax
import jax.numpy as jnp
from jax import lax
from jax.experimental import pallas as pl
from jax.experimental.pallas import tpu as pltpu
from jax.sharding import PartitionSpec as P

G = 2
SWEEPS = 4
OUTER = 2


def partner(block, axis, bit):
    count = lax.axis_size(axis)
    route = []
    for low in range(count):
        high = low | 1 << bit
        if high != low and high < count:
            route += [(low, high), (high, low)]
    return lax.ppermute(block, axis, route)


def sweep_kernel(*refs, coupled_terms, first, blocks):
    if coupled_terms:
        cols_ref, c_ref, inv_ref, state_ref, ghost_ref, f_ref, p_ref, o_ref = refs
    else:
        inv_ref, f_ref, o_ref = refs
    rows = inv_ref.shape[0]
    base = (pl.program_id(0) + first) * rows
    for r in range(rows):
        y = f_ref[r]
        if coupled_terms:
            bands = c_ref.shape[1]
            row = base + r
            acc = None
            for b in range(bands):
                col = cols_ref[row * bands + b]
                own = state_ref[jnp.minimum(col, blocks - 1)]
                other = ghost_ref[jnp.maximum(col - blocks, 0)]
                xb = jnp.where(col >= blocks, other, own)
                term = c_ref[r, b].astype(jnp.float32) * xb
                acc = term if acc is None else acc + term
            y = y - jnp.sum(acc.T, axis=0, keepdims=True)
            y = y - p_ref[r] * state_ref[row]
        o_ref[r] = jnp.sum((inv_ref[r] * y).T, axis=0, keepdims=True)


def block_sweep(inv, forcing, rows, first, count, coupling=None):
    blocks, width = forcing.shape[0], forcing.shape[2]
    at = lambda g, *_: (g + first, 0, 0)
    if coupling is None:
        operands = [inv, forcing]
        specs = [pl.BlockSpec((rows, width, width), at), pl.BlockSpec((rows, 1, width), at)]
        prefetch = 0
        bands = 0
    else:
        cols, tile, state, ghost, prows = coupling
        bands = tile.shape[1]
        operands = [cols, tile, inv, state, ghost, forcing, prows]
        specs = [
            pl.BlockSpec((rows, bands, width, width), lambda g, *_: (g + first, 0, 0, 0)),
            pl.BlockSpec((rows, width, width), at),
            pl.BlockSpec(state.shape, lambda g, *_: (0, 0, 0)),
            pl.BlockSpec(ghost.shape, lambda g, *_: (0, 0, 0)),
            pl.BlockSpec((rows, 1, width), at),
            pl.BlockSpec((rows, 1, width), at),
        ]
        prefetch = 1
    done = count * rows
    grid_spec = pltpu.PrefetchScalarGridSpec(
        num_scalar_prefetch=prefetch,
        grid=(count,),
        in_specs=specs,
        out_specs=pl.BlockSpec((rows, 1, width), lambda g, *_: (g, 0, 0)),
    )
    return pl.pallas_call(
        functools.partial(sweep_kernel, coupled_terms=coupling is not None, first=first, blocks=blocks),
        grid_spec=grid_spec,
        out_shape=jax.ShapeDtypeStruct((done, 1, width), jnp.float32),
        cost_estimate=pl.CostEstimate(
            flops=2 * done * width * width * (bands + 1),
            transcendentals=0,
            bytes_accessed=done * width * width * (2 * bands + 4),
        ),
    )(*operands)


def doubling_order(bits):
    if bits == 7:
        return [3, 5, 2, 6, 4, 1, 0]
    return list(range(bits - 1, -1, -1))


def exchange(outgoing, partners):
    count = lax.axis_size("sub")
    bits = count.bit_length() - 1
    me = lax.axis_index("sub")
    if 1 << bits != count:
        every = lax.all_gather(outgoing, "sub", axis=0, tiled=False)
        return every[partners, jnp.arange(outgoing.shape[0])]
    order = doubling_order(bits)
    held = outgoing[None]
    for bit in order:
        route = [(low, low ^ (1 << bit)) for low in range(count)]
        held = jnp.concatenate([held, lax.ppermute(held, "sub", route)], axis=0)
    flipped = partners ^ me
    entry = jnp.zeros_like(partners)
    for step, bit in enumerate(order):
        entry = entry | (((flipped >> bit) & 1) << step)
    return held[entry, jnp.arange(outgoing.shape[0])]


def per_device(
    recharge,
    inv_diag,
    couple,
    col_index,
    soil_id,
    field_id,
    robin_table,
    field_rate,
    matching,
    lambda_in,
):
    blocks = recharge.shape[2]
    width = recharge.shape[3]
    colours = lambda_in.shape[2]
    per_colour = lambda_in.shape[3]
    iface = colours * per_colour
    nitrate = (jnp.arange(width) >= width // 2).astype(jnp.float32)
    rate = jnp.take(field_rate, field_id[0, 0], axis=0)
    rhs = recharge[0, 0] + rate[:, None] * nitrate
    soil_hits = soil_id[0, 0][:, None] == jnp.arange(robin_table.shape[0], dtype=jnp.int32)[None, :]
    p_block = jnp.sum(jnp.where(soil_hits, robin_table[None, :], 0.0), axis=1)
    p_face = p_block[:iface]
    inverse = inv_diag[0, 0]
    columns = col_index[0, 0]
    partners = lax.dynamic_index_in_dim(matching, lax.axis_index("sub"), axis=1, keepdims=False)
    robin_data = lambda_in[0, 0]

    flat_columns = columns.reshape(-1)
    prows = jnp.concatenate([p_face, jnp.zeros((blocks - iface,), jnp.float32)])[:, None, None] * jnp.ones((1, 1, width), jnp.float32)

    def sweep_rows(state, ghost, forcing, rows, first, count):
        if state is None:
            return block_sweep(inverse, forcing, rows, first, count)
        coupling = (flat_columns, couple[0, 0], state, ghost, prows)
        return block_sweep(inverse, forcing, rows, first, count, coupling)

    head_forcing = rhs[:, None]
    state = None
    ghost = None
    for outer in range(OUTER):
        forcing = jnp.concatenate([rhs[:iface] + robin_data.reshape(iface, width), rhs[iface:]], axis=0)[:, None]
        for sweep in range(SWEEPS):
            top = sweep_rows(state, ghost, head_forcing if blocks - G >= iface else forcing, G, (blocks - G) // G, 1)
            sent = partner(top, "depth", 0)
            state = sweep_rows(state, ghost, forcing, 8, 0, blocks // 8)
            ghost = sent
        state2 = state[:, 0]
        outgoing = (
            2.0
            * p_face.reshape(colours, per_colour)[..., None]
            * state2[:iface].reshape(colours, per_colour, width)
            - robin_data
        )
        robin_data = exchange(outgoing, partners)
    return (state[:, 0][None, None], robin_data[None, None])


def solution(mesh):
    placed = (
        P("sub", "depth", None, None),
        P("sub", "depth", None, None, None),
        P("sub", "depth", None, None, None, None),
        P("sub", "depth", None, None),
        P("sub", "depth", None),
        P("sub", "depth", None),
        P(),
        P(),
        P(),
        P("sub", "depth", None, None, None),
    )
    return jax.shard_map(
        per_device,
        mesh=mesh,
        in_specs=placed,
        out_specs=(P("sub", "depth", None, None), P("sub", "depth", None, None, None)),
        check_vma=False,
    )
```

profile of v0, /device:TPU:1, one launch (start us, length us, event | category | flops | bytes accessed | tf_op | source)
XLA Modules:
  0.0 176.5 jit_solution(4983335295466158447)
XLA Ops:
  2.8 1.4 multiply_add_fusion.refs_1_.refs_5_
  4.2 1.6 shard_map.114
  5.8 3.6 %collective-permute-start = (f32[2,1,128]{2,1,0:T(1,128)}, f32[2,1,128]{2,1,0:T(1,128)S(1)}, u32[]{:S(2)}, u32[]{:S(2)}) collective-permute-start(f32[2,1,128]{2,1,0:T(1,128)} %shard_map.114), channel_id=1, source_target_pairs={{0,1},{1,0},{2,3},{3,2},{4,5},{5,4},{6,7},{7,6},{8,9},{9,8},{10,11... | collective-permute-start | bytes 3080 | tf_op jit(solution)/shard_map/ppermute | solution.py:22
  14.3 4.4 %shard_map.113.refs_3_ = f32[40,1,128]{2,1,0:T(1,128)} custom-call(f32[40,128,128]{2,1,0:T(8,128)} %bitcast.44, f32[40,1,128]{2,1,0:T(1,128)} %bitcast.62), custom_call_target="tpu_custom_call" | custom-call | flops 1310720 | bytes 2621440 | tf_op jit(solution)/shard_map/pallas_call | solution.py:78
  19.5 2.6 %shard_map.116 = f32[2,1,128]{2,1,0:T(1,128)} custom-call(s32[240]{0:T(256)} %reshape_squeeze.6.refs_0_, bf16[40,6,128,128]{3,2,1,0:T(8,128)(2,1)} %bitcast.30, f32[40,128,128]{2,1,0:T(8,128)} %bitcast.45, f32[40,1,128]{2,1,0:T(1,128)} %shard_map.113.refs_3_, f32[2,1,128]{2,1,0:T(1,128)} %copy-done.5, f32[40,1,128]{2,1,0:T(1,128)} %multiply_add_fusion.refs_1_.refs_5_, ...), custom_call_target="tpu_custom_call" | custom-call | flops 458752 | bytes 524288 | tf_op jit(solution)/shard_map/pallas_call | solution.py:78
  22.1 7.8 %shard_map.115.refs_3_ = f32[40,1,128]{2,1,0:T(1,128)} custom-call(s32[240]{0:T(256)} %reshape_squeeze.6.refs_0_, bf16[40,6,128,128]{3,2,1,0:T(8,128)(2,1)} %bitcast.31, f32[40,128,128]{2,1,0:T(8,128)} %bitcast.46, f32[40,1,128]{2,1,0:T(1,128)} %shard_map.113.refs_3_, f32[2,1,128]{2,1,0:T(1,128)} %copy-done.5, f32[40,1,128]{2,1,0:T(1,128)} %bitcast.63, ...), custom_call_target="tpu_custom_call" | custom-call | flops 9175040 | bytes 10485760 | tf_op jit(solution)/shard_map/pallas_call | solution.py:78
  30.4 2.6 %shard_map.118 = f32[2,1,128]{2,1,0:T(1,128)} custom-call(s32[240]{0:T(256)} %reshape_squeeze.6.refs_0_, bf16[40,6,128,128]{3,2,1,0:T(8,128)(2,1)} %bitcast.32, f32[40,128,128]{2,1,0:T(8,128)} %bitcast.47, f32[40,1,128]{2,1,0:T(1,128)} %shard_map.115.refs_3_, f32[2,1,128]{2,1,0:T(1,128)} %copy-done.6, f32[40,1,128]{2,1,0:T(1,128)} %multiply_add_fusion.refs_1_.refs_5_, ...), custom_call_target="tpu_custom_call" | custom-call | flops 458752 | bytes 524288 | tf_op jit(solution)/shard_map/pallas_call | solution.py:78
  33.0 3.0 %collective-permute-start.2 = (f32[2,1,128]{2,1,0:T(1,128)}, f32[2,1,128]{2,1,0:T(1,128)S(1)}, u32[]{:S(2)}, u32[]{:S(2)}) collective-permute-start(f32[2,1,128]{2,1,0:T(1,128)} %shard_map.118), channel_id=1, source_target_pairs={{0,1},{1,0},{2,3},{3,2},{4,5},{5,4},{6,7},{7,6},{8,9},{9,8},{10,11... | collective-permute-start | bytes 3080 | tf_op jit(solution)/shard_map/ppermute | solution.py:22
  36.1 7.8 %shard_map.117.refs_3_ = f32[40,1,128]{2,1,0:T(1,128)} custom-call(s32[240]{0:T(256)} %reshape_squeeze.6.refs_0_, bf16[40,6,128,128]{3,2,1,0:T(8,128)(2,1)} %bitcast.33, f32[40,128,128]{2,1,0:T(8,128)} %bitcast.48, f32[40,1,128]{2,1,0:T(1,128)} %shard_map.115.refs_3_, f32[2,1,128]{2,1,0:T(1,128)} %copy-done.6, f32[40,1,128]{2,1,0:T(1,128)} %bitcast.64, ...), custom_call_target="tpu_custom_call" | custom-call | flops 9175040 | bytes 10485760 | tf_op jit(solution)/shard_map/pallas_call | solution.py:78
  44.5 7.8 %shard_map.119.refs_3_ = f32[40,1,128]{2,1,0:T(1,128)} custom-call(s32[240]{0:T(256)} %reshape_squeeze.6.refs_0_, bf16[40,6,128,128]{3,2,1,0:T(8,128)(2,1)} %bitcast.34, f32[40,128,128]{2,1,0:T(8,128)} %bitcast.49, f32[40,1,128]{2,1,0:T(1,128)} %shard_map.117.refs_3_, f32[2,1,128]{2,1,0:T(1,128)} %copy-done.2, f32[40,1,128]{2,1,0:T(1,128)} %bitcast.65, ...), custom_call_target="tpu_custom_call" | custom-call | flops 9175040 | bytes 10485760 | tf_op jit(solution)/shard_map/pallas_call | solution.py:78
  53.0 6.9 %collective-permute-start.4 = (f32[1,4,2,128]{3,2,1,0:T(2,128)S(1)}, f32[1,4,2,128]{3,2,1,0:T(2,128)S(1)}, u32[]{:S(2)}, u32[]{:S(2)}) collective-permute-start(f32[1,4,2,128]{3,2,1,0:T(2,128)S(1)} %get-tuple-element.5), channel_id=1, source_target_pairs={{0,16},{2,18},{4,20},{6,22},{8,24},{10,26},{12,28},{14,30},{16,0},... | collective-permute-start | bytes 12296 | tf_op jit(solution)/shard_map/ppermute | solution.py:107
  60.0 1.0 collective-permute-done.4
  61.0 2.9 %collective-permute-start.5 = (f32[2,4,2,128]{3,2,1,0:T(2,128)S(1)}, f32[2,4,2,128]{3,2,1,0:T(2,128)S(1)}, u32[]{:S(2)}, u32[]{:S(2)}) collective-permute-start(f32[2,4,2,128]{3,2,1,0:T(2,128)S(1)} %pad_maximum_fusion.6), channel_id=1, source_target_pairs={{0,64},{2,66},{4,68},{6,70},{8,72},{10,74},{12,76},{14,78},{16,80}... | collective-permute-start | bytes 24584 | tf_op jit(solution)/shard_map/ppermute | solution.py:107
  63.9 1.1 collective-permute-done.5
  65.0 1.5 collective-permute-start.6
  66.5 2.0 %collective-permute-done.6 = f32[4,4,2,128]{3,2,1,0:T(2,128)S(1)} collective-permute-done((f32[4,4,2,128]{3,2,1,0:T(2,128)S(1)}, f32[4,4,2,128]{3,2,1,0:T(2,128)S(1)}, u32[]{:S(2)}, u32[]{:S(2)}) %collective-permute-start.6) | collective-permute-done | bytes 16416 | tf_op jit(solution)/shard_map/ppermute | solution.py:107
  69.0 2.4 %collective-permute-done.7 = f32[8,4,2,128]{3,2,1,0:T(2,128)S(1)} collective-permute-done((f32[8,4,2,128]{3,2,1,0:T(2,128)S(1)}, f32[8,4,2,128]{3,2,1,0:T(2,128)S(1)}, u32[]{:S(2)}, u32[]{:S(2)}) %collective-permute-start.7) | collective-permute-done | bytes 32800 | tf_op jit(solution)/shard_map/ppermute | solution.py:107
  71.5 1.4 collective-permute-start.8
  72.9 1.8 %collective-permute-done.8 = f32[16,4,2,128]{3,2,1,0:T(2,128)S(1)} collective-permute-done((f32[16,4,2,128]{3,2,1,0:T(2,128)S(1)}, f32[16,4,2,128]{3,2,1,0:T(2,128)S(1)}, u32[]{:S(2)}, u32[]{:S(2)}) %collective-permute-start.8) | collective-permute-done | bytes 65568 | tf_op jit(solution)/shard_map/ppermute | solution.py:107
  74.8 0.8 collective-permute-start.9
  75.6 3.1 %collective-permute-done.9 = f32[32,4,2,128]{3,2,1,0:T(2,128)S(1)} collective-permute-done((f32[32,4,2,128]{3,2,1,0:T(2,128)S(1)}, f32[32,4,2,128]{3,2,1,0:T(2,128)S(1)}, u32[]{:S(2)}, u32[]{:S(2)}) %collective-permute-start.9) | collective-permute-done | bytes 131104 | tf_op jit(solution)/shard_map/ppermute | solution.py:107
  78.8 8.2 %collective-permute-start.10 = (f32[64,4,2,128]{3,2,1,0:T(2,128)S(1)}, f32[64,4,2,128]{3,2,1,0:T(2,128)S(1)}, u32[]{:S(2)}, u32[]{:S(2)}) collective-permute-start(f32[64,4,2,128]{3,2,1,0:T(2,128)S(1)} %get-tuple-element.8), channel_id=1, source_target_pairs={{0,2},{2,0},{4,6},{6,4},{8,10},{10,8},{12,14},{14,12},{16,18},{18,... | collective-permute-start | bytes 786440 | tf_op jit(solution)/shard_map/ppermute | solution.py:107
  87.0 2.6 %shard_map.120 = f32[2,1,128]{2,1,0:T(1,128)} custom-call(s32[240]{0:T(256)} %reshape_squeeze.6.refs_0_, bf16[40,6,128,128]{3,2,1,0:T(8,128)(2,1)} %bitcast.35, f32[40,128,128]{2,1,0:T(8,128)} %bitcast.50, f32[40,1,128]{2,1,0:T(1,128)} %shard_map.117.refs_3_, f32[2,1,128]{2,1,0:T(1,128)} %copy-done.2, f32[40,1,128]{2,1,0:T(1,128)} %multiply_add_fusion.refs_1_.refs_5_, ...), custom_call_target="tpu_custom_call" | custom-call | flops 458752 | bytes 524288 | tf_op jit(solution)/shard_map/pallas_call | solution.py:78
  89.6 0.9 collective-permute-start.3
  90.6 3.1 %collective-permute-done.3.refs_4_ = f32[2,1,128]{2,1,0:T(1,128)S(1)} collective-permute-done((f32[2,1,128]{2,1,0:T(1,128)}, f32[2,1,128]{2,1,0:T(1,128)S(1)}, u32[]{:S(2)}, u32[]{:S(2)}) %collective-permute-start.3) | collective-permute-done | bytes 1056 | tf_op jit(solution)/shard_map/ppermute | solution.py:22
  94.3 2.6 %shard_map.122 = f32[2,1,128]{2,1,0:T(1,128)} custom-call(s32[240]{0:T(256)} %reshape_squeeze.6.refs_0_, bf16[40,6,128,128]{3,2,1,0:T(8,128)(2,1)} %bitcast.36, f32[40,128,128]{2,1,0:T(8,128)} %bitcast.51, f32[40,1,128]{2,1,0:T(1,128)} %shard_map.119.refs_3_, f32[2,1,128]{2,1,0:T(1,128)} %copy-done.3, f32[40,1,128]{2,1,0:T(1,128)} %multiply_add_fusion.refs_1_.refs_5_, ...), custom_call_target="tpu_custom_call" | custom-call | flops 458752 | bytes 524288 | tf_op jit(solution)/shard_map/pallas_call | solution.py:78
  96.9 0.9 collective-permute-start.11
  99.0 7.8 %shard_map.121.refs_3_ = f32[40,1,128]{2,1,0:T(1,128)} custom-call(s32[240]{0:T(256)} %reshape_squeeze.6.refs_0_, bf16[40,6,128,128]{3,2,1,0:T(8,128)(2,1)} %bitcast.37, f32[40,128,128]{2,1,0:T(8,128)} %bitcast.52, f32[40,1,128]{2,1,0:T(1,128)} %shard_map.119.refs_3_, f32[2,1,128]{2,1,0:T(1,128)} %copy-done.3, f32[40,1,128]{2,1,0:T(1,128)} %bitcast.58, ...), custom_call_target="tpu_custom_call" | custom-call | flops 9175040 | bytes 10485760 | tf_op jit(solution)/shard_map/pallas_call | solution.py:78
  107.3 2.6 %shard_map.124 = f32[2,1,128]{2,1,0:T(1,128)} custom-call(s32[240]{0:T(256)} %reshape_squeeze.6.refs_0_, bf16[40,6,128,128]{3,2,1,0:T(8,128)(2,1)} %bitcast.38, f32[40,128,128]{2,1,0:T(8,128)} %bitcast.53, f32[40,1,128]{2,1,0:T(1,128)} %shard_map.121.refs_3_, f32[2,1,128]{2,1,0:T(1,128)} %copy-done.4, f32[40,1,128]{2,1,0:T(1,128)} %multiply_add_fusion.refs_1_.refs_5_, ...), custom_call_target="tpu_custom_call" | custom-call | flops 458752 | bytes 524288 | tf_op jit(solution)/shard_map/pallas_call | solution.py:78
  110.0 2.1 %collective-permute-start.12 = (f32[2,1,128]{2,1,0:T(1,128)}, f32[2,1,128]{2,1,0:T(1,128)S(1)}, u32[]{:S(2)}, u32[]{:S(2)}) collective-permute-start(f32[2,1,128]{2,1,0:T(1,128)} %shard_map.124), channel_id=1, source_target_pairs={{0,1},{1,0},{2,3},{3,2},{4,5},{5,4},{6,7},{7,6},{8,9},{9,8},{10,11... | collective-permute-start | bytes 3080 | tf_op jit(solution)/shard_map/ppermute | solution.py:22
  112.1 7.8 %shard_map.123.refs_3_ = f32[40,1,128]{2,1,0:T(1,128)} custom-call(s32[240]{0:T(256)} %reshape_squeeze.6.refs_0_, bf16[40,6,128,128]{3,2,1,0:T(8,128)(2,1)} %bitcast.39, f32[40,128,128]{2,1,0:T(8,128)} %bitcast.54, f32[40,1,128]{2,1,0:T(1,128)} %shard_map.121.refs_3_, f32[2,1,128]{2,1,0:T(1,128)} %copy-done.4, f32[40,1,128]{2,1,0:T(1,128)} %bitcast.59, ...), custom_call_target="tpu_custom_call" | custom-call | flops 9175040 | bytes 10485760 | tf_op jit(solution)/shard_map/pallas_call | solution.py:78
  120.4 2.6 %shard_map.126 = f32[2,1,128]{2,1,0:T(1,128)} custom-call(s32[240]{0:T(256)} %reshape_squeeze.6.refs_0_, bf16[40,6,128,128]{3,2,1,0:T(8,128)(2,1)} %bitcast.40, f32[40,128,128]{2,1,0:T(8,128)} %bitcast.55, f32[40,1,128]{2,1,0:T(1,128)} %shard_map.123.refs_3_, f32[2,1,128]{2,1,0:T(1,128)} %copy-done.7, f32[40,1,128]{2,1,0:T(1,128)} %multiply_add_fusion.refs_1_.refs_5_, ...), custom_call_target="tpu_custom_call" | custom-call | flops 458752 | bytes 524288 | tf_op jit(solution)/shard_map/pallas_call | solution.py:78
  123.0 0.9 collective-permute-start.13
  123.9 7.8 %shard_map.125.refs_3_ = f32[40,1,128]{2,1,0:T(1,128)} custom-call(s32[240]{0:T(256)} %reshape_squeeze.6.refs_0_, bf16[40,6,128,128]{3,2,1,0:T(8,128)(2,1)} %bitcast.41, f32[40,128,128]{2,1,0:T(8,128)} %bitcast.56, f32[40,1,128]{2,1,0:T(1,128)} %shard_map.123.refs_3_, f32[2,1,128]{2,1,0:T(1,128)} %copy-done.7, f32[40,1,128]{2,1,0:T(1,128)} %bitcast.60, ...), custom_call_target="tpu_custom_call" | custom-call | flops 9175040 | bytes 10485760 | tf_op jit(solution)/shard_map/pallas_call | solution.py:78
  132.3 7.8 %shard_map.127 = f32[40,1,128]{2,1,0:T(1,128)} custom-call(s32[240]{0:T(256)} %reshape_squeeze.6.refs_0_, bf16[40,6,128,128]{3,2,1,0:T(8,128)(2,1)} %bitcast.42, f32[40,128,128]{2,1,0:T(8,128)} %bitcast.57, f32[40,1,128]{2,1,0:T(1,128)} %shard_map.125.refs_3_, f32[2,1,128]{2,1,0:T(1,128)} %copy-done.9, f32[40,1,128]{2,1,0:T(1,128)} %bitcast.61, ...), custom_call_target="tpu_custom_call" | custom-call | flops 9175040 | bytes 10485760 | tf_op jit(solution)/shard_map/pallas_call | solution.py:78
  140.8 5.1 %collective-permute-start.14 = (f32[1,4,2,128]{3,2,1,0:T(2,128)S(1)}, f32[1,4,2,128]{3,2,1,0:T(2,128)S(1)}, u32[]{:S(2)}, u32[]{:S(2)}) collective-permute-start(f32[1,4,2,128]{3,2,1,0:T(2,128)S(1)} %get-tuple-element.3), channel_id=1, source_target_pairs={{0,16},{2,18},{4,20},{6,22},{8,24},{10,26},{12,28},{14,30},{16,0},... | collective-permute-start | bytes 12296 | tf_op jit(solution)/shard_map/ppermute | solution.py:107
  145.9 1.3 collective-permute-done.14
  147.2 2.6 %collective-permute-start.15 = (f32[2,4,2,128]{3,2,1,0:T(2,128)S(1)}, f32[2,4,2,128]{3,2,1,0:T(2,128)S(1)}, u32[]{:S(2)}, u32[]{:S(2)}) collective-permute-start(f32[2,4,2,128]{3,2,1,0:T(2,128)S(1)} %pad_maximum_fusion.7), channel_id=1, source_target_pairs={{0,64},{2,66},{4,68},{6,70},{8,72},{10,74},{12,76},{14,78},{16,80}... | collective-permute-start | bytes 24584 | tf_op jit(solution)/shard_map/ppermute | solution.py:107
  149.9 1.3 collective-permute-done.15
  151.2 1.3 collective-permute-start.16
  152.5 2.6 %collective-permute-done.16 = f32[4,4,2,128]{3,2,1,0:T(2,128)S(1)} collective-permute-done((f32[4,4,2,128]{3,2,1,0:T(2,128)S(1)}, f32[4,4,2,128]{3,2,1,0:T(2,128)S(1)}, u32[]{:S(2)}, u32[]{:S(2)}) %collective-permute-start.16) | collective-permute-done | bytes 16416 | tf_op jit(solution)/shard_map/ppermute | solution.py:107
  155.9 2.1 %collective-permute-done.17 = f32[8,4,2,128]{3,2,1,0:T(2,128)S(1)} collective-permute-done((f32[8,4,2,128]{3,2,1,0:T(2,128)S(1)}, f32[8,4,2,128]{3,2,1,0:T(2,128)S(1)}, u32[]{:S(2)}, u32[]{:S(2)}) %collective-permute-start.17) | collective-permute-done | bytes 32800 | tf_op jit(solution)/shard_map/ppermute | solution.py:107
  158.0 0.9 collective-permute-start.18
  158.9 2.3 %collective-permute-done.18 = f32[16,4,2,128]{3,2,1,0:T(2,128)S(1)} collective-permute-done((f32[16,4,2,128]{3,2,1,0:T(2,128)S(1)}, f32[16,4,2,128]{3,2,1,0:T(2,128)S(1)}, u32[]{:S(2)}, u32[]{:S(2)}) %collective-permute-start.18) | collective-permute-done | bytes 65568 | tf_op jit(solution)/shard_map/ppermute | solution.py:107
  161.6 3.6 %collective-permute-done.19 = f32[32,4,2,128]{3,2,1,0:T(2,128)S(1)} collective-permute-done((f32[32,4,2,128]{3,2,1,0:T(2,128)S(1)}, f32[32,4,2,128]{3,2,1,0:T(2,128)S(1)}, u32[]{:S(2)}, u32[]{:S(2)}) %collective-permute-start.19) | collective-permute-done | bytes 131104 | tf_op jit(solution)/shard_map/ppermute | solution.py:107
  165.3 8.8 %collective-permute-start.20 = (f32[64,4,2,128]{3,2,1,0:T(2,128)S(1)}, f32[64,4,2,128]{3,2,1,0:T(2,128)S(1)}, u32[]{:S(2)}, u32[]{:S(2)}) collective-permute-start(f32[64,4,2,128]{3,2,1,0:T(2,128)S(1)} %get-tuple-element.6), channel_id=1, source_target_pairs={{0,2},{2,0},{4,6},{6,4},{8,10},{10,8},{12,14},{14,12},{16,18},{18,... | collective-permute-start | bytes 786440 | tf_op jit(solution)/shard_map/ppermute | solution.py:107
  174.1 1.2 collective-permute-done.20
  175.3 1.2 gather_fusion.2
  (77 shorter events, 16.3 us)
Async XLA Ops:
  0.6 0.7 copy-start
  5.8 13.0 %collective-permute-start = (f32[2,1,128]{2,1,0:T(1,128)}, f32[2,1,128]{2,1,0:T(1,128)S(1)}, u32[]{:S(2)}, u32[]{:S(2)}) collective-permute-start(f32[2,1,128]{2,1,0:T(1,128)} %shard_map.114), channel_id=1, source_target_pairs={{0,1},{1,0},{2,3},{3,2},{4,5},{5,4},{6,7},{7,6},{8,9},{9,8},{10,11... | collective-permute-start | bytes 3080 | tf_op jit(solution)/shard_map/ppermute | solution.py:22
  18.7 0.7 copy-start.5
  22.1 7.8 %collective-permute-start.1 = (f32[2,1,128]{2,1,0:T(1,128)}, f32[2,1,128]{2,1,0:T(1,128)S(1)}, u32[]{:S(2)}, u32[]{:S(2)}) collective-permute-start(f32[2,1,128]{2,1,0:T(1,128)} %shard_map.116), channel_id=1, source_target_pairs={{0,1},{1,0},{2,3},{3,2},{4,5},{5,4},{6,7},{7,6},{8,9},{9,8},{10,11... | collective-permute-start | bytes 3080 | tf_op jit(solution)/shard_map/ppermute | solution.py:22
  29.9 0.6 copy-start.6
  33.0 10.8 %collective-permute-start.2 = (f32[2,1,128]{2,1,0:T(1,128)}, f32[2,1,128]{2,1,0:T(1,128)S(1)}, u32[]{:S(2)}, u32[]{:S(2)}) collective-permute-start(f32[2,1,128]{2,1,0:T(1,128)} %shard_map.118), channel_id=1, source_target_pairs={{0,1},{1,0},{2,3},{3,2},{4,5},{5,4},{6,7},{7,6},{8,9},{9,8},{10,11... | collective-permute-start | bytes 3080 | tf_op jit(solution)/shard_map/ppermute | solution.py:22
  43.9 9.1 %copy-start.1 = (f32[1,1,4,2,128]{4,3,2,1,0:T(2,128)S(1)}, f32[1,1,4,2,128]{4,3,2,1,0:T(2,128)}, u32[]{:S(2)}) copy-start(f32[1,1,4,2,128]{4,3,2,1,0:T(2,128)} %param.19) | copy-start | bytes 12292
  43.9 0.6 copy-start.2
  52.3 38.2 %copy-start.8 = (s32[4,128]{1,0:T(4,128)S(1)}, s32[4,128]{1,0:T(4,128)}, u32[]{:S(2)}) copy-start(s32[4,128]{1,0:T(4,128)} %param.18) | copy-start | bytes 6148
  53.0 7.9 %collective-permute-start.4 = (f32[1,4,2,128]{3,2,1,0:T(2,128)S(1)}, f32[1,4,2,128]{3,2,1,0:T(2,128)S(1)}, u32[]{:S(2)}, u32[]{:S(2)}) collective-permute-start(f32[1,4,2,128]{3,2,1,0:T(2,128)S(1)} %get-tuple-element.5), channel_id=1, source_target_pairs={{0,16},{2,18},{4,20},{6,22},{8,24},{10,26},{12,28},{14,30},{16,0},... | collective-permute-start | bytes 12296 | tf_op jit(solution)/shard_map/ppermute | solution.py:107
  61.0 4.0 %collective-permute-start.5 = (f32[2,4,2,128]{3,2,1,0:T(2,128)S(1)}, f32[2,4,2,128]{3,2,1,0:T(2,128)S(1)}, u32[]{:S(2)}, u32[]{:S(2)}) collective-permute-start(f32[2,4,2,128]{3,2,1,0:T(2,128)S(1)} %pad_maximum_fusion.6), channel_id=1, source_target_pairs={{0,64},{2,66},{4,68},{6,70},{8,72},{10,74},{12,76},{14,78},{16,80}... | collective-permute-start | bytes 24584 | tf_op jit(solution)/shard_map/ppermute | solution.py:107
  65.0 3.6 %collective-permute-start.6 = (f32[4,4,2,128]{3,2,1,0:T(2,128)S(1)}, f32[4,4,2,128]{3,2,1,0:T(2,128)S(1)}, u32[]{:S(2)}, u32[]{:S(2)}) collective-permute-start(f32[4,4,2,128]{3,2,1,0:T(2,128)S(1)} %pad_maximum_fusion.4), channel_id=1, source_target_pairs={{0,8},{2,10},{4,12},{6,14},{8,0},{10,2},{12,4},{14,6},{16,24},{18,... | collective-permute-start | bytes 49160 | tf_op jit(solution)/shard_map/ppermute | solution.py:107
  68.6 2.9 %collective-permute-start.7 = (f32[8,4,2,128]{3,2,1,0:T(2,128)S(1)}, f32[8,4,2,128]{3,2,1,0:T(2,128)S(1)}, u32[]{:S(2)}, u32[]{:S(2)}) collective-permute-start(f32[8,4,2,128]{3,2,1,0:T(2,128)S(1)} %pad_maximum_fusion), channel_id=1, source_target_pairs={{0,128},{2,130},{4,132},{6,134},{8,136},{10,138},{12,140},{14,142}... | collective-permute-start | bytes 98312 | tf_op jit(solution)/shard_map/ppermute | solution.py:107
  71.5 3.2 %collective-permute-start.8 = (f32[16,4,2,128]{3,2,1,0:T(2,128)S(1)}, f32[16,4,2,128]{3,2,1,0:T(2,128)S(1)}, u32[]{:S(2)}, u32[]{:S(2)}) collective-permute-start(f32[16,4,2,128]{3,2,1,0:T(2,128)S(1)} %get-tuple-element.23), channel_id=1, source_target_pairs={{0,32},{2,34},{4,36},{6,38},{8,40},{10,42},{12,44},{14,46},{16,48}... | collective-permute-start | bytes 196616 | tf_op jit(solution)/shard_map/ppermute | solution.py:107
  74.8 3.9 %collective-permute-start.9 = (f32[32,4,2,128]{3,2,1,0:T(2,128)S(1)}, f32[32,4,2,128]{3,2,1,0:T(2,128)S(1)}, u32[]{:S(2)}, u32[]{:S(2)}) collective-permute-start(f32[32,4,2,128]{3,2,1,0:T(2,128)S(1)} %get-tuple-element.15), channel_id=1, source_target_pairs={{0,4},{2,6},{4,0},{6,2},{8,12},{10,14},{12,8},{14,10},{16,20},{18,... | collective-permute-start | bytes 393224 | tf_op jit(solution)/shard_map/ppermute | solution.py:107
  78.8 19.0 %collective-permute-start.10 = (f32[64,4,2,128]{3,2,1,0:T(2,128)S(1)}, f32[64,4,2,128]{3,2,1,0:T(2,128)S(1)}, u32[]{:S(2)}, u32[]{:S(2)}) collective-permute-start(f32[64,4,2,128]{3,2,1,0:T(2,128)S(1)} %get-tuple-element.8), channel_id=1, source_target_pairs={{0,2},{2,0},{4,6},{6,4},{8,10},{10,8},{12,14},{14,12},{16,18},{18,... | collective-permute-start | bytes 786440 | tf_op jit(solution)/shard_map/ppermute | solution.py:107
  89.6 4.1 %collective-permute-start.3 = (f32[2,1,128]{2,1,0:T(1,128)}, f32[2,1,128]{2,1,0:T(1,128)S(1)}, u32[]{:S(2)}, u32[]{:S(2)}) collective-permute-start(f32[2,1,128]{2,1,0:T(1,128)} %shard_map.120), channel_id=1, source_target_pairs={{0,1},{1,0},{2,3},{3,2},{4,5},{5,4},{6,7},{7,6},{8,9},{9,8},{10,11... | collective-permute-start | bytes 3080 | tf_op jit(solution)/shard_map/ppermute | solution.py:22
  93.7 0.6 copy-start.3
  96.9 9.9 %collective-permute-start.11 = (f32[2,1,128]{2,1,0:T(1,128)}, f32[2,1,128]{2,1,0:T(1,128)S(1)}, u32[]{:S(2)}, u32[]{:S(2)}) collective-permute-start(f32[2,1,128]{2,1,0:T(1,128)} %shard_map.122), channel_id=1, source_target_pairs={{0,1},{1,0},{2,3},{3,2},{4,5},{5,4},{6,7},{7,6},{8,9},{9,8},{10,11... | collective-permute-start | bytes 3080 | tf_op jit(solution)/shard_map/ppermute | solution.py:22
  106.8 0.6 copy-start.4
  110.0 9.9 %collective-permute-start.12 = (f32[2,1,128]{2,1,0:T(1,128)}, f32[2,1,128]{2,1,0:T(1,128)S(1)}, u32[]{:S(2)}, u32[]{:S(2)}) collective-permute-start(f32[2,1,128]{2,1,0:T(1,128)} %shard_map.124), channel_id=1, source_target_pairs={{0,1},{1,0},{2,3},{3,2},{4,5},{5,4},{6,7},{7,6},{8,9},{9,8},{10,11... | collective-permute-start | bytes 3080 | tf_op jit(solution)/shard_map/ppermute | solution.py:22
  119.9 0.6 copy-start.7
  123.0 8.7 %collective-permute-start.13 = (f32[2,1,128]{2,1,0:T(1,128)}, f32[2,1,128]{2,1,0:T(1,128)S(1)}, u32[]{:S(2)}, u32[]{:S(2)}) collective-permute-start(f32[2,1,128]{2,1,0:T(1,128)} %shard_map.126), channel_id=1, source_target_pairs={{0,1},{1,0},{2,3},{3,2},{4,5},{5,4},{6,7},{7,6},{8,9},{9,8},{10,11... | collective-permute-start | bytes 3080 | tf_op jit(solution)/shard_map/ppermute | solution.py:22
  131.7 0.6 copy-start.9
  140.8 6.4 %collective-permute-start.14 = (f32[1,4,2,128]{3,2,1,0:T(2,128)S(1)}, f32[1,4,2,128]{3,2,1,0:T(2,128)S(1)}, u32[]{:S(2)}, u32[]{:S(2)}) collective-permute-start(f32[1,4,2,128]{3,2,1,0:T(2,128)S(1)} %get-tuple-element.3), channel_id=1, source_target_pairs={{0,16},{2,18},{4,20},{6,22},{8,24},{10,26},{12,28},{14,30},{16,0},... | collective-permute-start | bytes 12296 | tf_op jit(solution)/shard_map/ppermute | solution.py:107
  147.2 4.0 %collective-permute-start.15 = (f32[2,4,2,128]{3,2,1,0:T(2,128)S(1)}, f32[2,4,2,128]{3,2,1,0:T(2,128)S(1)}, u32[]{:S(2)}, u32[]{:S(2)}) collective-permute-start(f32[2,4,2,128]{3,2,1,0:T(2,128)S(1)} %pad_maximum_fusion.7), channel_id=1, source_target_pairs={{0,64},{2,66},{4,68},{6,70},{8,72},{10,74},{12,76},{14,78},{16,80}... | collective-permute-start | bytes 24584 | tf_op jit(solution)/shard_map/ppermute | solution.py:107
  151.2 3.9 %collective-permute-start.16 = (f32[4,4,2,128]{3,2,1,0:T(2,128)S(1)}, f32[4,4,2,128]{3,2,1,0:T(2,128)S(1)}, u32[]{:S(2)}, u32[]{:S(2)}) collective-permute-start(f32[4,4,2,128]{3,2,1,0:T(2,128)S(1)} %pad_maximum_fusion.5), channel_id=1, source_target_pairs={{0,8},{2,10},{4,12},{6,14},{8,0},{10,2},{12,4},{14,6},{16,24},{18,... | collective-permute-start | bytes 49160 | tf_op jit(solution)/shard_map/ppermute | solution.py:107
  155.1 2.9 %collective-permute-start.17 = (f32[8,4,2,128]{3,2,1,0:T(2,128)S(1)}, f32[8,4,2,128]{3,2,1,0:T(2,128)S(1)}, u32[]{:S(2)}, u32[]{:S(2)}) collective-permute-start(f32[8,4,2,128]{3,2,1,0:T(2,128)S(1)} %pad_maximum_fusion.1), channel_id=1, source_target_pairs={{0,128},{2,130},{4,132},{6,134},{8,136},{10,138},{12,140},{14,142}... | collective-permute-start | bytes 98312 | tf_op jit(solution)/shard_map/ppermute | solution.py:107
  158.0 3.2 %collective-permute-start.18 = (f32[16,4,2,128]{3,2,1,0:T(2,128)S(1)}, f32[16,4,2,128]{3,2,1,0:T(2,128)S(1)}, u32[]{:S(2)}, u32[]{:S(2)}) collective-permute-start(f32[16,4,2,128]{3,2,1,0:T(2,128)S(1)} %get-tuple-element.19), channel_id=1, source_target_pairs={{0,32},{2,34},{4,36},{6,38},{8,40},{10,42},{12,44},{14,46},{16,48}... | collective-permute-start | bytes 196616 | tf_op jit(solution)/shard_map/ppermute | solution.py:107
  161.3 3.9 %collective-permute-start.19 = (f32[32,4,2,128]{3,2,1,0:T(2,128)S(1)}, f32[32,4,2,128]{3,2,1,0:T(2,128)S(1)}, u32[]{:S(2)}, u32[]{:S(2)}) collective-permute-start(f32[32,4,2,128]{3,2,1,0:T(2,128)S(1)} %get-tuple-element.12), channel_id=1, source_target_pairs={{0,4},{2,6},{4,0},{6,2},{8,12},{10,14},{12,8},{14,10},{16,20},{18,... | collective-permute-start | bytes 393224 | tf_op jit(solution)/shard_map/ppermute | solution.py:107
  165.3 10.0 %collective-permute-start.20 = (f32[64,4,2,128]{3,2,1,0:T(2,128)S(1)}, f32[64,4,2,128]{3,2,1,0:T(2,128)S(1)}, u32[]{:S(2)}, u32[]{:S(2)}) collective-permute-start(f32[64,4,2,128]{3,2,1,0:T(2,128)S(1)} %get-tuple-element.6), channel_id=1, source_target_pairs={{0,2},{2,0},{4,6},{6,4},{8,10},{10,8},{12,14},{14,12},{16,18},{18,... | collective-permute-start | bytes 786440 | tf_op jit(solution)/shard_map/ppermute | solution.py:107
where the time goes:
time: 178 us; the launch traced here: 176 us
  Pallas kernels  76.1 us (43%)
  starting transfers between devices  53.2 us (30%)
  waiting for transfers between devices  28.9 us (16%)
  local copies, waits for them, and re-layouts  10.2 us (6%)
  other arithmetic  7.3 us (4%)
    pallas_call x15, Pallas kernels, block_sweep(): pl.pallas_call(functools.partial(sweep_kernel, coupled_terms=coupling is...  76.1 us
    ppermute x14, starting transfers between devices, exchange(): held = jnp.concatenate([held, lax.ppermute(held, 'sub', route)], axis=0)  41.9 us
    ppermute x14, waiting for transfers between devices, exchange(): held = jnp.concatenate([held, lax.ppermute(held, 'sub', route)], axis=0)  25.8 us
    ppermute x7, starting transfers between devices, partner(): return lax.ppermute(block, axis, route)  11.2 us
    unnamed x33, local copies, waits for them, and re-layouts  4.56 us
  transfers between devices with their start and end apart: 21, of which 14 were waited for; matrix products, arithmetic and copies ran while one was open for 4% of the time, Pallas kernels for 28%

commit v1 on v0

--- a/solution.py
+++ b/solution.py
@@ -93,23 +93,31 @@
     return list(range(bits - 1, -1, -1))
 
 
-def exchange(outgoing, partners):
+def exchange(outgoing, partners, tie=None, midway=None):
     count = lax.axis_size("sub")
     bits = count.bit_length() - 1
     me = lax.axis_index("sub")
+    extra = None
+    if tie is not None:
+        outgoing, tie = lax.optimization_barrier((outgoing, tie))
     if 1 << bits != count:
         every = lax.all_gather(outgoing, "sub", axis=0, tiled=False)
-        return every[partners, jnp.arange(outgoing.shape[0])]
+        if midway is not None:
+            extra = midway()
+        return every[partners, jnp.arange(outgoing.shape[0])], extra
     order = doubling_order(bits)
     held = outgoing[None]
-    for bit in order:
+    for step, bit in enumerate(order):
         route = [(low, low ^ (1 << bit)) for low in range(count)]
         held = jnp.concatenate([held, lax.ppermute(held, "sub", route)], axis=0)
+        if midway is not None and step == min(2, len(order) - 1):
+            extra = midway()
+            held, extra = lax.optimization_barrier((held, extra))
     flipped = partners ^ me
     entry = jnp.zeros_like(partners)
     for step, bit in enumerate(order):
         entry = entry | (((flipped >> bit) & 1) << step)
-    return held[entry, jnp.arange(outgoing.shape[0])]
+    return held[entry, jnp.arange(outgoing.shape[0])], extra
 
 
 def per_device(
@@ -150,12 +158,17 @@
         return block_sweep(inverse, forcing, rows, first, count, coupling)
 
     head_forcing = rhs[:, None]
+    head_source = lambda forcing: head_forcing if blocks - G >= iface else forcing
+    pending = None
     state = None
     ghost = None
     for outer in range(OUTER):
         forcing = jnp.concatenate([rhs[:iface] + robin_data.reshape(iface, width), rhs[iface:]], axis=0)[:, None]
         for sweep in range(SWEEPS):
-            top = sweep_rows(state, ghost, head_forcing if blocks - G >= iface else forcing, G, (blocks - G) // G, 1)
+            if pending is not None:
+                top, pending = pending, None
+            else:
+                top = sweep_rows(state, ghost, head_source(forcing), G, (blocks - G) // G, 1)
             sent = partner(top, "depth", 0)
             state = sweep_rows(state, ghost, forcing, 8, 0, blocks // 8)
             ghost = sent
@@ -166,7 +179,11 @@
             * state2[:iface].reshape(colours, per_colour, width)
             - robin_data
         )
-        robin_data = exchange(outgoing, partners)
+        if outer < OUTER - 1 and blocks - G >= iface:
+            ahead = lambda state=state, ghost=ghost: sweep_rows(state, ghost, head_forcing, G, (blocks - G) // G, 1)
+            robin_data, pending = exchange(outgoing, partners, tie=top, midway=ahead)
+        else:
+            robin_data, _ = exchange(outgoing, partners)
     return (state[:, 0][None, None], robin_data[None, None])
 
 

time: 178 us -> 175 us (0.983)
  waiting for transfers between devices: 28.9 us -> 25.5 us
    ppermute x14, waiting for transfers between devices: 25.8 us -> 21.6 us  [exchange(): held = jnp.concatenate([held, lax.ppermute(held, 'sub', route)], axis=0)]
    ppermute x14, starting transfers between devices: 41.9 us -> 43.8 us  [exchange(): held = jnp.concatenate([held, lax.ppermute(held, 'sub', route)], axis=0)]
    unnamed x33 -> x31, local copies, waits for them, and re-layouts: 4.56 us -> 4.3 us
  transfers between devices with their start and end apart: 21 -> 21, of which waited for: 14 -> 14; matrix products, arithmetic and copies ran while one was open for 4% -> 4% of each run, Pallas kernels for 28% -> 26%
where the time goes in v1:
time: 175 us; the launch traced here: 174 us
  Pallas kernels  76.1 us (43%)
  starting transfers between devices  54.2 us (31%)
  waiting for transfers between devices  25.5 us (15%)
  local copies, waits for them, and re-layouts  9.8 us (6%)
  other arithmetic  7.52 us (4%)
    pallas_call x15, Pallas kernels, block_sweep(): pl.pallas_call(functools.partial(sweep_kernel, coupled_terms=coupling is...  76.1 us
    ppermute x14, starting transfers between devices, exchange(): held = jnp.concatenate([held, lax.ppermute(held, 'sub', route)], axis=0)  43.8 us
    ppermute x14, waiting for transfers between devices, exchange(): held = jnp.concatenate([held, lax.ppermute(held, 'sub', route)], axis=0)  21.6 us
    ppermute x7, starting transfers between devices, partner(): return lax.ppermute(block, axis, route)  10.4 us
    unnamed x31, local copies, waits for them, and re-layouts  4.3 us
    ppermute x7, waiting for transfers between devices, partner(): return lax.ppermute(block, axis, route)  3.92 us
  transfers between devices with their start and end apart: 21, of which 14 were waited for; matrix products, arithmetic and copies ran while one was open for 4% of the time, Pallas kernels for 26%

profile of v1, /device:TPU:1, one launch (start us, length us, event | category | flops | bytes accessed | tf_op | source)
XLA Modules:
  0.0 173.9 jit_solution(10151718028181869350)
XLA Ops:
  1.4 0.8 gather_fusion
  2.8 1.4 multiply_add_fusion.refs_1_.refs_5_
  4.2 1.6 shard_map.114
  5.8 3.6 %collective-permute-start = (f32[2,1,128]{2,1,0:T(1,128)}, f32[2,1,128]{2,1,0:T(1,128)S(1)}, u32[]{:S(2)}, u32[]{:S(2)}) collective-permute-start(f32[2,1,128]{2,1,0:T(1,128)} %shard_map.114), channel_id=1, source_target_pairs={{0,1},{1,0},{2,3},{3,2},{4,5},{5,4},{6,7},{7,6},{8,9},{9,8},{10,11... | collective-permute-start | bytes 3080 | tf_op jit(solution)/shard_map/ppermute | solution.py:22
  9.4 0.8 bitcast_add_fusion
  14.4 4.4 %shard_map.113.refs_3_ = f32[40,1,128]{2,1,0:T(1,128)} custom-call(f32[40,128,128]{2,1,0:T(8,128)} %bitcast.44, f32[40,1,128]{2,1,0:T(1,128)} %bitcast.62), custom_call_target="tpu_custom_call" | custom-call | flops 1310720 | bytes 2621440 | tf_op jit(solution)/shard_map/pallas_call | solution.py:78
  19.5 2.6 %shard_map.116 = f32[2,1,128]{2,1,0:T(1,128)} custom-call(s32[240]{0:T(256)} %reshape_squeeze.6.refs_0_, bf16[40,6,128,128]{3,2,1,0:T(8,128)(2,1)} %bitcast.30, f32[40,128,128]{2,1,0:T(8,128)} %bitcast.45, f32[40,1,128]{2,1,0:T(1,128)} %shard_map.113.refs_3_, f32[2,1,128]{2,1,0:T(1,128)} %copy-done.4, f32[40,1,128]{2,1,0:T(1,128)} %multiply_add_fusion.refs_1_.refs_5_, ...), custom_call_target="tpu_custom_call" | custom-call | flops 458752 | bytes 524288 | tf_op jit(solution)/shard_map/pallas_call | solution.py:78
  22.1 7.8 %shard_map.115.refs_3_ = f32[40,1,128]{2,1,0:T(1,128)} custom-call(s32[240]{0:T(256)} %reshape_squeeze.6.refs_0_, bf16[40,6,128,128]{3,2,1,0:T(8,128)(2,1)} %bitcast.31, f32[40,128,128]{2,1,0:T(8,128)} %bitcast.46, f32[40,1,128]{2,1,0:T(1,128)} %shard_map.113.refs_3_, f32[2,1,128]{2,1,0:T(1,128)} %copy-done.4, f32[40,1,128]{2,1,0:T(1,128)} %bitcast.63, ...), custom_call_target="tpu_custom_call" | custom-call | flops 9175040 | bytes 10485760 | tf_op jit(solution)/shard_map/pallas_call | solution.py:78
  30.4 2.6 %shard_map.118 = f32[2,1,128]{2,1,0:T(1,128)} custom-call(s32[240]{0:T(256)} %reshape_squeeze.6.refs_0_, bf16[40,6,128,128]{3,2,1,0:T(8,128)(2,1)} %bitcast.32, f32[40,128,128]{2,1,0:T(8,128)} %bitcast.47, f32[40,1,128]{2,1,0:T(1,128)} %shard_map.115.refs_3_, f32[2,1,128]{2,1,0:T(1,128)} %copy-done.5, f32[40,1,128]{2,1,0:T(1,128)} %multiply_add_fusion.refs_1_.refs_5_, ...), custom_call_target="tpu_custom_call" | custom-call | flops 458752 | bytes 524288 | tf_op jit(solution)/shard_map/pallas_call | solution.py:78
  33.0 3.0 %collective-permute-start.2 = (f32[2,1,128]{2,1,0:T(1,128)}, f32[2,1,128]{2,1,0:T(1,128)S(1)}, u32[]{:S(2)}, u32[]{:S(2)}) collective-permute-start(f32[2,1,128]{2,1,0:T(1,128)} %shard_map.118), channel_id=1, source_target_pairs={{0,1},{1,0},{2,3},{3,2},{4,5},{5,4},{6,7},{7,6},{8,9},{9,8},{10,11... | collective-permute-start | bytes 3080 | tf_op jit(solution)/shard_map/ppermute | solution.py:22
  36.1 7.8 %shard_map.117.refs_3_ = f32[40,1,128]{2,1,0:T(1,128)} custom-call(s32[240]{0:T(256)} %reshape_squeeze.6.refs_0_, bf16[40,6,128,128]{3,2,1,0:T(8,128)(2,1)} %bitcast.33, f32[40,128,128]{2,1,0:T(8,128)} %bitcast.48, f32[40,1,128]{2,1,0:T(1,128)} %shard_map.115.refs_3_, f32[2,1,128]{2,1,0:T(1,128)} %copy-done.5, f32[40,1,128]{2,1,0:T(1,128)} %bitcast.64, ...), custom_call_target="tpu_custom_call" | custom-call | flops 9175040 | bytes 10485760 | tf_op jit(solution)/shard_map/pallas_call | solution.py:78
  44.4 7.8 %shard_map.119.refs_3_ = f32[40,1,128]{2,1,0:T(1,128)} custom-call(s32[240]{0:T(256)} %reshape_squeeze.6.refs_0_, bf16[40,6,128,128]{3,2,1,0:T(8,128)(2,1)} %bitcast.34, f32[40,128,128]{2,1,0:T(8,128)} %bitcast.49, f32[40,1,128]{2,1,0:T(1,128)} %shard_map.117.refs_3_, f32[2,1,128]{2,1,0:T(1,128)} %copy-done.6, f32[40,1,128]{2,1,0:T(1,128)} %bitcast.65, ...), custom_call_target="tpu_custom_call" | custom-call | flops 9175040 | bytes 10485760 | tf_op jit(solution)/shard_map/pallas_call | solution.py:78
  53.0 2.6 %shard_map.120 = f32[2,1,128]{2,1,0:T(1,128)} custom-call(s32[240]{0:T(256)} %reshape_squeeze.6.refs_0_, bf16[40,6,128,128]{3,2,1,0:T(8,128)(2,1)} %bitcast.35, f32[40,128,128]{2,1,0:T(8,128)} %bitcast.50, f32[40,1,128]{2,1,0:T(1,128)} %shard_map.117.refs_3_, f32[2,1,128]{2,1,0:T(1,128)} %copy-done.6, f32[40,1,128]{2,1,0:T(1,128)} %multiply_add_fusion.refs_1_.refs_5_, ...), custom_call_target="tpu_custom_call" | custom-call | flops 458752 | bytes 524288 | tf_op jit(solution)/shard_map/pallas_call | solution.py:78
  55.6 6.9 %collective-permute-start.4 = (f32[1,4,2,128]{3,2,1,0:T(2,128)S(1)}, f32[1,4,2,128]{3,2,1,0:T(2,128)S(1)}, u32[]{:S(2)}, u32[]{:S(2)}) collective-permute-start(f32[1,4,2,128]{3,2,1,0:T(2,128)S(1)} %bitcast.67), channel_id=1, source_target_pairs={{0,16},{2,18},{4,20},{6,22},{8,24},{10,26},{12,28},{14,30},{16,0},... | collective-permute-start | bytes 12296 | tf_op jit(solution)/shard_map/ppermute | solution.py:112
  62.5 1.0 collective-permute-done.4
  63.5 2.9 %collective-permute-start.5 = (f32[2,4,2,128]{3,2,1,0:T(2,128)S(1)}, f32[2,4,2,128]{3,2,1,0:T(2,128)S(1)}, u32[]{:S(2)}, u32[]{:S(2)}) collective-permute-start(f32[2,4,2,128]{3,2,1,0:T(2,128)S(1)} %pad_maximum_fusion.9), channel_id=1, source_target_pairs={{0,64},{2,66},{4,68},{6,70},{8,72},{10,74},{12,76},{14,78},{16,80}... | collective-permute-start | bytes 24584 | tf_op jit(solution)/shard_map/ppermute | solution.py:112
  66.4 1.1 collective-permute-done.5
  67.5 1.5 collective-permute-start.6
  69.3 3.9 %collective-permute-done.3.refs_4_ = f32[2,1,128]{2,1,0:T(1,128)S(1)} collective-permute-done((f32[2,1,128]{2,1,0:T(1,128)}, f32[2,1,128]{2,1,0:T(1,128)S(1)}, u32[]{:S(2)}, u32[]{:S(2)}) %collective-permute-start.3) | collective-permute-done | bytes 1056 | tf_op jit(solution)/shard_map/ppermute | solution.py:22
  73.7 2.6 %shard_map.121 = f32[2,1,128]{2,1,0:T(1,128)} custom-call(s32[240]{0:T(256)} %reshape_squeeze.6.refs_0_, bf16[40,6,128,128]{3,2,1,0:T(8,128)(2,1)} %bitcast.36, f32[40,128,128]{2,1,0:T(8,128)} %bitcast.51, f32[40,1,128]{2,1,0:T(1,128)} %shard_map.119.refs_3_, f32[2,1,128]{2,1,0:T(1,128)} %copy-done.2, f32[40,1,128]{2,1,0:T(1,128)} %multiply_add_fusion.refs_1_.refs_5_, ...), custom_call_target="tpu_custom_call" | custom-call | flops 458752 | bytes 524288 | tf_op jit(solution)/shard_map/pallas_call | solution.py:78
  76.8 2.5 %collective-permute-done.7 = f32[8,4,2,128]{3,2,1,0:T(2,128)S(1)} collective-permute-done((f32[8,4,2,128]{3,2,1,0:T(2,128)S(1)}, f32[8,4,2,128]{3,2,1,0:T(2,128)S(1)}, u32[]{:S(2)}, u32[]{:S(2)}) %collective-permute-start.7) | collective-permute-done | bytes 32800 | tf_op jit(solution)/shard_map/ppermute | solution.py:112
  79.2 1.4 collective-permute-start.8
  80.6 1.8 %collective-permute-done.8 = f32[16,4,2,128]{3,2,1,0:T(2,128)S(1)} collective-permute-done((f32[16,4,2,128]{3,2,1,0:T(2,128)S(1)}, f32[16,4,2,128]{3,2,1,0:T(2,128)S(1)}, u32[]{:S(2)}, u32[]{:S(2)}) %collective-permute-start.8) | collective-permute-done | bytes 65568 | tf_op jit(solution)/shard_map/ppermute | solution.py:112
  82.5 1.7 collective-permute-start.9
  85.1 1.5 collective-permute-done.9
  86.7 8.6 %collective-permute-start.10 = (f32[64,4,2,128]{3,2,1,0:T(2,128)S(1)}, f32[64,4,2,128]{3,2,1,0:T(2,128)S(1)}, u32[]{:S(2)}, u32[]{:S(2)}) collective-permute-start(f32[64,4,2,128]{3,2,1,0:T(2,128)S(1)} %pad_maximum_fusion), channel_id=1, source_target_pairs={{0,2},{2,0},{4,6},{6,4},{8,10},{10,8},{12,14},{14,12},{16,18},{18,... | collective-permute-start | bytes 786440 | tf_op jit(solution)/shard_map/ppermute | solution.py:112
  95.4 1.1 collective-permute-done.10
  97.7 7.8 %shard_map.122.refs_3_ = f32[40,1,128]{2,1,0:T(1,128)} custom-call(s32[240]{0:T(256)} %reshape_squeeze.6.refs_0_, bf16[40,6,128,128]{3,2,1,0:T(8,128)(2,1)} %bitcast.37, f32[40,128,128]{2,1,0:T(8,128)} %bitcast.52, f32[40,1,128]{2,1,0:T(1,128)} %shard_map.119.refs_3_, f32[2,1,128]{2,1,0:T(1,128)} %copy-done.2, f32[40,1,128]{2,1,0:T(1,128)} %bitcast.58, ...), custom_call_target="tpu_custom_call" | custom-call | flops 9175040 | bytes 10485760 | tf_op jit(solution)/shard_map/pallas_call | solution.py:78
  106.0 2.6 %shard_map.124 = f32[2,1,128]{2,1,0:T(1,128)} custom-call(s32[240]{0:T(256)} %reshape_squeeze.6.refs_0_, bf16[40,6,128,128]{3,2,1,0:T(8,128)(2,1)} %bitcast.38, f32[40,128,128]{2,1,0:T(8,128)} %bitcast.53, f32[40,1,128]{2,1,0:T(1,128)} %shard_map.122.refs_3_, f32[2,1,128]{2,1,0:T(1,128)} %copy-done.3, f32[40,1,128]{2,1,0:T(1,128)} %multiply_add_fusion.refs_1_.refs_5_, ...), custom_call_target="tpu_custom_call" | custom-call | flops 458752 | bytes 524288 | tf_op jit(solution)/shard_map/pallas_call | solution.py:78
  109.1 7.8 %shard_map.123.refs_3_ = f32[40,1,128]{2,1,0:T(1,128)} custom-call(s32[240]{0:T(256)} %reshape_squeeze.6.refs_0_, bf16[40,6,128,128]{3,2,1,0:T(8,128)(2,1)} %bitcast.39, f32[40,128,128]{2,1,0:T(8,128)} %bitcast.54, f32[40,1,128]{2,1,0:T(1,128)} %shard_map.122.refs_3_, f32[2,1,128]{2,1,0:T(1,128)} %copy-done.3, f32[40,1,128]{2,1,0:T(1,128)} %bitcast.59, ...), custom_call_target="tpu_custom_call" | custom-call | flops 9175040 | bytes 10485760 | tf_op jit(solution)/shard_map/pallas_call | solution.py:78
  117.5 2.6 %shard_map.126 = f32[2,1,128]{2,1,0:T(1,128)} custom-call(s32[240]{0:T(256)} %reshape_squeeze.6.refs_0_, bf16[40,6,128,128]{3,2,1,0:T(8,128)(2,1)} %bitcast.40, f32[40,128,128]{2,1,0:T(8,128)} %bitcast.55, f32[40,1,128]{2,1,0:T(1,128)} %shard_map.123.refs_3_, f32[2,1,128]{2,1,0:T(1,128)} %copy-done.7, f32[40,1,128]{2,1,0:T(1,128)} %multiply_add_fusion.refs_1_.refs_5_, ...), custom_call_target="tpu_custom_call" | custom-call | flops 458752 | bytes 524288 | tf_op jit(solution)/shard_map/pallas_call | solution.py:78
  120.0 2.5 %collective-permute-start.13 = (f32[2,1,128]{2,1,0:T(1,128)}, f32[2,1,128]{2,1,0:T(1,128)S(1)}, u32[]{:S(2)}, u32[]{:S(2)}) collective-permute-start(f32[2,1,128]{2,1,0:T(1,128)} %shard_map.126), channel_id=1, source_target_pairs={{0,1},{1,0},{2,3},{3,2},{4,5},{5,4},{6,7},{7,6},{8,9},{9,8},{10,11... | collective-permute-start | bytes 3080 | tf_op jit(solution)/shard_map/ppermute | solution.py:22
  122.5 7.8 %shard_map.125.refs_3_ = f32[40,1,128]{2,1,0:T(1,128)} custom-call(s32[240]{0:T(256)} %reshape_squeeze.6.refs_0_, bf16[40,6,128,128]{3,2,1,0:T(8,128)(2,1)} %bitcast.41, f32[40,128,128]{2,1,0:T(8,128)} %bitcast.56, f32[40,1,128]{2,1,0:T(1,128)} %shard_map.123.refs_3_, f32[2,1,128]{2,1,0:T(1,128)} %copy-done.7, f32[40,1,128]{2,1,0:T(1,128)} %bitcast.60, ...), custom_call_target="tpu_custom_call" | custom-call | flops 9175040 | bytes 10485760 | tf_op jit(solution)/shard_map/pallas_call | solution.py:78
  130.9 7.8 %shard_map.127 = f32[40,1,128]{2,1,0:T(1,128)} custom-call(s32[240]{0:T(256)} %reshape_squeeze.6.refs_0_, bf16[40,6,128,128]{3,2,1,0:T(8,128)(2,1)} %bitcast.42, f32[40,128,128]{2,1,0:T(8,128)} %bitcast.57, f32[40,1,128]{2,1,0:T(1,128)} %shard_map.125.refs_3_, f32[2,1,128]{2,1,0:T(1,128)} %copy-done.9, f32[40,1,128]{2,1,0:T(1,128)} %bitcast.61, ...), custom_call_target="tpu_custom_call" | custom-call | flops 9175040 | bytes 10485760 | tf_op jit(solution)/shard_map/pallas_call | solution.py:78
  139.4 5.1 %collective-permute-start.14 = (f32[1,4,2,128]{3,2,1,0:T(2,128)S(1)}, f32[1,4,2,128]{3,2,1,0:T(2,128)S(1)}, u32[]{:S(2)}, u32[]{:S(2)}) collective-permute-start(f32[1,4,2,128]{3,2,1,0:T(2,128)S(1)} %get-tuple-element.9), channel_id=1, source_target_pairs={{0,16},{2,18},{4,20},{6,22},{8,24},{10,26},{12,28},{14,30},{16,0},... | collective-permute-start | bytes 12296 | tf_op jit(solution)/shard_map/ppermute | solution.py:112
  144.6 1.2 collective-permute-done.14
  145.8 2.9 %collective-permute-start.15 = (f32[2,4,2,128]{3,2,1,0:T(2,128)S(1)}, f32[2,4,2,128]{3,2,1,0:T(2,128)S(1)}, u32[]{:S(2)}, u32[]{:S(2)}) collective-permute-start(f32[2,4,2,128]{3,2,1,0:T(2,128)S(1)} %pad_maximum_fusion.10), channel_id=1, source_target_pairs={{0,64},{2,66},{4,68},{6,70},{8,72},{10,74},{12,76},{14,78},{16,80}... | collective-permute-start | bytes 24584 | tf_op jit(solution)/shard_map/ppermute | solution.py:112
  148.7 1.1 collective-permute-done.15
  149.8 1.0 collective-permute-start.16
  150.9 2.5 %collective-permute-done.16 = f32[4,4,2,128]{3,2,1,0:T(2,128)S(1)} collective-permute-done((f32[4,4,2,128]{3,2,1,0:T(2,128)S(1)}, f32[4,4,2,128]{3,2,1,0:T(2,128)S(1)}, u32[]{:S(2)}, u32[]{:S(2)}) %collective-permute-start.16) | collective-permute-done | bytes 16416 | tf_op jit(solution)/shard_map/ppermute | solution.py:112
  153.9 2.4 %collective-permute-done.17 = f32[8,4,2,128]{3,2,1,0:T(2,128)S(1)} collective-permute-done((f32[8,4,2,128]{3,2,1,0:T(2,128)S(1)}, f32[8,4,2,128]{3,2,1,0:T(2,128)S(1)}, u32[]{:S(2)}, u32[]{:S(2)}) %collective-permute-start.17) | collective-permute-done | bytes 32800 | tf_op jit(solution)/shard_map/ppermute | solution.py:112
  156.3 1.4 collective-permute-start.18
  157.7 1.8 %collective-permute-done.18 = f32[16,4,2,128]{3,2,1,0:T(2,128)S(1)} collective-permute-done((f32[16,4,2,128]{3,2,1,0:T(2,128)S(1)}, f32[16,4,2,128]{3,2,1,0:T(2,128)S(1)}, u32[]{:S(2)}, u32[]{:S(2)}) %collective-permute-start.18) | collective-permute-done | bytes 65568 | tf_op jit(solution)/shard_map/ppermute | solution.py:112
  159.6 1.7 collective-permute-start.19
  161.3 2.4 %collective-permute-done.19 = f32[32,4,2,128]{3,2,1,0:T(2,128)S(1)} collective-permute-done((f32[32,4,2,128]{3,2,1,0:T(2,128)S(1)}, f32[32,4,2,128]{3,2,1,0:T(2,128)S(1)}, u32[]{:S(2)}, u32[]{:S(2)}) %collective-permute-start.19) | collective-permute-done | bytes 131104 | tf_op jit(solution)/shard_map/ppermute | solution.py:112
  163.8 7.7 %collective-permute-start.20 = (f32[64,4,2,128]{3,2,1,0:T(2,128)S(1)}, f32[64,4,2,128]{3,2,1,0:T(2,128)S(1)}, u32[]{:S(2)}, u32[]{:S(2)}) collective-permute-start(f32[64,4,2,128]{3,2,1,0:T(2,128)S(1)} %get-tuple-element.10), channel_id=1, source_target_pairs={{0,2},{2,0},{4,6},{6,4},{8,10},{10,8},{12,14},{14,12},{16,18},{18,... | collective-permute-start | bytes 786440 | tf_op jit(solution)/shard_map/ppermute | solution.py:112
  171.5 1.2 collective-permute-done.20
  172.7 1.2 gather_fusion.2
  (77 shorter events, 15.3 us)
Async XLA Ops:
  0.6 0.7 copy-start
  5.8 13.0 %collective-permute-start = (f32[2,1,128]{2,1,0:T(1,128)}, f32[2,1,128]{2,1,0:T(1,128)S(1)}, u32[]{:S(2)}, u32[]{:S(2)}) collective-permute-start(f32[2,1,128]{2,1,0:T(1,128)} %shard_map.114), channel_id=1, source_target_pairs={{0,1},{1,0},{2,3},{3,2},{4,5},{5,4},{6,7},{7,6},{8,9},{9,8},{10,11... | collective-permute-start | bytes 3080 | tf_op jit(solution)/shard_map/ppermute | solution.py:22
  18.8 0.7 copy-start.4
  22.1 7.8 %collective-permute-start.1 = (f32[2,1,128]{2,1,0:T(1,128)}, f32[2,1,128]{2,1,0:T(1,128)S(1)}, u32[]{:S(2)}, u32[]{:S(2)}) collective-permute-start(f32[2,1,128]{2,1,0:T(1,128)} %shard_map.116), channel_id=1, source_target_pairs={{0,1},{1,0},{2,3},{3,2},{4,5},{5,4},{6,7},{7,6},{8,9},{9,8},{10,11... | collective-permute-start | bytes 3080 | tf_op jit(solution)/shard_map/ppermute | solution.py:22
  29.9 0.5 copy-start.5
  33.0 10.9 %collective-permute-start.2 = (f32[2,1,128]{2,1,0:T(1,128)}, f32[2,1,128]{2,1,0:T(1,128)S(1)}, u32[]{:S(2)}, u32[]{:S(2)}) collective-permute-start(f32[2,1,128]{2,1,0:T(1,128)} %shard_map.118), channel_id=1, source_target_pairs={{0,1},{1,0},{2,3},{3,2},{4,5},{5,4},{6,7},{7,6},{8,9},{9,8},{10,11... | collective-permute-start | bytes 3080 | tf_op jit(solution)/shard_map/ppermute | solution.py:22
  43.9 9.1 %copy-start.1 = (f32[1,1,4,2,128]{4,3,2,1,0:T(2,128)S(1)}, f32[1,1,4,2,128]{4,3,2,1,0:T(2,128)}, u32[]{:S(2)}) copy-start(f32[1,1,4,2,128]{4,3,2,1,0:T(2,128)} %param.19) | copy-start | bytes 12292
  43.9 0.6 copy-start.6
  55.6 28.6 %copy-start.8 = (s32[4,128]{1,0:T(4,128)S(1)}, s32[4,128]{1,0:T(4,128)}, u32[]{:S(2)}) copy-start(s32[4,128]{1,0:T(4,128)} %param.18) | copy-start | bytes 6148
  55.6 7.9 %collective-permute-start.4 = (f32[1,4,2,128]{3,2,1,0:T(2,128)S(1)}, f32[1,4,2,128]{3,2,1,0:T(2,128)S(1)}, u32[]{:S(2)}, u32[]{:S(2)}) collective-permute-start(f32[1,4,2,128]{3,2,1,0:T(2,128)S(1)} %bitcast.67), channel_id=1, source_target_pairs={{0,16},{2,18},{4,20},{6,22},{8,24},{10,26},{12,28},{14,30},{16,0},... | collective-permute-start | bytes 12296 | tf_op jit(solution)/shard_map/ppermute | solution.py:112
  63.5 4.0 %collective-permute-start.5 = (f32[2,4,2,128]{3,2,1,0:T(2,128)S(1)}, f32[2,4,2,128]{3,2,1,0:T(2,128)S(1)}, u32[]{:S(2)}, u32[]{:S(2)}) collective-permute-start(f32[2,4,2,128]{3,2,1,0:T(2,128)S(1)} %pad_maximum_fusion.9), channel_id=1, source_target_pairs={{0,64},{2,66},{4,68},{6,70},{8,72},{10,74},{12,76},{14,78},{16,80}... | collective-permute-start | bytes 24584 | tf_op jit(solution)/shard_map/ppermute | solution.py:112
  67.5 8.8 %collective-permute-start.6 = (f32[4,4,2,128]{3,2,1,0:T(2,128)S(1)}, f32[4,4,2,128]{3,2,1,0:T(2,128)S(1)}, u32[]{:S(2)}, u32[]{:S(2)}) collective-permute-start(f32[4,4,2,128]{3,2,1,0:T(2,128)S(1)} %pad_maximum_fusion.7), channel_id=1, source_target_pairs={{0,8},{2,10},{4,12},{6,14},{8,0},{10,2},{12,4},{14,6},{16,24},{18,... | collective-permute-start | bytes 49160 | tf_op jit(solution)/shard_map/ppermute | solution.py:112
  69.1 4.1 %collective-permute-start.3 = (f32[2,1,128]{2,1,0:T(1,128)}, f32[2,1,128]{2,1,0:T(1,128)S(1)}, u32[]{:S(2)}, u32[]{:S(2)}) collective-permute-start(f32[2,1,128]{2,1,0:T(1,128)} %shard_map.120), channel_id=1, source_target_pairs={{0,1},{1,0},{2,3},{3,2},{4,5},{5,4},{6,7},{7,6},{8,9},{9,8},{10,11... | collective-permute-start | bytes 3080 | tf_op jit(solution)/shard_map/ppermute | solution.py:22
  73.2 0.5 copy-start.2
  76.4 2.9 %collective-permute-start.7 = (f32[8,4,2,128]{3,2,1,0:T(2,128)S(1)}, f32[8,4,2,128]{3,2,1,0:T(2,128)S(1)}, u32[]{:S(2)}, u32[]{:S(2)}) collective-permute-start(f32[8,4,2,128]{3,2,1,0:T(2,128)S(1)} %pad_maximum_fusion.3), channel_id=1, source_target_pairs={{0,128},{2,130},{4,132},{6,134},{8,136},{10,138},{12,140},{14,142}... | collective-permute-start | bytes 98312 | tf_op jit(solution)/shard_map/ppermute | solution.py:112
  79.2 3.2 %collective-permute-start.8 = (f32[16,4,2,128]{3,2,1,0:T(2,128)S(1)}, f32[16,4,2,128]{3,2,1,0:T(2,128)S(1)}, u32[]{:S(2)}, u32[]{:S(2)}) collective-permute-start(f32[16,4,2,128]{3,2,1,0:T(2,128)S(1)} %pad_maximum_fusion.2), channel_id=1, source_target_pairs={{0,32},{2,34},{4,36},{6,38},{8,40},{10,42},{12,44},{14,46},{16,48}... | collective-permute-start | bytes 196616 | tf_op jit(solution)/shard_map/ppermute | solution.py:112
  82.5 4.1 %collective-permute-start.9 = (f32[32,4,2,128]{3,2,1,0:T(2,128)S(1)}, f32[32,4,2,128]{3,2,1,0:T(2,128)S(1)}, u32[]{:S(2)}, u32[]{:S(2)}) collective-permute-start(f32[32,4,2,128]{3,2,1,0:T(2,128)S(1)} %pad_maximum_fusion.1), channel_id=1, source_target_pairs={{0,4},{2,6},{4,0},{6,2},{8,12},{10,14},{12,8},{14,10},{16,20},{18,... | collective-permute-start | bytes 393224 | tf_op jit(solution)/shard_map/ppermute | solution.py:112
  84.4 21.1 %collective-permute-start.11 = (f32[2,1,128]{2,1,0:T(1,128)}, f32[2,1,128]{2,1,0:T(1,128)S(1)}, u32[]{:S(2)}, u32[]{:S(2)}) collective-permute-start(f32[2,1,128]{2,1,0:T(1,128)} %shard_map.121), channel_id=1, source_target_pairs={{0,1},{1,0},{2,3},{3,2},{4,5},{5,4},{6,7},{7,6},{8,9},{9,8},{10,11... | collective-permute-start | bytes 3080 | tf_op jit(solution)/shard_map/ppermute | solution.py:22
  86.7 9.8 %collective-permute-start.10 = (f32[64,4,2,128]{3,2,1,0:T(2,128)S(1)}, f32[64,4,2,128]{3,2,1,0:T(2,128)S(1)}, u32[]{:S(2)}, u32[]{:S(2)}) collective-permute-start(f32[64,4,2,128]{3,2,1,0:T(2,128)S(1)} %pad_maximum_fusion), channel_id=1, source_target_pairs={{0,2},{2,0},{4,6},{6,4},{8,10},{10,8},{12,14},{14,12},{16,18},{18,... | collective-permute-start | bytes 786440 | tf_op jit(solution)/shard_map/ppermute | solution.py:112
  105.5 0.5 copy-start.3
  108.6 8.3 %collective-permute-start.12 = (f32[2,1,128]{2,1,0:T(1,128)}, f32[2,1,128]{2,1,0:T(1,128)S(1)}, u32[]{:S(2)}, u32[]{:S(2)}) collective-permute-start(f32[2,1,128]{2,1,0:T(1,128)} %shard_map.124), channel_id=1, source_target_pairs={{0,1},{1,0},{2,3},{3,2},{4,5},{5,4},{6,7},{7,6},{8,9},{9,8},{10,11... | collective-permute-start | bytes 3080 | tf_op jit(solution)/shard_map/ppermute | solution.py:22
  116.9 0.6 copy-start.7
  120.0 10.3 %collective-permute-start.13 = (f32[2,1,128]{2,1,0:T(1,128)}, f32[2,1,128]{2,1,0:T(1,128)S(1)}, u32[]{:S(2)}, u32[]{:S(2)}) collective-permute-start(f32[2,1,128]{2,1,0:T(1,128)} %shard_map.126), channel_id=1, source_target_pairs={{0,1},{1,0},{2,3},{3,2},{4,5},{5,4},{6,7},{7,6},{8,9},{9,8},{10,11... | collective-permute-start | bytes 3080 | tf_op jit(solution)/shard_map/ppermute | solution.py:22
  130.3 0.5 copy-start.9
  139.4 6.4 %collective-permute-start.14 = (f32[1,4,2,128]{3,2,1,0:T(2,128)S(1)}, f32[1,4,2,128]{3,2,1,0:T(2,128)S(1)}, u32[]{:S(2)}, u32[]{:S(2)}) collective-permute-start(f32[1,4,2,128]{3,2,1,0:T(2,128)S(1)} %get-tuple-element.9), channel_id=1, source_target_pairs={{0,16},{2,18},{4,20},{6,22},{8,24},{10,26},{12,28},{14,30},{16,0},... | collective-permute-start | bytes 12296 | tf_op jit(solution)/shard_map/ppermute | solution.py:112
  145.8 4.0 %collective-permute-start.15 = (f32[2,4,2,128]{3,2,1,0:T(2,128)S(1)}, f32[2,4,2,128]{3,2,1,0:T(2,128)S(1)}, u32[]{:S(2)}, u32[]{:S(2)}) collective-permute-start(f32[2,4,2,128]{3,2,1,0:T(2,128)S(1)} %pad_maximum_fusion.10), channel_id=1, source_target_pairs={{0,64},{2,66},{4,68},{6,70},{8,72},{10,74},{12,76},{14,78},{16,80}... | collective-permute-start | bytes 24584 | tf_op jit(solution)/shard_map/ppermute | solution.py:112
  149.8 3.6 %collective-permute-start.16 = (f32[4,4,2,128]{3,2,1,0:T(2,128)S(1)}, f32[4,4,2,128]{3,2,1,0:T(2,128)S(1)}, u32[]{:S(2)}, u32[]{:S(2)}) collective-permute-start(f32[4,4,2,128]{3,2,1,0:T(2,128)S(1)} %pad_maximum_fusion.8), channel_id=1, source_target_pairs={{0,8},{2,10},{4,12},{6,14},{8,0},{10,2},{12,4},{14,6},{16,24},{18,... | collective-permute-start | bytes 49160 | tf_op jit(solution)/shard_map/ppermute | solution.py:112
  153.4 2.9 %collective-permute-start.17 = (f32[8,4,2,128]{3,2,1,0:T(2,128)S(1)}, f32[8,4,2,128]{3,2,1,0:T(2,128)S(1)}, u32[]{:S(2)}, u32[]{:S(2)}) collective-permute-start(f32[8,4,2,128]{3,2,1,0:T(2,128)S(1)} %pad_maximum_fusion.4), channel_id=1, source_target_pairs={{0,128},{2,130},{4,132},{6,134},{8,136},{10,138},{12,140},{14,142}... | collective-permute-start | bytes 98312 | tf_op jit(solution)/shard_map/ppermute | solution.py:112
  156.3 3.2 %collective-permute-start.18 = (f32[16,4,2,128]{3,2,1,0:T(2,128)S(1)}, f32[16,4,2,128]{3,2,1,0:T(2,128)S(1)}, u32[]{:S(2)}, u32[]{:S(2)}) collective-permute-start(f32[16,4,2,128]{3,2,1,0:T(2,128)S(1)} %get-tuple-element.18), channel_id=1, source_target_pairs={{0,32},{2,34},{4,36},{6,38},{8,40},{10,42},{12,44},{14,46},{16,48}... | collective-permute-start | bytes 196616 | tf_op jit(solution)/shard_map/ppermute | solution.py:112
  159.6 4.1 %collective-permute-start.19 = (f32[32,4,2,128]{3,2,1,0:T(2,128)S(1)}, f32[32,4,2,128]{3,2,1,0:T(2,128)S(1)}, u32[]{:S(2)}, u32[]{:S(2)}) collective-permute-start(f32[32,4,2,128]{3,2,1,0:T(2,128)S(1)} %get-tuple-element.14), channel_id=1, source_target_pairs={{0,4},{2,6},{4,0},{6,2},{8,12},{10,14},{12,8},{14,10},{16,20},{18,... | collective-permute-start | bytes 393224 | tf_op jit(solution)/shard_map/ppermute | solution.py:112
  163.8 8.9 %collective-permute-start.20 = (f32[64,4,2,128]{3,2,1,0:T(2,128)S(1)}, f32[64,4,2,128]{3,2,1,0:T(2,128)S(1)}, u32[]{:S(2)}, u32[]{:S(2)}) collective-permute-start(f32[64,4,2,128]{3,2,1,0:T(2,128)S(1)} %get-tuple-element.10), channel_id=1, source_target_pairs={{0,2},{2,0},{4,6},{6,4},{8,10},{10,8},{12,14},{14,12},{16,18},{18,... | collective-permute-start | bytes 786440 | tf_op jit(solution)/shard_map/ppermute | solution.py:112

commit v2 on v1

--- a/solution.py
+++ b/solution.py
@@ -93,26 +93,26 @@
     return list(range(bits - 1, -1, -1))
 
 
-def exchange(outgoing, partners, tie=None, midway=None):
+def exchange(outgoing, partners, tie=None, hooks=()):
     count = lax.axis_size("sub")
     bits = count.bit_length() - 1
     me = lax.axis_index("sub")
-    extra = None
+    extra = [None] * len(hooks)
     if tie is not None:
         outgoing, tie = lax.optimization_barrier((outgoing, tie))
     if 1 << bits != count:
         every = lax.all_gather(outgoing, "sub", axis=0, tiled=False)
-        if midway is not None:
-            extra = midway()
+        extra = [hook() for _, hook in hooks]
         return every[partners, jnp.arange(outgoing.shape[0])], extra
     order = doubling_order(bits)
     held = outgoing[None]
     for step, bit in enumerate(order):
         route = [(low, low ^ (1 << bit)) for low in range(count)]
         held = jnp.concatenate([held, lax.ppermute(held, "sub", route)], axis=0)
-        if midway is not None and step == min(2, len(order) - 1):
-            extra = midway()
-            held, extra = lax.optimization_barrier((held, extra))
+        for index, (at, hook) in enumerate(hooks):
+            if step == min(at, len(order) - 1):
+                extra[index] = hook()
+                held, extra[index] = lax.optimization_barrier((held, extra[index]))
     flipped = partners ^ me
     entry = jnp.zeros_like(partners)
     for step, bit in enumerate(order):
@@ -160,8 +160,15 @@
     head_forcing = rhs[:, None]
     head_source = lambda forcing: head_forcing if blocks - G >= iface else forcing
     pending = None
+    upper = None
     state = None
     ghost = None
+    face_blocks = -(-iface // 8)
+    split_ok = face_blocks * 8 <= blocks - G and blocks % 8 == 0 and blocks - G >= iface
+
+    def upper_rows(state, ghost, forcing):
+        return sweep_rows(state, ghost, forcing, 8, face_blocks, blocks // 8 - face_blocks)
+
     for outer in range(OUTER):
         forcing = jnp.concatenate([rhs[:iface] + robin_data.reshape(iface, width), rhs[iface:]], axis=0)[:, None]
         for sweep in range(SWEEPS):
@@ -170,7 +177,17 @@
             else:
                 top = sweep_rows(state, ghost, head_source(forcing), G, (blocks - G) // G, 1)
             sent = partner(top, "depth", 0)
-            state = sweep_rows(state, ghost, forcing, 8, 0, blocks // 8)
+            final = outer == OUTER - 1 and sweep == SWEEPS - 1
+            if upper is not None:
+                low = sweep_rows(state, ghost, forcing, 8, 0, face_blocks)
+                state = jnp.concatenate([low, upper], axis=0)
+                upper = None
+            elif final and split_ok and state is not None:
+                low = sweep_rows(state, ghost, forcing, 8, 0, face_blocks)
+                later = (state, ghost, forcing)
+                state = low
+            else:
+                state = sweep_rows(state, ghost, forcing, 8, 0, blocks // 8)
             ghost = sent
         state2 = state[:, 0]
         outgoing = (
@@ -179,9 +196,14 @@
             * state2[:iface].reshape(colours, per_colour, width)
             - robin_data
         )
-        if outer < OUTER - 1 and blocks - G >= iface:
+        if outer < OUTER - 1 and split_ok:
             ahead = lambda state=state, ghost=ghost: sweep_rows(state, ghost, head_forcing, G, (blocks - G) // G, 1)
-            robin_data, pending = exchange(outgoing, partners, tie=top, midway=ahead)
+            rest = lambda state=state, ghost=ghost: upper_rows(state, ghost, head_forcing)
+            robin_data, (pending, upper) = exchange(outgoing, partners, tie=top, hooks=((2, ahead), (4, rest)))
+        elif outer == OUTER - 1 and split_ok:
+            rest = lambda: upper_rows(*later)
+            robin_data, (upper,) = exchange(outgoing, partners, hooks=((1, rest),))
+            state = jnp.concatenate([state, upper], axis=0)
         else:
             robin_data, _ = exchange(outgoing, partners)
     return (state[:, 0][None, None], robin_data[None, None])

time: 175 us -> 176 us (level)
  Pallas kernels: 76.1 us -> 80.2 us
  other arithmetic: 7.52 us -> 11.2 us
  starting transfers between devices: 54.2 us -> 51 us
  waiting for transfers between devices: 25.5 us -> 22.6 us
    pallas_call x15 -> x17, Pallas kernels: 76.1 us -> 80.2 us  [block_sweep(): pl.pallas_call(functools.partial(sweep_kernel, coupled_terms=coupling is...]
    ppermute x14, starting transfers between devices: 43.8 us -> 40.6 us  [exchange(): held = jnp.concatenate([held, lax.ppermute(held, 'sub', route)], axis=0)]
    ppermute x14, waiting for transfers between devices: 21.6 us -> 18.7 us  [exchange(): held = jnp.concatenate([held, lax.ppermute(held, 'sub', route)], axis=0)]
    concatenate x0 -> x2, other arithmetic: none -> 2.64 us  [the longest x1 1.34 us: per_device(): state = jnp.concatenate([state, upper], axis=0)]
  transfers between devices with their start and end apart: 21 -> 21, of which waited for: 14 -> 11; matrix products, arithmetic and copies ran while one was open for 4% -> 5% of each run, Pallas kernels for 26% -> 31%
where the time goes in v2:
time: 176 us; the launch traced here: 175 us
  Pallas kernels  80.2 us (46%)
  starting transfers between devices  51 us (29%)
  waiting for transfers between devices  22.6 us (13%)
  other arithmetic  11.2 us (6%)
  local copies, waits for them, and re-layouts  9.08 us (5%)
    pallas_call x17, Pallas kernels, block_sweep(): pl.pallas_call(functools.partial(sweep_kernel, coupled_terms=coupling is...  80.2 us
    ppermute x14, starting transfers between devices, exchange(): held = jnp.concatenate([held, lax.ppermute(held, 'sub', route)], axis=0)  40.6 us
    ppermute x14, waiting for transfers between devices, exchange(): held = jnp.concatenate([held, lax.ppermute(held, 'sub', route)], axis=0)  18.7 us
    ppermute x7, starting transfers between devices, partner(): return lax.ppermute(block, axis, route)  10.3 us
    unnamed x31, local copies, waits for them, and re-layouts  4.32 us
    ppermute x7, waiting for transfers between devices, partner(): return lax.ppermute(block, axis, route)  3.92 us
  transfers between devices with their start and end apart: 21, of which 11 were waited for; matrix products, arithmetic and copies ran while one was open for 5% of the time, Pallas kernels for 31%

profile of v2, /device:TPU:1, one launch (start us, length us, event | category | flops | bytes accessed | tf_op | source)
XLA Modules:
  0.0 174.9 jit_solution(5645579691195699220)
XLA Ops:
  2.8 1.4 multiply_add_fusion.refs_1_.refs_5_
  4.2 1.6 shard_map.114
  5.8 3.6 %collective-permute-start = (f32[2,1,128]{2,1,0:T(1,128)}, f32[2,1,128]{2,1,0:T(1,128)S(1)}, u32[]{:S(2)}, u32[]{:S(2)}) collective-permute-start(f32[2,1,128]{2,1,0:T(1,128)} %shard_map.114), channel_id=1, source_target_pairs={{0,1},{1,0},{2,3},{3,2},{4,5},{5,4},{6,7},{7,6},{8,9},{9,8},{10,11... | collective-permute-start | bytes 3080 | tf_op jit(solution)/shard_map/ppermute | solution.py:22
  9.4 0.8 bitcast_add_fusion
  14.3 4.4 %shard_map.113.refs_3_ = f32[40,1,128]{2,1,0:T(1,128)} custom-call(f32[40,128,128]{2,1,0:T(8,128)} %bitcast.45, f32[40,1,128]{2,1,0:T(1,128)} %bitcast.66), custom_call_target="tpu_custom_call" | custom-call | flops 1310720 | bytes 2621440 | tf_op jit(solution)/shard_map/pallas_call | solution.py:78
  19.5 2.6 %shard_map.116 = f32[2,1,128]{2,1,0:T(1,128)} custom-call(s32[240]{0:T(256)} %reshape_squeeze.9.refs_0_, bf16[40,6,128,128]{3,2,1,0:T(8,128)(2,1)} %bitcast.29, f32[40,128,128]{2,1,0:T(8,128)} %bitcast.46, f32[40,1,128]{2,1,0:T(1,128)} %shard_map.113.refs_3_, f32[2,1,128]{2,1,0:T(1,128)} %copy-done.7, f32[40,1,128]{2,1,0:T(1,128)} %multiply_add_fusion.refs_1_.refs_5_, ...), custom_call_target="tpu_custom_call" | custom-call | flops 458752 | bytes 524288 | tf_op jit(solution)/shard_map/pallas_call | solution.py:78
  22.1 7.8 %shard_map.115.refs_3_ = f32[40,1,128]{2,1,0:T(1,128)} custom-call(s32[240]{0:T(256)} %reshape_squeeze.9.refs_0_, bf16[40,6,128,128]{3,2,1,0:T(8,128)(2,1)} %bitcast.30, f32[40,128,128]{2,1,0:T(8,128)} %bitcast.47, f32[40,1,128]{2,1,0:T(1,128)} %shard_map.113.refs_3_, f32[2,1,128]{2,1,0:T(1,128)} %copy-done.7, f32[40,1,128]{2,1,0:T(1,128)} %bitcast.67, ...), custom_call_target="tpu_custom_call" | custom-call | flops 9175040 | bytes 10485760 | tf_op jit(solution)/shard_map/pallas_call | solution.py:78
  30.4 2.6 %shard_map.118 = f32[2,1,128]{2,1,0:T(1,128)} custom-call(s32[240]{0:T(256)} %reshape_squeeze.9.refs_0_, bf16[40,6,128,128]{3,2,1,0:T(8,128)(2,1)} %bitcast.31, f32[40,128,128]{2,1,0:T(8,128)} %bitcast.48, f32[40,1,128]{2,1,0:T(1,128)} %shard_map.115.refs_3_, f32[2,1,128]{2,1,0:T(1,128)} %copy-done.8, f32[40,1,128]{2,1,0:T(1,128)} %multiply_add_fusion.refs_1_.refs_5_, ...), custom_call_target="tpu_custom_call" | custom-call | flops 458752 | bytes 524288 | tf_op jit(solution)/shard_map/pallas_call | solution.py:78
  33.0 3.0 %collective-permute-start.2 = (f32[2,1,128]{2,1,0:T(1,128)}, f32[2,1,128]{2,1,0:T(1,128)S(1)}, u32[]{:S(2)}, u32[]{:S(2)}) collective-permute-start(f32[2,1,128]{2,1,0:T(1,128)} %shard_map.118), channel_id=1, source_target_pairs={{0,1},{1,0},{2,3},{3,2},{4,5},{5,4},{6,7},{7,6},{8,9},{9,8},{10,11... | collective-permute-start | bytes 3080 | tf_op jit(solution)/shard_map/ppermute | solution.py:22
  36.1 7.8 %shard_map.117.refs_3_ = f32[40,1,128]{2,1,0:T(1,128)} custom-call(s32[240]{0:T(256)} %reshape_squeeze.9.refs_0_, bf16[40,6,128,128]{3,2,1,0:T(8,128)(2,1)} %bitcast.32, f32[40,128,128]{2,1,0:T(8,128)} %bitcast.49, f32[40,1,128]{2,1,0:T(1,128)} %shard_map.115.refs_3_, f32[2,1,128]{2,1,0:T(1,128)} %copy-done.8, f32[40,1,128]{2,1,0:T(1,128)} %bitcast.68, ...), custom_call_target="tpu_custom_call" | custom-call | flops 9175040 | bytes 10485760 | tf_op jit(solution)/shard_map/pallas_call | solution.py:78
  44.4 7.8 %shard_map.119.refs_3_ = f32[40,1,128]{2,1,0:T(1,128)} custom-call(s32[240]{0:T(256)} %reshape_squeeze.9.refs_0_, bf16[40,6,128,128]{3,2,1,0:T(8,128)(2,1)} %bitcast.33, f32[40,128,128]{2,1,0:T(8,128)} %bitcast.50, f32[40,1,128]{2,1,0:T(1,128)} %shard_map.117.refs_3_, f32[2,1,128]{2,1,0:T(1,128)} %copy-done.9, f32[40,1,128]{2,1,0:T(1,128)} %bitcast.69, ...), custom_call_target="tpu_custom_call" | custom-call | flops 9175040 | bytes 10485760 | tf_op jit(solution)/shard_map/pallas_call | solution.py:78
  53.0 2.6 %shard_map.120 = f32[2,1,128]{2,1,0:T(1,128)} custom-call(s32[240]{0:T(256)} %reshape_squeeze.9.refs_0_, bf16[40,6,128,128]{3,2,1,0:T(8,128)(2,1)} %bitcast.34, f32[40,128,128]{2,1,0:T(8,128)} %bitcast.51, f32[40,1,128]{2,1,0:T(1,128)} %shard_map.117.refs_3_, f32[2,1,128]{2,1,0:T(1,128)} %copy-done.9, f32[40,1,128]{2,1,0:T(1,128)} %multiply_add_fusion.refs_1_.refs_5_, ...), custom_call_target="tpu_custom_call" | custom-call | flops 458752 | bytes 524288 | tf_op jit(solution)/shard_map/pallas_call | solution.py:78
  55.6 6.9 %collective-permute-start.4 = (f32[1,4,2,128]{3,2,1,0:T(2,128)S(1)}, f32[1,4,2,128]{3,2,1,0:T(2,128)S(1)}, u32[]{:S(2)}, u32[]{:S(2)}) collective-permute-start(f32[1,4,2,128]{3,2,1,0:T(2,128)S(1)} %bitcast.71), channel_id=1, source_target_pairs={{0,16},{2,18},{4,20},{6,22},{8,24},{10,26},{12,28},{14,30},{16,0},... | collective-permute-start | bytes 12296 | tf_op jit(solution)/shard_map/ppermute | solution.py:111
  62.5 1.0 collective-permute-done.4
  63.5 2.9 %collective-permute-start.5 = (f32[2,4,2,128]{3,2,1,0:T(2,128)S(1)}, f32[2,4,2,128]{3,2,1,0:T(2,128)S(1)}, u32[]{:S(2)}, u32[]{:S(2)}) collective-permute-start(f32[2,4,2,128]{3,2,1,0:T(2,128)S(1)} %pad_maximum_fusion.14), channel_id=1, source_target_pairs={{0,64},{2,66},{4,68},{6,70},{8,72},{10,74},{12,76},{14,78},{16,80}... | collective-permute-start | bytes 24584 | tf_op jit(solution)/shard_map/ppermute | solution.py:111
  66.4 1.1 collective-permute-done.5
  67.5 1.5 collective-permute-start.6
  69.3 3.9 %collective-permute-done.3.refs_4_ = f32[2,1,128]{2,1,0:T(1,128)S(1)} collective-permute-done((f32[2,1,128]{2,1,0:T(1,128)}, f32[2,1,128]{2,1,0:T(1,128)S(1)}, u32[]{:S(2)}, u32[]{:S(2)}) %collective-permute-start.3) | collective-permute-done | bytes 1056 | tf_op jit(solution)/shard_map/ppermute | solution.py:22
  73.8 2.6 %shard_map.121 = f32[2,1,128]{2,1,0:T(1,128)} custom-call(s32[240]{0:T(256)} %reshape_squeeze.9.refs_0_, bf16[40,6,128,128]{3,2,1,0:T(8,128)(2,1)} %bitcast.35, f32[40,128,128]{2,1,0:T(8,128)} %bitcast.52, f32[40,1,128]{2,1,0:T(1,128)} %shard_map.119.refs_3_, f32[2,1,128]{2,1,0:T(1,128)} %copy-done.4, f32[40,1,128]{2,1,0:T(1,128)} %multiply_add_fusion.refs_1_.refs_5_, ...), custom_call_target="tpu_custom_call" | custom-call | flops 458752 | bytes 524288 | tf_op jit(solution)/shard_map/pallas_call | solution.py:78
  76.8 2.5 %collective-permute-done.7 = f32[8,4,2,128]{3,2,1,0:T(2,128)S(1)} collective-permute-done((f32[8,4,2,128]{3,2,1,0:T(2,128)S(1)}, f32[8,4,2,128]{3,2,1,0:T(2,128)S(1)}, u32[]{:S(2)}, u32[]{:S(2)}) %collective-permute-start.7) | collective-permute-done | bytes 32800 | tf_op jit(solution)/shard_map/ppermute | solution.py:111
  79.3 1.4 collective-permute-start.8
  80.7 6.4 %shard_map.122 = f32[32,1,128]{2,1,0:T(1,128)} custom-call(s32[240]{0:T(256)} %reshape_squeeze.9.refs_0_, bf16[40,6,128,128]{3,2,1,0:T(8,128)(2,1)} %bitcast.36, f32[40,128,128]{2,1,0:T(8,128)} %bitcast.53, f32[40,1,128]{2,1,0:T(1,128)} %shard_map.119.refs_3_, f32[2,1,128]{2,1,0:T(1,128)} %copy-done.4, f32[40,1,128]{2,1,0:T(1,128)} %multiply_add_fusion.refs_1_.refs_5_, ...), custom_call_target="tpu_custom_call" | custom-call | flops 7340032 | bytes 8388608 | tf_op jit(solution)/shard_map/pallas_call | solution.py:78
  87.2 1.7 collective-permute-start.9
  88.9 2.4 %collective-permute-done.9 = f32[32,4,2,128]{3,2,1,0:T(2,128)S(1)} collective-permute-done((f32[32,4,2,128]{3,2,1,0:T(2,128)S(1)}, f32[32,4,2,128]{3,2,1,0:T(2,128)S(1)}, u32[]{:S(2)}, u32[]{:S(2)}) %collective-permute-start.9) | collective-permute-done | bytes 131104 | tf_op jit(solution)/shard_map/ppermute | solution.py:111
  91.4 7.7 %collective-permute-start.10 = (f32[64,4,2,128]{3,2,1,0:T(2,128)S(1)}, f32[64,4,2,128]{3,2,1,0:T(2,128)S(1)}, u32[]{:S(2)}, u32[]{:S(2)}) collective-permute-start(f32[64,4,2,128]{3,2,1,0:T(2,128)S(1)} %pad_maximum_fusion.1), channel_id=1, source_target_pairs={{0,2},{2,0},{4,6},{6,4},{8,10},{10,8},{12,14},{14,12},{16,18},{18,... | collective-permute-start | bytes 786440 | tf_op jit(solution)/shard_map/ppermute | solution.py:111
  101.7 3.4 %shard_map.123 = f32[8,1,128]{2,1,0:T(1,128)} custom-call(s32[240]{0:T(256)} %reshape_squeeze.9.refs_0_, bf16[40,6,128,128]{3,2,1,0:T(8,128)(2,1)} %bitcast.37, f32[40,128,128]{2,1,0:T(8,128)} %bitcast.54, f32[40,1,128]{2,1,0:T(1,128)} %shard_map.119.refs_3_, f32[2,1,128]{2,1,0:T(1,128)} %copy-done.4, f32[40,1,128]{2,1,0:T(1,128)} %bitcast.61, ...), custom_call_target="tpu_custom_call" | custom-call | flops 1835008 | bytes 2097152 | tf_op jit(solution)/shard_map/pallas_call | solution.py:78
  105.1 1.3 pad_maximum_fusion.10.refs_3_
  107.0 2.6 %shard_map.125 = f32[2,1,128]{2,1,0:T(1,128)} custom-call(s32[240]{0:T(256)} %reshape_squeeze.9.refs_0_, bf16[40,6,128,128]{3,2,1,0:T(8,128)(2,1)} %bitcast.38, f32[40,128,128]{2,1,0:T(8,128)} %bitcast.55, f32[40,1,128]{2,1,0:T(1,128)} %pad_maximum_fusion.10.refs_3_, f32[2,1,128]{2,1,0:T(1,128)} %copy-done.5, ...), custom_call_target="tpu_custom_call" | custom-call | flops 458752 | bytes 524288 | tf_op jit(solution)/shard_map/pallas_call | solution.py:78
  109.6 2.3 %collective-permute-start.12 = (f32[2,1,128]{2,1,0:T(1,128)}, f32[2,1,128]{2,1,0:T(1,128)S(1)}, u32[]{:S(2)}, u32[]{:S(2)}) collective-permute-start(f32[2,1,128]{2,1,0:T(1,128)} %shard_map.125), channel_id=1, source_target_pairs={{0,1},{1,0},{2,3},{3,2},{4,5},{5,4},{6,7},{7,6},{8,9},{9,8},{10,11... | collective-permute-start | bytes 3080 | tf_op jit(solution)/shard_map/ppermute | solution.py:22
  111.8 7.8 %shard_map.124.refs_3_ = f32[40,1,128]{2,1,0:T(1,128)} custom-call(s32[240]{0:T(256)} %reshape_squeeze.9.refs_0_, bf16[40,6,128,128]{3,2,1,0:T(8,128)(2,1)} %bitcast.39, f32[40,128,128]{2,1,0:T(8,128)} %bitcast.56, f32[40,1,128]{2,1,0:T(1,128)} %pad_maximum_fusion.10.refs_3_, f32[2,1,128]{2,1,0:T(1,128)} %copy-done.5, f32[40,1,128]{2,1,0:T(1,128)} %bitcast.62, ...), custom_call_target="tpu_custom_call" | custom-call | flops 9175040 | bytes 10485760 | tf_op jit(solution)/shard_map/pallas_call | solution.py:78
  120.2 2.6 %shard_map.127 = f32[2,1,128]{2,1,0:T(1,128)} custom-call(s32[240]{0:T(256)} %reshape_squeeze.9.refs_0_, bf16[40,6,128,128]{3,2,1,0:T(8,128)(2,1)} %bitcast.40, f32[40,128,128]{2,1,0:T(8,128)} %bitcast.57, f32[40,1,128]{2,1,0:T(1,128)} %shard_map.124.refs_3_, f32[2,1,128]{2,1,0:T(1,128)} %copy-done.10, f32[40,1,128]{2,1,0:T(1,128)} %multiply_add_fusion.refs_1_.refs_5_, ...), custom_call_target="tpu_custom_call" | custom-call | flops 458752 | bytes 524288 | tf_op jit(solution)/shard_map/pallas_call | solution.py:78
  123.5 7.8 %shard_map.126.refs_3_ = f32[40,1,128]{2,1,0:T(1,128)} custom-call(s32[240]{0:T(256)} %reshape_squeeze.9.refs_0_, bf16[40,6,128,128]{3,2,1,0:T(8,128)(2,1)} %bitcast.41, f32[40,128,128]{2,1,0:T(8,128)} %bitcast.58, f32[40,1,128]{2,1,0:T(1,128)} %shard_map.124.refs_3_, f32[2,1,128]{2,1,0:T(1,128)} %copy-done.10, f32[40,1,128]{2,1,0:T(1,128)} %bitcast.63, ...), custom_call_target="tpu_custom_call" | custom-call | flops 9175040 | bytes 10485760 | tf_op jit(solution)/shard_map/pallas_call | solution.py:78
  131.9 3.4 %shard_map.128 = f32[8,1,128]{2,1,0:T(1,128)} custom-call(s32[240]{0:T(256)} %reshape_squeeze.9.refs_0_, bf16[40,6,128,128]{3,2,1,0:T(8,128)(2,1)} %bitcast.42, f32[40,128,128]{2,1,0:T(8,128)} %bitcast.59, f32[40,1,128]{2,1,0:T(1,128)} %shard_map.126.refs_3_, f32[2,1,128]{2,1,0:T(1,128)} %copy-done.6, f32[40,1,128]{2,1,0:T(1,128)} %bitcast.64, ...), custom_call_target="tpu_custom_call" | custom-call | flops 1835008 | bytes 2097152 | tf_op jit(solution)/shard_map/pallas_call | solution.py:78
  135.3 0.8 bitcast_subtract_fusion
  136.1 5.1 %collective-permute-start.14 = (f32[1,4,2,128]{3,2,1,0:T(2,128)S(1)}, f32[1,4,2,128]{3,2,1,0:T(2,128)S(1)}, u32[]{:S(2)}, u32[]{:S(2)}) collective-permute-start(f32[1,4,2,128]{3,2,1,0:T(2,128)S(1)} %bitcast_subtract_fusion), channel_id=1, source_target_pairs={{0,16},{2,18},{4,20},{6,22},{8,24},{10,26},{12,28},{14,30},{16,0},... | collective-permute-start | bytes 12296 | tf_op jit(solution)/shard_map/ppermute | solution.py:111
  141.3 1.2 collective-permute-done.14
  142.5 2.6 %collective-permute-start.15 = (f32[2,4,2,128]{3,2,1,0:T(2,128)S(1)}, f32[2,4,2,128]{3,2,1,0:T(2,128)S(1)}, u32[]{:S(2)}, u32[]{:S(2)}) collective-permute-start(f32[2,4,2,128]{3,2,1,0:T(2,128)S(1)} %pad_maximum_fusion.15), channel_id=1, source_target_pairs={{0,64},{2,66},{4,68},{6,70},{8,72},{10,74},{12,76},{14,78},{16,80}... | collective-permute-start | bytes 24584 | tf_op jit(solution)/shard_map/ppermute | solution.py:111
  145.1 6.4 %shard_map.129 = f32[32,1,128]{2,1,0:T(1,128)} custom-call(s32[240]{0:T(256)} %reshape_squeeze.9.refs_0_, bf16[40,6,128,128]{3,2,1,0:T(8,128)(2,1)} %bitcast.43, f32[40,128,128]{2,1,0:T(8,128)} %bitcast.60, f32[40,1,128]{2,1,0:T(1,128)} %shard_map.126.refs_3_, f32[2,1,128]{2,1,0:T(1,128)} %copy-done.6, f32[40,1,128]{2,1,0:T(1,128)} %bitcast.65, ...), custom_call_target="tpu_custom_call" | custom-call | flops 7340032 | bytes 8388608 | tf_op jit(solution)/shard_map/pallas_call | solution.py:78
  151.5 1.0 collective-permute-start.16
  152.6 2.6 %collective-permute-done.16 = f32[4,4,2,128]{3,2,1,0:T(2,128)S(1)} collective-permute-done((f32[4,4,2,128]{3,2,1,0:T(2,128)S(1)}, f32[4,4,2,128]{3,2,1,0:T(2,128)S(1)}, u32[]{:S(2)}, u32[]{:S(2)}) %collective-permute-start.16) | collective-permute-done | bytes 16416 | tf_op jit(solution)/shard_map/ppermute | solution.py:111
  155.1 0.8 collective-permute-start.17
  156.0 2.2 %collective-permute-done.17 = f32[8,4,2,128]{3,2,1,0:T(2,128)S(1)} collective-permute-done((f32[8,4,2,128]{3,2,1,0:T(2,128)S(1)}, f32[8,4,2,128]{3,2,1,0:T(2,128)S(1)}, u32[]{:S(2)}, u32[]{:S(2)}) %collective-permute-start.17) | collective-permute-done | bytes 32800 | tf_op jit(solution)/shard_map/ppermute | solution.py:111
  158.4 3.1 %collective-permute-done.18 = f32[16,4,2,128]{3,2,1,0:T(2,128)S(1)} collective-permute-done((f32[16,4,2,128]{3,2,1,0:T(2,128)S(1)}, f32[16,4,2,128]{3,2,1,0:T(2,128)S(1)}, u32[]{:S(2)}, u32[]{:S(2)}) %collective-permute-start.18) | collective-permute-done | bytes 65568 | tf_op jit(solution)/shard_map/ppermute | solution.py:111
  161.5 1.7 collective-permute-start.19
  163.3 2.3 %collective-permute-done.19 = f32[32,4,2,128]{3,2,1,0:T(2,128)S(1)} collective-permute-done((f32[32,4,2,128]{3,2,1,0:T(2,128)S(1)}, f32[32,4,2,128]{3,2,1,0:T(2,128)S(1)}, u32[]{:S(2)}, u32[]{:S(2)}) %collective-permute-start.19) | collective-permute-done | bytes 131104 | tf_op jit(solution)/shard_map/ppermute | solution.py:111
  165.7 6.6 %collective-permute-start.20 = (f32[64,4,2,128]{3,2,1,0:T(2,128)S(1)}, f32[64,4,2,128]{3,2,1,0:T(2,128)S(1)}, u32[]{:S(2)}, u32[]{:S(2)}) collective-permute-start(f32[64,4,2,128]{3,2,1,0:T(2,128)S(1)} %get-tuple-element.16), channel_id=1, source_target_pairs={{0,2},{2,0},{4,6},{6,4},{8,10},{10,8},{12,14},{14,12},{16,18},{18,... | collective-permute-start | bytes 786440 | tf_op jit(solution)/shard_map/ppermute | solution.py:111
  172.3 1.3 pad_maximum_fusion.11
  173.7 1.2 gather_fusion.2
  (82 shorter events, 15.8 us)
Async XLA Ops:
  0.6 0.7 copy-start
  5.8 12.9 %collective-permute-start = (f32[2,1,128]{2,1,0:T(1,128)}, f32[2,1,128]{2,1,0:T(1,128)S(1)}, u32[]{:S(2)}, u32[]{:S(2)}) collective-permute-start(f32[2,1,128]{2,1,0:T(1,128)} %shard_map.114), channel_id=1, source_target_pairs={{0,1},{1,0},{2,3},{3,2},{4,5},{5,4},{6,7},{7,6},{8,9},{9,8},{10,11... | collective-permute-start | bytes 3080 | tf_op jit(solution)/shard_map/ppermute | solution.py:22
  18.7 0.7 copy-start.7
  22.1 7.8 %collective-permute-start.1 = (f32[2,1,128]{2,1,0:T(1,128)}, f32[2,1,128]{2,1,0:T(1,128)S(1)}, u32[]{:S(2)}, u32[]{:S(2)}) collective-permute-start(f32[2,1,128]{2,1,0:T(1,128)} %shard_map.116), channel_id=1, source_target_pairs={{0,1},{1,0},{2,3},{3,2},{4,5},{5,4},{6,7},{7,6},{8,9},{9,8},{10,11... | collective-permute-start | bytes 3080 | tf_op jit(solution)/shard_map/ppermute | solution.py:22
  29.9 0.6 copy-start.8
  33.0 10.9 %collective-permute-start.2 = (f32[2,1,128]{2,1,0:T(1,128)}, f32[2,1,128]{2,1,0:T(1,128)S(1)}, u32[]{:S(2)}, u32[]{:S(2)}) collective-permute-start(f32[2,1,128]{2,1,0:T(1,128)} %shard_map.118), channel_id=1, source_target_pairs={{0,1},{1,0},{2,3},{3,2},{4,5},{5,4},{6,7},{7,6},{8,9},{9,8},{10,11... | collective-permute-start | bytes 3080 | tf_op jit(solution)/shard_map/ppermute | solution.py:22
  43.9 9.0 %copy-start.3 = (f32[1,1,4,2,128]{4,3,2,1,0:T(2,128)S(1)}, f32[1,1,4,2,128]{4,3,2,1,0:T(2,128)}, u32[]{:S(2)}) copy-start(f32[1,1,4,2,128]{4,3,2,1,0:T(2,128)} %param.19) | copy-start | bytes 12292
  43.9 0.6 copy-start.9
  55.6 7.9 %collective-permute-start.4 = (f32[1,4,2,128]{3,2,1,0:T(2,128)S(1)}, f32[1,4,2,128]{3,2,1,0:T(2,128)S(1)}, u32[]{:S(2)}, u32[]{:S(2)}) collective-permute-start(f32[1,4,2,128]{3,2,1,0:T(2,128)S(1)} %bitcast.71), channel_id=1, source_target_pairs={{0,16},{2,18},{4,20},{6,22},{8,24},{10,26},{12,28},{14,30},{16,0},... | collective-permute-start | bytes 12296 | tf_op jit(solution)/shard_map/ppermute | solution.py:111
  63.5 4.0 %collective-permute-start.5 = (f32[2,4,2,128]{3,2,1,0:T(2,128)S(1)}, f32[2,4,2,128]{3,2,1,0:T(2,128)S(1)}, u32[]{:S(2)}, u32[]{:S(2)}) collective-permute-start(f32[2,4,2,128]{3,2,1,0:T(2,128)S(1)} %pad_maximum_fusion.14), channel_id=1, source_target_pairs={{0,64},{2,66},{4,68},{6,70},{8,72},{10,74},{12,76},{14,78},{16,80}... | collective-permute-start | bytes 24584 | tf_op jit(solution)/shard_map/ppermute | solution.py:111
  67.5 8.9 %collective-permute-start.6 = (f32[4,4,2,128]{3,2,1,0:T(2,128)S(1)}, f32[4,4,2,128]{3,2,1,0:T(2,128)S(1)}, u32[]{:S(2)}, u32[]{:S(2)}) collective-permute-start(f32[4,4,2,128]{3,2,1,0:T(2,128)S(1)} %pad_maximum_fusion.12), channel_id=1, source_target_pairs={{0,8},{2,10},{4,12},{6,14},{8,0},{10,2},{12,4},{14,6},{16,24},{18,... | collective-permute-start | bytes 49160 | tf_op jit(solution)/shard_map/ppermute | solution.py:111
  69.1 4.1 %collective-permute-start.3 = (f32[2,1,128]{2,1,0:T(1,128)}, f32[2,1,128]{2,1,0:T(1,128)S(1)}, u32[]{:S(2)}, u32[]{:S(2)}) collective-permute-start(f32[2,1,128]{2,1,0:T(1,128)} %shard_map.120), channel_id=1, source_target_pairs={{0,1},{1,0},{2,3},{3,2},{4,5},{5,4},{6,7},{7,6},{8,9},{9,8},{10,11... | collective-permute-start | bytes 3080 | tf_op jit(solution)/shard_map/ppermute | solution.py:22
  73.2 0.6 copy-start.4
  76.4 22.7 %copy-start.11 = (s32[4,128]{1,0:T(4,128)S(1)}, s32[4,128]{1,0:T(4,128)}, u32[]{:S(2)}) copy-start(s32[4,128]{1,0:T(4,128)} %param.18) | copy-start | bytes 6148
  76.4 22.9 %copy-start.12 = (f32[2,1,128]{2,1,0:T(1,128)S(1)}, f32[2,1,128]{2,1,0:T(1,128)}, u32[]{:S(2)}) copy-start(f32[2,1,128]{2,1,0:T(1,128)} %shard_map.121) | copy-start | bytes 3076
  76.4 2.9 %collective-permute-start.7 = (f32[8,4,2,128]{3,2,1,0:T(2,128)S(1)}, f32[8,4,2,128]{3,2,1,0:T(2,128)S(1)}, u32[]{:S(2)}, u32[]{:S(2)}) collective-permute-start(f32[8,4,2,128]{3,2,1,0:T(2,128)S(1)} %pad_maximum_fusion.6), channel_id=1, source_target_pairs={{0,128},{2,130},{4,132},{6,134},{8,136},{10,138},{12,140},{14,142}... | collective-permute-start | bytes 98312 | tf_op jit(solution)/shard_map/ppermute | solution.py:111
  79.3 7.8 %collective-permute-start.8 = (f32[16,4,2,128]{3,2,1,0:T(2,128)S(1)}, f32[16,4,2,128]{3,2,1,0:T(2,128)S(1)}, u32[]{:S(2)}, u32[]{:S(2)}) collective-permute-start(f32[16,4,2,128]{3,2,1,0:T(2,128)S(1)} %pad_maximum_fusion.4), channel_id=1, source_target_pairs={{0,32},{2,34},{4,36},{6,38},{8,40},{10,42},{12,44},{14,46},{16,48}... | collective-permute-start | bytes 196616 | tf_op jit(solution)/shard_map/ppermute | solution.py:111
  87.1 18.0 %copy-start.1 = (f32[32,1,128]{2,1,0:T(1,128)S(1)}, f32[32,1,128]{2,1,0:T(1,128)}, u32[]{:S(2)}) copy-start(f32[32,1,128]{2,1,0:T(1,128)} %shard_map.122) | copy-start | bytes 49156
  87.2 4.1 %collective-permute-start.9 = (f32[32,4,2,128]{3,2,1,0:T(2,128)S(1)}, f32[32,4,2,128]{3,2,1,0:T(2,128)S(1)}, u32[]{:S(2)}, u32[]{:S(2)}) collective-permute-start(f32[32,4,2,128]{3,2,1,0:T(2,128)S(1)} %pad_maximum_fusion.2), channel_id=1, source_target_pairs={{0,4},{2,6},{4,0},{6,2},{8,12},{10,14},{12,8},{14,10},{16,20},{18,... | collective-permute-start | bytes 393224 | tf_op jit(solution)/shard_map/ppermute | solution.py:111
  91.4 8.9 %collective-permute-start.10 = (f32[64,4,2,128]{3,2,1,0:T(2,128)S(1)}, f32[64,4,2,128]{3,2,1,0:T(2,128)S(1)}, u32[]{:S(2)}, u32[]{:S(2)}) collective-permute-start(f32[64,4,2,128]{3,2,1,0:T(2,128)S(1)} %pad_maximum_fusion.1), channel_id=1, source_target_pairs={{0,2},{2,0},{4,6},{6,4},{8,10},{10,8},{12,14},{14,12},{16,18},{18,... | collective-permute-start | bytes 786440 | tf_op jit(solution)/shard_map/ppermute | solution.py:111
  99.3 7.1 %collective-permute-start.11 = (f32[2,1,128]{2,1,0:T(1,128)S(1)}, f32[2,1,128]{2,1,0:T(1,128)S(1)}, u32[]{:S(2)}, u32[]{:S(2)}) collective-permute-start(f32[2,1,128]{2,1,0:T(1,128)S(1)} %copy-done.12), channel_id=1, source_target_pairs={{0,1},{1,0},{2,3},{3,2},{4,5},{5,4},{6,7},{7,6},{8,9},{9,8},{10,11... | collective-permute-start | bytes 3080 | tf_op jit(solution)/shard_map/ppermute | solution.py:22
  106.4 0.6 copy-start.5
  109.6 10.1 %collective-permute-start.12 = (f32[2,1,128]{2,1,0:T(1,128)}, f32[2,1,128]{2,1,0:T(1,128)S(1)}, u32[]{:S(2)}, u32[]{:S(2)}) collective-permute-start(f32[2,1,128]{2,1,0:T(1,128)} %shard_map.125), channel_id=1, source_target_pairs={{0,1},{1,0},{2,3},{3,2},{4,5},{5,4},{6,7},{7,6},{8,9},{9,8},{10,11... | collective-permute-start | bytes 3080 | tf_op jit(solution)/shard_map/ppermute | solution.py:22
  119.6 0.6 copy-start.10
  122.8 8.5 %collective-permute-start.13 = (f32[2,1,128]{2,1,0:T(1,128)}, f32[2,1,128]{2,1,0:T(1,128)S(1)}, u32[]{:S(2)}, u32[]{:S(2)}) collective-permute-start(f32[2,1,128]{2,1,0:T(1,128)} %shard_map.127), channel_id=1, source_target_pairs={{0,1},{1,0},{2,3},{3,2},{4,5},{5,4},{6,7},{7,6},{8,9},{9,8},{10,11... | collective-permute-start | bytes 3080 | tf_op jit(solution)/shard_map/ppermute | solution.py:22
  131.3 0.6 copy-start.6
  135.3 37.1 %copy-start.2 = (f32[8,1,128]{2,1,0:T(1,128)S(1)}, f32[8,1,128]{2,1,0:T(1,128)}, u32[]{:S(2)}) copy-start(f32[8,1,128]{2,1,0:T(1,128)} %shard_map.128) | copy-start | bytes 12292
  136.1 6.4 %collective-permute-start.14 = (f32[1,4,2,128]{3,2,1,0:T(2,128)S(1)}, f32[1,4,2,128]{3,2,1,0:T(2,128)S(1)}, u32[]{:S(2)}, u32[]{:S(2)}) collective-permute-start(f32[1,4,2,128]{3,2,1,0:T(2,128)S(1)} %bitcast_subtract_fusion), channel_id=1, source_target_pairs={{0,16},{2,18},{4,20},{6,22},{8,24},{10,26},{12,28},{14,30},{16,0},... | collective-permute-start | bytes 12296 | tf_op jit(solution)/shard_map/ppermute | solution.py:111
  142.5 9.0 %collective-permute-start.15 = (f32[2,4,2,128]{3,2,1,0:T(2,128)S(1)}, f32[2,4,2,128]{3,2,1,0:T(2,128)S(1)}, u32[]{:S(2)}, u32[]{:S(2)}) collective-permute-start(f32[2,4,2,128]{3,2,1,0:T(2,128)S(1)} %pad_maximum_fusion.15), channel_id=1, source_target_pairs={{0,64},{2,66},{4,68},{6,70},{8,72},{10,74},{12,76},{14,78},{16,80}... | collective-permute-start | bytes 24584 | tf_op jit(solution)/shard_map/ppermute | solution.py:111
  151.5 3.6 %collective-permute-start.16 = (f32[4,4,2,128]{3,2,1,0:T(2,128)S(1)}, f32[4,4,2,128]{3,2,1,0:T(2,128)S(1)}, u32[]{:S(2)}, u32[]{:S(2)}) collective-permute-start(f32[4,4,2,128]{3,2,1,0:T(2,128)S(1)} %pad_maximum_fusion.13), channel_id=1, source_target_pairs={{0,8},{2,10},{4,12},{6,14},{8,0},{10,2},{12,4},{14,6},{16,24},{18,... | collective-permute-start | bytes 49160 | tf_op jit(solution)/shard_map/ppermute | solution.py:111
  155.1 3.1 %collective-permute-start.17 = (f32[8,4,2,128]{3,2,1,0:T(2,128)S(1)}, f32[8,4,2,128]{3,2,1,0:T(2,128)S(1)}, u32[]{:S(2)}, u32[]{:S(2)}) collective-permute-start(f32[8,4,2,128]{3,2,1,0:T(2,128)S(1)} %pad_maximum_fusion.7), channel_id=1, source_target_pairs={{0,128},{2,130},{4,132},{6,134},{8,136},{10,138},{12,140},{14,142}... | collective-permute-start | bytes 98312 | tf_op jit(solution)/shard_map/ppermute | solution.py:111
  158.3 3.2 %collective-permute-start.18 = (f32[16,4,2,128]{3,2,1,0:T(2,128)S(1)}, f32[16,4,2,128]{3,2,1,0:T(2,128)S(1)}, u32[]{:S(2)}, u32[]{:S(2)}) collective-permute-start(f32[16,4,2,128]{3,2,1,0:T(2,128)S(1)} %pad_maximum_fusion.5), channel_id=1, source_target_pairs={{0,32},{2,34},{4,36},{6,38},{8,40},{10,42},{12,44},{14,46},{16,48}... | collective-permute-start | bytes 196616 | tf_op jit(solution)/shard_map/ppermute | solution.py:111
  161.5 4.1 %collective-permute-start.19 = (f32[32,4,2,128]{3,2,1,0:T(2,128)S(1)}, f32[32,4,2,128]{3,2,1,0:T(2,128)S(1)}, u32[]{:S(2)}, u32[]{:S(2)}) collective-permute-start(f32[32,4,2,128]{3,2,1,0:T(2,128)S(1)} %pad_maximum_fusion.3), channel_id=1, source_target_pairs={{0,4},{2,6},{4,0},{6,2},{8,12},{10,14},{12,8},{14,10},{16,20},{18,... | collective-permute-start | bytes 393224 | tf_op jit(solution)/shard_map/ppermute | solution.py:111
  165.7 8.0 %collective-permute-start.20 = (f32[64,4,2,128]{3,2,1,0:T(2,128)S(1)}, f32[64,4,2,128]{3,2,1,0:T(2,128)S(1)}, u32[]{:S(2)}, u32[]{:S(2)}) collective-permute-start(f32[64,4,2,128]{3,2,1,0:T(2,128)S(1)} %get-tuple-element.16), channel_id=1, source_target_pairs={{0,2},{2,0},{4,6},{6,4},{8,10},{10,8},{12,14},{14,12},{16,18},{18,... | collective-permute-start | bytes 786440 | tf_op jit(solution)/shard_map/ppermute | solution.py:111

commit v3 on v1

--- a/solution.py
+++ b/solution.py
@@ -160,6 +160,7 @@
     head_forcing = rhs[:, None]
     head_source = lambda forcing: head_forcing if blocks - G >= iface else forcing
     pending = None
+    body_rows = next(size for size in (20, 10, 8, 5, 4, 2, 1) if blocks % size == 0)
     state = None
     ghost = None
     for outer in range(OUTER):
@@ -170,7 +171,7 @@
             else:
                 top = sweep_rows(state, ghost, head_source(forcing), G, (blocks - G) // G, 1)
             sent = partner(top, "depth", 0)
-            state = sweep_rows(state, ghost, forcing, 8, 0, blocks // 8)
+            state = sweep_rows(state, ghost, forcing, body_rows, 0, blocks // body_rows)
             ghost = sent
         state2 = state[:, 0]
         outgoing = (

time: 175 us -> 165 us (0.943)
  Pallas kernels: 76.1 us -> 65.9 us
    pallas_call x15, Pallas kernels: 76.1 us -> 65.9 us  [block_sweep(): pl.pallas_call(functools.partial(sweep_kernel, coupled_terms=coupling is...]
  transfers between devices with their start and end apart: 21 -> 21, of which waited for: 14 -> 14; matrix products, arithmetic and copies ran while one was open for 4% -> 4% of each run, Pallas kernels for 26% -> 23%
where the time goes in v3:
time: 165 us; the launch traced here: 164 us
  Pallas kernels  65.9 us (40%)
  starting transfers between devices  54.3 us (33%)
  waiting for transfers between devices  25.5 us (15%)
  local copies, waits for them, and re-layouts  9.8 us (6%)
  other arithmetic  7.52 us (5%)
    pallas_call x15, Pallas kernels, block_sweep(): pl.pallas_call(functools.partial(sweep_kernel, coupled_terms=coupling is...  65.9 us
    ppermute x14, starting transfers between devices, exchange(): held = jnp.concatenate([held, lax.ppermute(held, 'sub', route)], axis=0)  43.9 us
    ppermute x14, waiting for transfers between devices, exchange(): held = jnp.concatenate([held, lax.ppermute(held, 'sub', route)], axis=0)  21.6 us
    ppermute x7, starting transfers between devices, partner(): return lax.ppermute(block, axis, route)  10.4 us
    unnamed x31, local copies, waits for them, and re-layouts  4.3 us
    ppermute x7, waiting for transfers between devices, partner(): return lax.ppermute(block, axis, route)  3.92 us
  transfers between devices with their start and end apart: 21, of which 14 were waited for; matrix products, arithmetic and copies ran while one was open for 4% of the time, Pallas kernels for 23%

profile of v3, /device:TPU:1, one launch (start us, length us, event | category | flops | bytes accessed | tf_op | source)
XLA Modules:
  0.0 163.8 jit_solution(11206538372829725179)
XLA Ops:
  1.4 0.8 gather_fusion
  2.8 1.4 multiply_add_fusion.refs_1_.refs_5_
  4.2 1.6 shard_map.114
  5.8 3.6 %collective-permute-start = (f32[2,1,128]{2,1,0:T(1,128)}, f32[2,1,128]{2,1,0:T(1,128)S(1)}, u32[]{:S(2)}, u32[]{:S(2)}) collective-permute-start(f32[2,1,128]{2,1,0:T(1,128)} %shard_map.114), channel_id=1, source_target_pairs={{0,1},{1,0},{2,3},{3,2},{4,5},{5,4},{6,7},{7,6},{8,9},{9,8},{10,11... | collective-permute-start | bytes 3080 | tf_op jit(solution)/shard_map/ppermute | solution.py:22
  9.4 0.8 bitcast_add_fusion
  14.4 2.8 %shard_map.113.refs_3_ = f32[40,1,128]{2,1,0:T(1,128)} custom-call(f32[40,128,128]{2,1,0:T(8,128)} %bitcast.44, f32[40,1,128]{2,1,0:T(1,128)} %bitcast.62), custom_call_target="tpu_custom_call" | custom-call | flops 1310720 | bytes 2621440 | tf_op jit(solution)/shard_map/pallas_call | solution.py:78
  17.9 2.6 %shard_map.116 = f32[2,1,128]{2,1,0:T(1,128)} custom-call(s32[240]{0:T(256)} %reshape_squeeze.6.refs_0_, bf16[40,6,128,128]{3,2,1,0:T(8,128)(2,1)} %bitcast.30, f32[40,128,128]{2,1,0:T(8,128)} %bitcast.45, f32[40,1,128]{2,1,0:T(1,128)} %shard_map.113.refs_3_, f32[2,1,128]{2,1,0:T(1,128)} %copy-done.4, f32[40,1,128]{2,1,0:T(1,128)} %multiply_add_fusion.refs_1_.refs_5_, ...), custom_call_target="tpu_custom_call" | custom-call | flops 458752 | bytes 524288 | tf_op jit(solution)/shard_map/pallas_call | solution.py:78
  20.4 6.6 %shard_map.115.refs_3_ = f32[40,1,128]{2,1,0:T(1,128)} custom-call(s32[240]{0:T(256)} %reshape_squeeze.6.refs_0_, bf16[40,6,128,128]{3,2,1,0:T(8,128)(2,1)} %bitcast.31, f32[40,128,128]{2,1,0:T(8,128)} %bitcast.46, f32[40,1,128]{2,1,0:T(1,128)} %shard_map.113.refs_3_, f32[2,1,128]{2,1,0:T(1,128)} %copy-done.4, f32[40,1,128]{2,1,0:T(1,128)} %bitcast.63, ...), custom_call_target="tpu_custom_call" | custom-call | flops 9175040 | bytes 10485760 | tf_op jit(solution)/shard_map/pallas_call | solution.py:78
  27.5 2.6 %shard_map.118 = f32[2,1,128]{2,1,0:T(1,128)} custom-call(s32[240]{0:T(256)} %reshape_squeeze.6.refs_0_, bf16[40,6,128,128]{3,2,1,0:T(8,128)(2,1)} %bitcast.32, f32[40,128,128]{2,1,0:T(8,128)} %bitcast.47, f32[40,1,128]{2,1,0:T(1,128)} %shard_map.115.refs_3_, f32[2,1,128]{2,1,0:T(1,128)} %copy-done.5, f32[40,1,128]{2,1,0:T(1,128)} %multiply_add_fusion.refs_1_.refs_5_, ...), custom_call_target="tpu_custom_call" | custom-call | flops 458752 | bytes 524288 | tf_op jit(solution)/shard_map/pallas_call | solution.py:78
  30.1 3.0 %collective-permute-start.2 = (f32[2,1,128]{2,1,0:T(1,128)}, f32[2,1,128]{2,1,0:T(1,128)S(1)}, u32[]{:S(2)}, u32[]{:S(2)}) collective-permute-start(f32[2,1,128]{2,1,0:T(1,128)} %shard_map.118), channel_id=1, source_target_pairs={{0,1},{1,0},{2,3},{3,2},{4,5},{5,4},{6,7},{7,6},{8,9},{9,8},{10,11... | collective-permute-start | bytes 3080 | tf_op jit(solution)/shard_map/ppermute | solution.py:22
  33.2 6.6 %shard_map.117.refs_3_ = f32[40,1,128]{2,1,0:T(1,128)} custom-call(s32[240]{0:T(256)} %reshape_squeeze.6.refs_0_, bf16[40,6,128,128]{3,2,1,0:T(8,128)(2,1)} %bitcast.33, f32[40,128,128]{2,1,0:T(8,128)} %bitcast.48, f32[40,1,128]{2,1,0:T(1,128)} %shard_map.115.refs_3_, f32[2,1,128]{2,1,0:T(1,128)} %copy-done.5, f32[40,1,128]{2,1,0:T(1,128)} %bitcast.64, ...), custom_call_target="tpu_custom_call" | custom-call | flops 9175040 | bytes 10485760 | tf_op jit(solution)/shard_map/pallas_call | solution.py:78
  40.3 6.6 %shard_map.119.refs_3_ = f32[40,1,128]{2,1,0:T(1,128)} custom-call(s32[240]{0:T(256)} %reshape_squeeze.6.refs_0_, bf16[40,6,128,128]{3,2,1,0:T(8,128)(2,1)} %bitcast.34, f32[40,128,128]{2,1,0:T(8,128)} %bitcast.49, f32[40,1,128]{2,1,0:T(1,128)} %shard_map.117.refs_3_, f32[2,1,128]{2,1,0:T(1,128)} %copy-done.6, f32[40,1,128]{2,1,0:T(1,128)} %bitcast.65, ...), custom_call_target="tpu_custom_call" | custom-call | flops 9175040 | bytes 10485760 | tf_op jit(solution)/shard_map/pallas_call | solution.py:78
  47.6 2.6 %shard_map.120 = f32[2,1,128]{2,1,0:T(1,128)} custom-call(s32[240]{0:T(256)} %reshape_squeeze.6.refs_0_, bf16[40,6,128,128]{3,2,1,0:T(8,128)(2,1)} %bitcast.35, f32[40,128,128]{2,1,0:T(8,128)} %bitcast.50, f32[40,1,128]{2,1,0:T(1,128)} %shard_map.117.refs_3_, f32[2,1,128]{2,1,0:T(1,128)} %copy-done.6, f32[40,1,128]{2,1,0:T(1,128)} %multiply_add_fusion.refs_1_.refs_5_, ...), custom_call_target="tpu_custom_call" | custom-call | flops 458752 | bytes 524288 | tf_op jit(solution)/shard_map/pallas_call | solution.py:78
  50.2 6.9 %collective-permute-start.4 = (f32[1,4,2,128]{3,2,1,0:T(2,128)S(1)}, f32[1,4,2,128]{3,2,1,0:T(2,128)S(1)}, u32[]{:S(2)}, u32[]{:S(2)}) collective-permute-start(f32[1,4,2,128]{3,2,1,0:T(2,128)S(1)} %bitcast.67), channel_id=1, source_target_pairs={{0,16},{2,18},{4,20},{6,22},{8,24},{10,26},{12,28},{14,30},{16,0},... | collective-permute-start | bytes 12296 | tf_op jit(solution)/shard_map/ppermute | solution.py:112
  57.2 1.0 collective-permute-done.4
  58.2 2.9 %collective-permute-start.5 = (f32[2,4,2,128]{3,2,1,0:T(2,128)S(1)}, f32[2,4,2,128]{3,2,1,0:T(2,128)S(1)}, u32[]{:S(2)}, u32[]{:S(2)}) collective-permute-start(f32[2,4,2,128]{3,2,1,0:T(2,128)S(1)} %pad_maximum_fusion.9), channel_id=1, source_target_pairs={{0,64},{2,66},{4,68},{6,70},{8,72},{10,74},{12,76},{14,78},{16,80}... | collective-permute-start | bytes 24584 | tf_op jit(solution)/shard_map/ppermute | solution.py:112
  61.1 1.1 collective-permute-done.5
  62.2 1.5 collective-permute-start.6
  63.9 3.9 %collective-permute-done.3.refs_4_ = f32[2,1,128]{2,1,0:T(1,128)S(1)} collective-permute-done((f32[2,1,128]{2,1,0:T(1,128)}, f32[2,1,128]{2,1,0:T(1,128)S(1)}, u32[]{:S(2)}, u32[]{:S(2)}) %collective-permute-start.3) | collective-permute-done | bytes 1056 | tf_op jit(solution)/shard_map/ppermute | solution.py:22
  68.4 2.6 %shard_map.121 = f32[2,1,128]{2,1,0:T(1,128)} custom-call(s32[240]{0:T(256)} %reshape_squeeze.6.refs_0_, bf16[40,6,128,128]{3,2,1,0:T(8,128)(2,1)} %bitcast.36, f32[40,128,128]{2,1,0:T(8,128)} %bitcast.51, f32[40,1,128]{2,1,0:T(1,128)} %shard_map.119.refs_3_, f32[2,1,128]{2,1,0:T(1,128)} %copy-done.2, f32[40,1,128]{2,1,0:T(1,128)} %multiply_add_fusion.refs_1_.refs_5_, ...), custom_call_target="tpu_custom_call" | custom-call | flops 458752 | bytes 524288 | tf_op jit(solution)/shard_map/pallas_call | solution.py:78
  71.4 2.5 %collective-permute-done.7 = f32[8,4,2,128]{3,2,1,0:T(2,128)S(1)} collective-permute-done((f32[8,4,2,128]{3,2,1,0:T(2,128)S(1)}, f32[8,4,2,128]{3,2,1,0:T(2,128)S(1)}, u32[]{:S(2)}, u32[]{:S(2)}) %collective-permute-start.7) | collective-permute-done | bytes 32800 | tf_op jit(solution)/shard_map/ppermute | solution.py:112
  73.9 1.4 collective-permute-start.8
  75.3 1.8 %collective-permute-done.8 = f32[16,4,2,128]{3,2,1,0:T(2,128)S(1)} collective-permute-done((f32[16,4,2,128]{3,2,1,0:T(2,128)S(1)}, f32[16,4,2,128]{3,2,1,0:T(2,128)S(1)}, u32[]{:S(2)}, u32[]{:S(2)}) %collective-permute-start.8) | collective-permute-done | bytes 65568 | tf_op jit(solution)/shard_map/ppermute | solution.py:112
  77.2 1.7 %collective-permute-start.9 = (f32[32,4,2,128]{3,2,1,0:T(2,128)S(1)}, f32[32,4,2,128]{3,2,1,0:T(2,128)S(1)}, u32[]{:S(2)}, u32[]{:S(2)}) collective-permute-start(f32[32,4,2,128]{3,2,1,0:T(2,128)S(1)} %pad_maximum_fusion.1), channel_id=1, source_target_pairs={{0,4},{2,6},{4,0},{6,2},{8,12},{10,14},{12,8},{14,10},{16,20},{18,... | collective-permute-start | bytes 393224 | tf_op jit(solution)/shard_map/ppermute | solution.py:112
  79.8 1.5 collective-permute-done.9
  81.4 8.8 %collective-permute-start.10 = (f32[64,4,2,128]{3,2,1,0:T(2,128)S(1)}, f32[64,4,2,128]{3,2,1,0:T(2,128)S(1)}, u32[]{:S(2)}, u32[]{:S(2)}) collective-permute-start(f32[64,4,2,128]{3,2,1,0:T(2,128)S(1)} %pad_maximum_fusion), channel_id=1, source_target_pairs={{0,2},{2,0},{4,6},{6,4},{8,10},{10,8},{12,14},{14,12},{16,18},{18,... | collective-permute-start | bytes 786440 | tf_op jit(solution)/shard_map/ppermute | solution.py:112
  90.2 1.1 collective-permute-done.10
  92.5 6.6 %shard_map.122.refs_3_ = f32[40,1,128]{2,1,0:T(1,128)} custom-call(s32[240]{0:T(256)} %reshape_squeeze.6.refs_0_, bf16[40,6,128,128]{3,2,1,0:T(8,128)(2,1)} %bitcast.37, f32[40,128,128]{2,1,0:T(8,128)} %bitcast.52, f32[40,1,128]{2,1,0:T(1,128)} %shard_map.119.refs_3_, f32[2,1,128]{2,1,0:T(1,128)} %copy-done.2, f32[40,1,128]{2,1,0:T(1,128)} %bitcast.58, ...), custom_call_target="tpu_custom_call" | custom-call | flops 9175040 | bytes 10485760 | tf_op jit(solution)/shard_map/pallas_call | solution.py:78
  99.6 2.6 %shard_map.124 = f32[2,1,128]{2,1,0:T(1,128)} custom-call(s32[240]{0:T(256)} %reshape_squeeze.6.refs_0_, bf16[40,6,128,128]{3,2,1,0:T(8,128)(2,1)} %bitcast.38, f32[40,128,128]{2,1,0:T(8,128)} %bitcast.53, f32[40,1,128]{2,1,0:T(1,128)} %shard_map.122.refs_3_, f32[2,1,128]{2,1,0:T(1,128)} %copy-done.3, f32[40,1,128]{2,1,0:T(1,128)} %multiply_add_fusion.refs_1_.refs_5_, ...), custom_call_target="tpu_custom_call" | custom-call | flops 458752 | bytes 524288 | tf_op jit(solution)/shard_map/pallas_call | solution.py:78
  102.7 6.6 %shard_map.123.refs_3_ = f32[40,1,128]{2,1,0:T(1,128)} custom-call(s32[240]{0:T(256)} %reshape_squeeze.6.refs_0_, bf16[40,6,128,128]{3,2,1,0:T(8,128)(2,1)} %bitcast.39, f32[40,128,128]{2,1,0:T(8,128)} %bitcast.54, f32[40,1,128]{2,1,0:T(1,128)} %shard_map.122.refs_3_, f32[2,1,128]{2,1,0:T(1,128)} %copy-done.3, f32[40,1,128]{2,1,0:T(1,128)} %bitcast.59, ...), custom_call_target="tpu_custom_call" | custom-call | flops 9175040 | bytes 10485760 | tf_op jit(solution)/shard_map/pallas_call | solution.py:78
  109.8 2.6 %shard_map.126 = f32[2,1,128]{2,1,0:T(1,128)} custom-call(s32[240]{0:T(256)} %reshape_squeeze.6.refs_0_, bf16[40,6,128,128]{3,2,1,0:T(8,128)(2,1)} %bitcast.40, f32[40,128,128]{2,1,0:T(8,128)} %bitcast.55, f32[40,1,128]{2,1,0:T(1,128)} %shard_map.123.refs_3_, f32[2,1,128]{2,1,0:T(1,128)} %copy-done.7, f32[40,1,128]{2,1,0:T(1,128)} %multiply_add_fusion.refs_1_.refs_5_, ...), custom_call_target="tpu_custom_call" | custom-call | flops 458752 | bytes 524288 | tf_op jit(solution)/shard_map/pallas_call | solution.py:78
  112.4 2.5 %collective-permute-start.13 = (f32[2,1,128]{2,1,0:T(1,128)}, f32[2,1,128]{2,1,0:T(1,128)S(1)}, u32[]{:S(2)}, u32[]{:S(2)}) collective-permute-start(f32[2,1,128]{2,1,0:T(1,128)} %shard_map.126), channel_id=1, source_target_pairs={{0,1},{1,0},{2,3},{3,2},{4,5},{5,4},{6,7},{7,6},{8,9},{9,8},{10,11... | collective-permute-start | bytes 3080 | tf_op jit(solution)/shard_map/ppermute | solution.py:22
  114.9 6.6 %shard_map.125.refs_3_ = f32[40,1,128]{2,1,0:T(1,128)} custom-call(s32[240]{0:T(256)} %reshape_squeeze.6.refs_0_, bf16[40,6,128,128]{3,2,1,0:T(8,128)(2,1)} %bitcast.41, f32[40,128,128]{2,1,0:T(8,128)} %bitcast.56, f32[40,1,128]{2,1,0:T(1,128)} %shard_map.123.refs_3_, f32[2,1,128]{2,1,0:T(1,128)} %copy-done.7, f32[40,1,128]{2,1,0:T(1,128)} %bitcast.60, ...), custom_call_target="tpu_custom_call" | custom-call | flops 9175040 | bytes 10485760 | tf_op jit(solution)/shard_map/pallas_call | solution.py:78
  122.0 6.6 %shard_map.127 = f32[40,1,128]{2,1,0:T(1,128)} custom-call(s32[240]{0:T(256)} %reshape_squeeze.6.refs_0_, bf16[40,6,128,128]{3,2,1,0:T(8,128)(2,1)} %bitcast.42, f32[40,128,128]{2,1,0:T(8,128)} %bitcast.57, f32[40,1,128]{2,1,0:T(1,128)} %shard_map.125.refs_3_, f32[2,1,128]{2,1,0:T(1,128)} %copy-done.9, f32[40,1,128]{2,1,0:T(1,128)} %bitcast.61, ...), custom_call_target="tpu_custom_call" | custom-call | flops 9175040 | bytes 10485760 | tf_op jit(solution)/shard_map/pallas_call | solution.py:78
  129.4 5.1 %collective-permute-start.14 = (f32[1,4,2,128]{3,2,1,0:T(2,128)S(1)}, f32[1,4,2,128]{3,2,1,0:T(2,128)S(1)}, u32[]{:S(2)}, u32[]{:S(2)}) collective-permute-start(f32[1,4,2,128]{3,2,1,0:T(2,128)S(1)} %get-tuple-element.9), channel_id=1, source_target_pairs={{0,16},{2,18},{4,20},{6,22},{8,24},{10,26},{12,28},{14,30},{16,0},... | collective-permute-start | bytes 12296 | tf_op jit(solution)/shard_map/ppermute | solution.py:112
  134.5 1.2 collective-permute-done.14
  135.8 2.9 %collective-permute-start.15 = (f32[2,4,2,128]{3,2,1,0:T(2,128)S(1)}, f32[2,4,2,128]{3,2,1,0:T(2,128)S(1)}, u32[]{:S(2)}, u32[]{:S(2)}) collective-permute-start(f32[2,4,2,128]{3,2,1,0:T(2,128)S(1)} %pad_maximum_fusion.10), channel_id=1, source_target_pairs={{0,64},{2,66},{4,68},{6,70},{8,72},{10,74},{12,76},{14,78},{16,80}... | collective-permute-start | bytes 24584 | tf_op jit(solution)/shard_map/ppermute | solution.py:112
  138.7 1.1 collective-permute-done.15
  139.8 1.0 collective-permute-start.16
  140.8 2.6 %collective-permute-done.16 = f32[4,4,2,128]{3,2,1,0:T(2,128)S(1)} collective-permute-done((f32[4,4,2,128]{3,2,1,0:T(2,128)S(1)}, f32[4,4,2,128]{3,2,1,0:T(2,128)S(1)}, u32[]{:S(2)}, u32[]{:S(2)}) %collective-permute-start.16) | collective-permute-done | bytes 16416 | tf_op jit(solution)/shard_map/ppermute | solution.py:112
  143.8 2.4 %collective-permute-done.17 = f32[8,4,2,128]{3,2,1,0:T(2,128)S(1)} collective-permute-done((f32[8,4,2,128]{3,2,1,0:T(2,128)S(1)}, f32[8,4,2,128]{3,2,1,0:T(2,128)S(1)}, u32[]{:S(2)}, u32[]{:S(2)}) %collective-permute-start.17) | collective-permute-done | bytes 32800 | tf_op jit(solution)/shard_map/ppermute | solution.py:112
  146.3 1.4 collective-permute-start.18
  147.7 1.8 %collective-permute-done.18 = f32[16,4,2,128]{3,2,1,0:T(2,128)S(1)} collective-permute-done((f32[16,4,2,128]{3,2,1,0:T(2,128)S(1)}, f32[16,4,2,128]{3,2,1,0:T(2,128)S(1)}, u32[]{:S(2)}, u32[]{:S(2)}) %collective-permute-start.18) | collective-permute-done | bytes 65568 | tf_op jit(solution)/shard_map/ppermute | solution.py:112
  149.6 1.7 %collective-permute-start.19 = (f32[32,4,2,128]{3,2,1,0:T(2,128)S(1)}, f32[32,4,2,128]{3,2,1,0:T(2,128)S(1)}, u32[]{:S(2)}, u32[]{:S(2)}) collective-permute-start(f32[32,4,2,128]{3,2,1,0:T(2,128)S(1)} %get-tuple-element.14), channel_id=1, source_target_pairs={{0,4},{2,6},{4,0},{6,2},{8,12},{10,14},{12,8},{14,10},{16,20},{18,... | collective-permute-start | bytes 393224 | tf_op jit(solution)/shard_map/ppermute | solution.py:112
  151.3 2.4 %collective-permute-done.19 = f32[32,4,2,128]{3,2,1,0:T(2,128)S(1)} collective-permute-done((f32[32,4,2,128]{3,2,1,0:T(2,128)S(1)}, f32[32,4,2,128]{3,2,1,0:T(2,128)S(1)}, u32[]{:S(2)}, u32[]{:S(2)}) %collective-permute-start.19) | collective-permute-done | bytes 131104 | tf_op jit(solution)/shard_map/ppermute | solution.py:112
  153.7 7.7 %collective-permute-start.20 = (f32[64,4,2,128]{3,2,1,0:T(2,128)S(1)}, f32[64,4,2,128]{3,2,1,0:T(2,128)S(1)}, u32[]{:S(2)}, u32[]{:S(2)}) collective-permute-start(f32[64,4,2,128]{3,2,1,0:T(2,128)S(1)} %get-tuple-element.10), channel_id=1, source_target_pairs={{0,2},{2,0},{4,6},{6,4},{8,10},{10,8},{12,14},{14,12},{16,18},{18,... | collective-permute-start | bytes 786440 | tf_op jit(solution)/shard_map/ppermute | solution.py:112
  161.5 1.2 collective-permute-done.20
  162.7 1.2 gather_fusion.2
  (77 shorter events, 15.3 us)
Async XLA Ops:
  0.6 0.7 copy-start
  5.8 11.3 %collective-permute-start = (f32[2,1,128]{2,1,0:T(1,128)}, f32[2,1,128]{2,1,0:T(1,128)S(1)}, u32[]{:S(2)}, u32[]{:S(2)}) collective-permute-start(f32[2,1,128]{2,1,0:T(1,128)} %shard_map.114), channel_id=1, source_target_pairs={{0,1},{1,0},{2,3},{3,2},{4,5},{5,4},{6,7},{7,6},{8,9},{9,8},{10,11... | collective-permute-start | bytes 3080 | tf_op jit(solution)/shard_map/ppermute | solution.py:22
  17.1 0.7 copy-start.4
  20.4 6.6 %collective-permute-start.1 = (f32[2,1,128]{2,1,0:T(1,128)}, f32[2,1,128]{2,1,0:T(1,128)S(1)}, u32[]{:S(2)}, u32[]{:S(2)}) collective-permute-start(f32[2,1,128]{2,1,0:T(1,128)} %shard_map.116), channel_id=1, source_target_pairs={{0,1},{1,0},{2,3},{3,2},{4,5},{5,4},{6,7},{7,6},{8,9},{9,8},{10,11... | collective-permute-start | bytes 3080 | tf_op jit(solution)/shard_map/ppermute | solution.py:22
  27.0 0.5 copy-start.5
  30.1 9.6 %collective-permute-start.2 = (f32[2,1,128]{2,1,0:T(1,128)}, f32[2,1,128]{2,1,0:T(1,128)S(1)}, u32[]{:S(2)}, u32[]{:S(2)}) collective-permute-start(f32[2,1,128]{2,1,0:T(1,128)} %shard_map.118), channel_id=1, source_target_pairs={{0,1},{1,0},{2,3},{3,2},{4,5},{5,4},{6,7},{7,6},{8,9},{9,8},{10,11... | collective-permute-start | bytes 3080 | tf_op jit(solution)/shard_map/ppermute | solution.py:22
  39.7 7.8 %copy-start.1 = (f32[1,1,4,2,128]{4,3,2,1,0:T(2,128)S(1)}, f32[1,1,4,2,128]{4,3,2,1,0:T(2,128)}, u32[]{:S(2)}) copy-start(f32[1,1,4,2,128]{4,3,2,1,0:T(2,128)} %param.19) | copy-start | bytes 12292
  39.7 0.6 copy-start.6
  50.2 28.6 %copy-start.8 = (s32[4,128]{1,0:T(4,128)S(1)}, s32[4,128]{1,0:T(4,128)}, u32[]{:S(2)}) copy-start(s32[4,128]{1,0:T(4,128)} %param.18) | copy-start | bytes 6148
  50.2 7.9 %collective-permute-start.4 = (f32[1,4,2,128]{3,2,1,0:T(2,128)S(1)}, f32[1,4,2,128]{3,2,1,0:T(2,128)S(1)}, u32[]{:S(2)}, u32[]{:S(2)}) collective-permute-start(f32[1,4,2,128]{3,2,1,0:T(2,128)S(1)} %bitcast.67), channel_id=1, source_target_pairs={{0,16},{2,18},{4,20},{6,22},{8,24},{10,26},{12,28},{14,30},{16,0},... | collective-permute-start | bytes 12296 | tf_op jit(solution)/shard_map/ppermute | solution.py:112
  58.2 4.0 %collective-permute-start.5 = (f32[2,4,2,128]{3,2,1,0:T(2,128)S(1)}, f32[2,4,2,128]{3,2,1,0:T(2,128)S(1)}, u32[]{:S(2)}, u32[]{:S(2)}) collective-permute-start(f32[2,4,2,128]{3,2,1,0:T(2,128)S(1)} %pad_maximum_fusion.9), channel_id=1, source_target_pairs={{0,64},{2,66},{4,68},{6,70},{8,72},{10,74},{12,76},{14,78},{16,80}... | collective-permute-start | bytes 24584 | tf_op jit(solution)/shard_map/ppermute | solution.py:112
  62.2 8.8 %collective-permute-start.6 = (f32[4,4,2,128]{3,2,1,0:T(2,128)S(1)}, f32[4,4,2,128]{3,2,1,0:T(2,128)S(1)}, u32[]{:S(2)}, u32[]{:S(2)}) collective-permute-start(f32[4,4,2,128]{3,2,1,0:T(2,128)S(1)} %pad_maximum_fusion.7), channel_id=1, source_target_pairs={{0,8},{2,10},{4,12},{6,14},{8,0},{10,2},{12,4},{14,6},{16,24},{18,... | collective-permute-start | bytes 49160 | tf_op jit(solution)/shard_map/ppermute | solution.py:112
  63.7 4.1 %collective-permute-start.3 = (f32[2,1,128]{2,1,0:T(1,128)}, f32[2,1,128]{2,1,0:T(1,128)S(1)}, u32[]{:S(2)}, u32[]{:S(2)}) collective-permute-start(f32[2,1,128]{2,1,0:T(1,128)} %shard_map.120), channel_id=1, source_target_pairs={{0,1},{1,0},{2,3},{3,2},{4,5},{5,4},{6,7},{7,6},{8,9},{9,8},{10,11... | collective-permute-start | bytes 3080 | tf_op jit(solution)/shard_map/ppermute | solution.py:22
  67.8 0.5 copy-start.2
  71.0 2.9 %collective-permute-start.7 = (f32[8,4,2,128]{3,2,1,0:T(2,128)S(1)}, f32[8,4,2,128]{3,2,1,0:T(2,128)S(1)}, u32[]{:S(2)}, u32[]{:S(2)}) collective-permute-start(f32[8,4,2,128]{3,2,1,0:T(2,128)S(1)} %pad_maximum_fusion.3), channel_id=1, source_target_pairs={{0,128},{2,130},{4,132},{6,134},{8,136},{10,138},{12,140},{14,142}... | collective-permute-start | bytes 98312 | tf_op jit(solution)/shard_map/ppermute | solution.py:112
  73.9 3.2 %collective-permute-start.8 = (f32[16,4,2,128]{3,2,1,0:T(2,128)S(1)}, f32[16,4,2,128]{3,2,1,0:T(2,128)S(1)}, u32[]{:S(2)}, u32[]{:S(2)}) collective-permute-start(f32[16,4,2,128]{3,2,1,0:T(2,128)S(1)} %pad_maximum_fusion.2), channel_id=1, source_target_pairs={{0,32},{2,34},{4,36},{6,38},{8,40},{10,42},{12,44},{14,46},{16,48}... | collective-permute-start | bytes 196616 | tf_op jit(solution)/shard_map/ppermute | solution.py:112
  77.2 4.1 %collective-permute-start.9 = (f32[32,4,2,128]{3,2,1,0:T(2,128)S(1)}, f32[32,4,2,128]{3,2,1,0:T(2,128)S(1)}, u32[]{:S(2)}, u32[]{:S(2)}) collective-permute-start(f32[32,4,2,128]{3,2,1,0:T(2,128)S(1)} %pad_maximum_fusion.1), channel_id=1, source_target_pairs={{0,4},{2,6},{4,0},{6,2},{8,12},{10,14},{12,8},{14,10},{16,20},{18,... | collective-permute-start | bytes 393224 | tf_op jit(solution)/shard_map/ppermute | solution.py:112
  79.1 20.0 %collective-permute-start.11 = (f32[2,1,128]{2,1,0:T(1,128)}, f32[2,1,128]{2,1,0:T(1,128)S(1)}, u32[]{:S(2)}, u32[]{:S(2)}) collective-permute-start(f32[2,1,128]{2,1,0:T(1,128)} %shard_map.121), channel_id=1, source_target_pairs={{0,1},{1,0},{2,3},{3,2},{4,5},{5,4},{6,7},{7,6},{8,9},{9,8},{10,11... | collective-permute-start | bytes 3080 | tf_op jit(solution)/shard_map/ppermute | solution.py:22
  81.4 10.0 %collective-permute-start.10 = (f32[64,4,2,128]{3,2,1,0:T(2,128)S(1)}, f32[64,4,2,128]{3,2,1,0:T(2,128)S(1)}, u32[]{:S(2)}, u32[]{:S(2)}) collective-permute-start(f32[64,4,2,128]{3,2,1,0:T(2,128)S(1)} %pad_maximum_fusion), channel_id=1, source_target_pairs={{0,2},{2,0},{4,6},{6,4},{8,10},{10,8},{12,14},{14,12},{16,18},{18,... | collective-permute-start | bytes 786440 | tf_op jit(solution)/shard_map/ppermute | solution.py:112
  99.1 0.5 copy-start.3
  102.2 7.1 %collective-permute-start.12 = (f32[2,1,128]{2,1,0:T(1,128)}, f32[2,1,128]{2,1,0:T(1,128)S(1)}, u32[]{:S(2)}, u32[]{:S(2)}) collective-permute-start(f32[2,1,128]{2,1,0:T(1,128)} %shard_map.124), channel_id=1, source_target_pairs={{0,1},{1,0},{2,3},{3,2},{4,5},{5,4},{6,7},{7,6},{8,9},{9,8},{10,11... | collective-permute-start | bytes 3080 | tf_op jit(solution)/shard_map/ppermute | solution.py:22
  109.3 0.6 copy-start.7
  112.4 9.1 %collective-permute-start.13 = (f32[2,1,128]{2,1,0:T(1,128)}, f32[2,1,128]{2,1,0:T(1,128)S(1)}, u32[]{:S(2)}, u32[]{:S(2)}) collective-permute-start(f32[2,1,128]{2,1,0:T(1,128)} %shard_map.126), channel_id=1, source_target_pairs={{0,1},{1,0},{2,3},{3,2},{4,5},{5,4},{6,7},{7,6},{8,9},{9,8},{10,11... | collective-permute-start | bytes 3080 | tf_op jit(solution)/shard_map/ppermute | solution.py:22
  121.5 0.5 copy-start.9
  129.4 6.4 %collective-permute-start.14 = (f32[1,4,2,128]{3,2,1,0:T(2,128)S(1)}, f32[1,4,2,128]{3,2,1,0:T(2,128)S(1)}, u32[]{:S(2)}, u32[]{:S(2)}) collective-permute-start(f32[1,4,2,128]{3,2,1,0:T(2,128)S(1)} %get-tuple-element.9), channel_id=1, source_target_pairs={{0,16},{2,18},{4,20},{6,22},{8,24},{10,26},{12,28},{14,30},{16,0},... | collective-permute-start | bytes 12296 | tf_op jit(solution)/shard_map/ppermute | solution.py:112
  135.8 4.0 %collective-permute-start.15 = (f32[2,4,2,128]{3,2,1,0:T(2,128)S(1)}, f32[2,4,2,128]{3,2,1,0:T(2,128)S(1)}, u32[]{:S(2)}, u32[]{:S(2)}) collective-permute-start(f32[2,4,2,128]{3,2,1,0:T(2,128)S(1)} %pad_maximum_fusion.10), channel_id=1, source_target_pairs={{0,64},{2,66},{4,68},{6,70},{8,72},{10,74},{12,76},{14,78},{16,80}... | collective-permute-start | bytes 24584 | tf_op jit(solution)/shard_map/ppermute | solution.py:112
  139.8 3.6 %collective-permute-start.16 = (f32[4,4,2,128]{3,2,1,0:T(2,128)S(1)}, f32[4,4,2,128]{3,2,1,0:T(2,128)S(1)}, u32[]{:S(2)}, u32[]{:S(2)}) collective-permute-start(f32[4,4,2,128]{3,2,1,0:T(2,128)S(1)} %pad_maximum_fusion.8), channel_id=1, source_target_pairs={{0,8},{2,10},{4,12},{6,14},{8,0},{10,2},{12,4},{14,6},{16,24},{18,... | collective-permute-start | bytes 49160 | tf_op jit(solution)/shard_map/ppermute | solution.py:112
  143.4 2.9 %collective-permute-start.17 = (f32[8,4,2,128]{3,2,1,0:T(2,128)S(1)}, f32[8,4,2,128]{3,2,1,0:T(2,128)S(1)}, u32[]{:S(2)}, u32[]{:S(2)}) collective-permute-start(f32[8,4,2,128]{3,2,1,0:T(2,128)S(1)} %pad_maximum_fusion.4), channel_id=1, source_target_pairs={{0,128},{2,130},{4,132},{6,134},{8,136},{10,138},{12,140},{14,142}... | collective-permute-start | bytes 98312 | tf_op jit(solution)/shard_map/ppermute | solution.py:112
  146.3 3.2 %collective-permute-start.18 = (f32[16,4,2,128]{3,2,1,0:T(2,128)S(1)}, f32[16,4,2,128]{3,2,1,0:T(2,128)S(1)}, u32[]{:S(2)}, u32[]{:S(2)}) collective-permute-start(f32[16,4,2,128]{3,2,1,0:T(2,128)S(1)} %get-tuple-element.18), channel_id=1, source_target_pairs={{0,32},{2,34},{4,36},{6,38},{8,40},{10,42},{12,44},{14,46},{16,48}... | collective-permute-start | bytes 196616 | tf_op jit(solution)/shard_map/ppermute | solution.py:112
  149.6 4.1 %collective-permute-start.19 = (f32[32,4,2,128]{3,2,1,0:T(2,128)S(1)}, f32[32,4,2,128]{3,2,1,0:T(2,128)S(1)}, u32[]{:S(2)}, u32[]{:S(2)}) collective-permute-start(f32[32,4,2,128]{3,2,1,0:T(2,128)S(1)} %get-tuple-element.14), channel_id=1, source_target_pairs={{0,4},{2,6},{4,0},{6,2},{8,12},{10,14},{12,8},{14,10},{16,20},{18,... | collective-permute-start | bytes 393224 | tf_op jit(solution)/shard_map/ppermute | solution.py:112
  153.7 8.9 %collective-permute-start.20 = (f32[64,4,2,128]{3,2,1,0:T(2,128)S(1)}, f32[64,4,2,128]{3,2,1,0:T(2,128)S(1)}, u32[]{:S(2)}, u32[]{:S(2)}) collective-permute-start(f32[64,4,2,128]{3,2,1,0:T(2,128)S(1)} %get-tuple-element.10), channel_id=1, source_target_pairs={{0,2},{2,0},{4,6},{6,4},{8,10},{10,8},{12,14},{14,12},{16,18},{18,... | collective-permute-start | bytes 786440 | tf_op jit(solution)/shard_map/ppermute | solution.py:112

commit v4 on v3

--- a/solution.py
+++ b/solution.py
@@ -87,6 +87,33 @@
     )(*operands)
 
 
+def head_kernel(cols_ref, c_ref, inv_ref, state_ref, ghost_ref, f_ref, o_ref, *, blocks):
+    rows, bands = c_ref.shape[0], c_ref.shape[1]
+    for r in range(rows):
+        acc = None
+        for b in range(bands):
+            col = cols_ref[r * bands + b]
+            own = state_ref[jnp.minimum(col, blocks - 1)]
+            other = ghost_ref[jnp.maximum(col - blocks, 0)]
+            xb = jnp.where(col >= blocks, other, own)
+            term = c_ref[r, b].astype(jnp.float32) * xb
+            acc = term if acc is None else acc + term
+        y = f_ref[r] - jnp.sum(acc.T, axis=0, keepdims=True)
+        o_ref[r] = jnp.sum((inv_ref[r] * y).T, axis=0, keepdims=True)
+
+
+def head_sweep(cols, tile, inv, state, ghost, f):
+    blocks, width = state.shape[0], state.shape[2]
+    in_vmem = pl.BlockSpec(memory_space=pltpu.VMEM)
+    in_smem = pl.BlockSpec(memory_space=pltpu.SMEM)
+    return pl.pallas_call(
+        functools.partial(head_kernel, blocks=blocks),
+        in_specs=[in_smem, in_vmem, in_vmem, in_vmem, in_vmem, in_vmem],
+        out_specs=in_vmem,
+        out_shape=jax.ShapeDtypeStruct((tile.shape[0], 1, width), jnp.float32),
+    )(cols, tile, inv, state, ghost, f)
+
+
 def doubling_order(bits):
     if bits == 7:
         return [3, 5, 2, 6, 4, 1, 0]
@@ -151,7 +178,16 @@
     flat_columns = columns.reshape(-1)
     prows = jnp.concatenate([p_face, jnp.zeros((blocks - iface,), jnp.float32)])[:, None, None] * jnp.ones((1, 1, width), jnp.float32)
 
+    bands = couple.shape[3]
+    head_tables = (
+        flat_columns[(blocks - G) * bands:],
+        couple[0, 0, blocks - G:],
+        inverse[blocks - G:],
+    )
+
     def sweep_rows(state, ghost, forcing, rows, first, count):
+        if state is not None and rows == G and first * G == blocks - G and blocks - G >= iface:
+            return head_sweep(*head_tables, state, ghost, forcing[blocks - G:])
         if state is None:
             return block_sweep(inverse, forcing, rows, first, count)
         coupling = (flat_columns, couple[0, 0], state, ghost, prows)

time: 165 us -> 167 us (1.012)
  local copies, waits for them, and re-layouts: 9.8 us -> 15.9 us
  Pallas kernels: 65.9 us -> 61.9 us
    pallas_call x15 -> x9, Pallas kernels: 65.9 us -> 50.3 us  [block_sweep(): pl.pallas_call(functools.partial(sweep_kernel, coupled_terms=coupling is...]
    pallas_call x0 -> x6, Pallas kernels: none -> 11.6 us  [head_sweep(): pl.pallas_call(functools.partial(head_kernel, blocks=blocks), in_specs=[i...]
    slice x0 -> x5, local copies, waits for them, and re-layouts: none -> 3.58 us  [the longest x1 1.57 us: per_device(): inverse[blocks - G:]]
    squeeze x0 -> x1, local copies, waits for them, and re-layouts: none -> 1.76 us  [per_device(): couple[0, 0, blocks - G:]]
  transfers between devices with their start and end apart: 21 -> 21, of which waited for: 14 -> 14; matrix products, arithmetic and copies ran while one was open for 4% -> 8% of each run, Pallas kernels for 23% -> 23%
where the time goes in v4:
time: 167 us; the launch traced here: 166 us
  Pallas kernels  61.9 us (37%)
  starting transfers between devices  54.3 us (33%)
  waiting for transfers between devices  25.6 us (15%)
  local copies, waits for them, and re-layouts  15.9 us (10%)
  other arithmetic  7.52 us (5%)
    pallas_call x9, Pallas kernels, block_sweep(): pl.pallas_call(functools.partial(sweep_kernel, coupled_terms=coupling is...  50.3 us
    ppermute x14, starting transfers between devices, exchange(): held = jnp.concatenate([held, lax.ppermute(held, 'sub', route)], axis=0)  43.9 us
    ppermute x14, waiting for transfers between devices, exchange(): held = jnp.concatenate([held, lax.ppermute(held, 'sub', route)], axis=0)  21.6 us
    pallas_call x6, Pallas kernels, head_sweep(): pl.pallas_call(functools.partial(head_kernel, blocks=blocks), in_specs=[i...  11.6 us
    ppermute x7, starting transfers between devices, partner(): return lax.ppermute(block, axis, route)  10.4 us
    unnamed x31, local copies, waits for them, and re-layouts  5.02 us
    ppermute x7, waiting for transfers between devices, partner(): return lax.ppermute(block, axis, route)  3.92 us
  transfers between devices with their start and end apart: 21, of which 14 were waited for; matrix products, arithmetic and copies ran while one was open for 8% of the time, Pallas kernels for 23%

profile of v4, /device:TPU:1, one launch (start us, length us, event | category | flops | bytes accessed | tf_op | source)
XLA Modules:
  0.0 166.0 jit_solution(11556732824016508559)
XLA Ops:
  2.8 1.4 multiply_add_fusion.refs_1_
  4.2 1.6 shard_map.114
  5.8 3.6 %collective-permute-start = (f32[2,1,128]{2,1,0:T(1,128)}, f32[2,1,128]{2,1,0:T(1,128)S(1)}, u32[]{:S(2)}, u32[]{:S(2)}) collective-permute-start(f32[2,1,128]{2,1,0:T(1,128)} %shard_map.114), channel_id=1, source_target_pairs={{0,1},{1,0},{2,3},{3,2},{4,5},{5,4},{6,7},{7,6},{8,9},{9,8},{10,11... | collective-permute-start | bytes 3080 | tf_op jit(solution)/shard_map/ppermute | solution.py:22
  10.2 1.6 slice_bitcast_fusion.1.inv_ref
  12.4 1.8 %slice_bitcast_fusion.c_ref = bf16[2,6,128,128]{3,2,1,0:T(8,128)(2,1)} fusion(bf16[1,1,40,6,128,128]{5,4,3,2,1,0:T(8,128)(2,1)} %param.12), kind=kLoop, calls=%fused_computation.3 | loop fusion | bytes 786432 | tf_op jit(solution)/shard_map/squeeze | solution.py:184
  19.0 2.8 %shard_map.113.refs_3_.state_ref = f32[40,1,128]{2,1,0:T(1,128)} custom-call(f32[40,128,128]{2,1,0:T(8,128)} %bitcast.45, f32[40,1,128]{2,1,0:T(1,128)} %bitcast.57), custom_call_target="tpu_custom_call" | custom-call | flops 1310720 | bytes 2621440 | tf_op jit(solution)/shard_map/pallas_call | solution.py:78
  22.4 1.9 %shard_map.116 = f32[2,1,128]{2,1,0:T(1,128)} custom-call(s32[12]{0:T(128)} %slice.57.cols_ref, bf16[2,6,128,128]{3,2,1,0:T(8,128)(2,1)} %slice_bitcast_fusion.c_ref, f32[2,128,128]{2,1,0:T(8,128)} %slice_bitcast_fusion.1.inv_ref, f32[40,1,128]{2,1,0:T(1,128)} %shard_map.113.refs_3_.state_ref, f32[2,1,128]{2,1,0:T(1,128)} %copy-done.4, f32[2,1,128]{2,1,0:T(1,128)} %bitcast.66), custom_call_target="tpu_custom_call" | custom-call | tf_op jit(solution)/shard_map/pallas_call | solution.py:109
  25.7 6.6 %shard_map.115.refs_3_.state_ref = f32[40,1,128]{2,1,0:T(1,128)} custom-call(s32[240]{0:T(256)} %reshape_squeeze.6.refs_0_, bf16[40,6,128,128]{3,2,1,0:T(8,128)(2,1)} %bitcast.37, f32[40,128,128]{2,1,0:T(8,128)} %bitcast.46, f32[40,1,128]{2,1,0:T(1,128)} %shard_map.113.refs_3_.state_ref, f32[2,1,128]{2,1,0:T(1,128)} %copy-done.4, f32[40,1,128]{2,1,0:T(1,128)} %bitcast.58, ...), custom_call_target="tpu_custom_call" | custom-call | flops 9175040 | bytes 10485760 | tf_op jit(solution)/shard_map/pallas_call | solution.py:78
  32.8 1.9 %shard_map.118 = f32[2,1,128]{2,1,0:T(1,128)} custom-call(s32[12]{0:T(128)} %slice.57.cols_ref, bf16[2,6,128,128]{3,2,1,0:T(8,128)(2,1)} %slice_bitcast_fusion.c_ref, f32[2,128,128]{2,1,0:T(8,128)} %slice_bitcast_fusion.1.inv_ref, f32[40,1,128]{2,1,0:T(1,128)} %shard_map.115.refs_3_.state_ref, f32[2,1,128]{2,1,0:T(1,128)} %copy-done.5, f32[2,1,128]{2,1,0:T(1,128)} %bitcast.67), custom_call_target="tpu_custom_call" | custom-call | tf_op jit(solution)/shard_map/pallas_call | solution.py:109
  34.7 3.0 %collective-permute-start.2 = (f32[2,1,128]{2,1,0:T(1,128)}, f32[2,1,128]{2,1,0:T(1,128)S(1)}, u32[]{:S(2)}, u32[]{:S(2)}) collective-permute-start(f32[2,1,128]{2,1,0:T(1,128)} %shard_map.118), channel_id=1, source_target_pairs={{0,1},{1,0},{2,3},{3,2},{4,5},{5,4},{6,7},{7,6},{8,9},{9,8},{10,11... | collective-permute-start | bytes 3080 | tf_op jit(solution)/shard_map/ppermute | solution.py:22
  37.8 6.6 %shard_map.117.refs_3_.state_ref = f32[40,1,128]{2,1,0:T(1,128)} custom-call(s32[240]{0:T(256)} %reshape_squeeze.6.refs_0_, bf16[40,6,128,128]{3,2,1,0:T(8,128)(2,1)} %bitcast.38, f32[40,128,128]{2,1,0:T(8,128)} %bitcast.47, f32[40,1,128]{2,1,0:T(1,128)} %shard_map.115.refs_3_.state_ref, f32[2,1,128]{2,1,0:T(1,128)} %copy-done.5, f32[40,1,128]{2,1,0:T(1,128)} %bitcast.59, ...), custom_call_target="tpu_custom_call" | custom-call | flops 9175040 | bytes 10485760 | tf_op jit(solution)/shard_map/pallas_call | solution.py:78
  45.0 6.6 %shard_map.119.state_ref.refs_3_ = f32[40,1,128]{2,1,0:T(1,128)} custom-call(s32[240]{0:T(256)} %reshape_squeeze.6.refs_0_, bf16[40,6,128,128]{3,2,1,0:T(8,128)(2,1)} %bitcast.39, f32[40,128,128]{2,1,0:T(8,128)} %bitcast.48, f32[40,1,128]{2,1,0:T(1,128)} %shard_map.117.refs_3_.state_ref, f32[2,1,128]{2,1,0:T(1,128)} %copy-done.6, f32[40,1,128]{2,1,0:T(1,128)} %bitcast.60, ...), custom_call_target="tpu_custom_call" | custom-call | flops 9175040 | bytes 10485760 | tf_op jit(solution)/shard_map/pallas_call | solution.py:78
  52.3 1.9 %shard_map.120 = f32[2,1,128]{2,1,0:T(1,128)} custom-call(s32[12]{0:T(128)} %slice.57.cols_ref, bf16[2,6,128,128]{3,2,1,0:T(8,128)(2,1)} %slice_bitcast_fusion.c_ref, f32[2,128,128]{2,1,0:T(8,128)} %slice_bitcast_fusion.1.inv_ref, f32[40,1,128]{2,1,0:T(1,128)} %shard_map.117.refs_3_.state_ref, f32[2,1,128]{2,1,0:T(1,128)} %copy-done.6, f32[2,1,128]{2,1,0:T(1,128)} %bitcast.68), custom_call_target="tpu_custom_call" | custom-call | tf_op jit(solution)/shard_map/pallas_call | solution.py:109
  54.2 6.9 %collective-permute-start.4 = (f32[1,4,2,128]{3,2,1,0:T(2,128)S(1)}, f32[1,4,2,128]{3,2,1,0:T(2,128)S(1)}, u32[]{:S(2)}, u32[]{:S(2)}) collective-permute-start(f32[1,4,2,128]{3,2,1,0:T(2,128)S(1)} %bitcast.62), channel_id=1, source_target_pairs={{0,16},{2,18},{4,20},{6,22},{8,24},{10,26},{12,28},{14,30},{16,0},... | collective-permute-start | bytes 12296 | tf_op jit(solution)/shard_map/ppermute | solution.py:139
  61.1 1.0 collective-permute-done.4
  62.1 2.9 %collective-permute-start.5 = (f32[2,4,2,128]{3,2,1,0:T(2,128)S(1)}, f32[2,4,2,128]{3,2,1,0:T(2,128)S(1)}, u32[]{:S(2)}, u32[]{:S(2)}) collective-permute-start(f32[2,4,2,128]{3,2,1,0:T(2,128)S(1)} %pad_maximum_fusion.9), channel_id=1, source_target_pairs={{0,64},{2,66},{4,68},{6,70},{8,72},{10,74},{12,76},{14,78},{16,80}... | collective-permute-start | bytes 24584 | tf_op jit(solution)/shard_map/ppermute | solution.py:139
  65.0 1.1 collective-permute-done.5
  66.1 1.5 collective-permute-start.6
  67.9 3.9 %collective-permute-done.3.ghost_ref.refs_4_ = f32[2,1,128]{2,1,0:T(1,128)S(1)} collective-permute-done((f32[2,1,128]{2,1,0:T(1,128)}, f32[2,1,128]{2,1,0:T(1,128)S(1)}, u32[]{:S(2)}, u32[]{:S(2)}) %collective-permute-start.3) | collective-permute-done | bytes 1056 | tf_op jit(solution)/shard_map/ppermute | solution.py:22
  72.4 1.9 %shard_map.121 = f32[2,1,128]{2,1,0:T(1,128)} custom-call(s32[12]{0:T(128)} %slice.57.cols_ref, bf16[2,6,128,128]{3,2,1,0:T(8,128)(2,1)} %slice_bitcast_fusion.c_ref, f32[2,128,128]{2,1,0:T(8,128)} %slice_bitcast_fusion.1.inv_ref, f32[40,1,128]{2,1,0:T(1,128)} %shard_map.119.state_ref.refs_3_, f32[2,1,128]{2,1,0:T(1,128)} %copy-done.2, f32[2,1,128]{2,1,0:T(1,128)} %bitcast.69), custom_call_target="tpu_custom_call" | custom-call | tf_op jit(solution)/shard_map/pallas_call | solution.py:109
  74.7 2.5 %collective-permute-done.7 = f32[8,4,2,128]{3,2,1,0:T(2,128)S(1)} collective-permute-done((f32[8,4,2,128]{3,2,1,0:T(2,128)S(1)}, f32[8,4,2,128]{3,2,1,0:T(2,128)S(1)}, u32[]{:S(2)}, u32[]{:S(2)}) %collective-permute-start.7) | collective-permute-done | bytes 32800 | tf_op jit(solution)/shard_map/ppermute | solution.py:139
  77.2 1.4 collective-permute-start.8
  78.6 1.8 %collective-permute-done.8 = f32[16,4,2,128]{3,2,1,0:T(2,128)S(1)} collective-permute-done((f32[16,4,2,128]{3,2,1,0:T(2,128)S(1)}, f32[16,4,2,128]{3,2,1,0:T(2,128)S(1)}, u32[]{:S(2)}, u32[]{:S(2)}) %collective-permute-start.8) | collective-permute-done | bytes 65568 | tf_op jit(solution)/shard_map/ppermute | solution.py:139
  80.5 1.7 %collective-permute-start.9 = (f32[32,4,2,128]{3,2,1,0:T(2,128)S(1)}, f32[32,4,2,128]{3,2,1,0:T(2,128)S(1)}, u32[]{:S(2)}, u32[]{:S(2)}) collective-permute-start(f32[32,4,2,128]{3,2,1,0:T(2,128)S(1)} %pad_maximum_fusion.1), channel_id=1, source_target_pairs={{0,4},{2,6},{4,0},{6,2},{8,12},{10,14},{12,8},{14,10},{16,20},{18,... | collective-permute-start | bytes 393224 | tf_op jit(solution)/shard_map/ppermute | solution.py:139
  83.1 1.5 collective-permute-done.9
  84.7 8.8 %collective-permute-start.10 = (f32[64,4,2,128]{3,2,1,0:T(2,128)S(1)}, f32[64,4,2,128]{3,2,1,0:T(2,128)S(1)}, u32[]{:S(2)}, u32[]{:S(2)}) collective-permute-start(f32[64,4,2,128]{3,2,1,0:T(2,128)S(1)} %pad_maximum_fusion), channel_id=1, source_target_pairs={{0,2},{2,0},{4,6},{6,4},{8,10},{10,8},{12,14},{14,12},{16,18},{18,... | collective-permute-start | bytes 786440 | tf_op jit(solution)/shard_map/ppermute | solution.py:139
  93.5 1.1 collective-permute-done.10
  95.9 6.6 %shard_map.122.refs_3_.state_ref = f32[40,1,128]{2,1,0:T(1,128)} custom-call(s32[240]{0:T(256)} %reshape_squeeze.6.refs_0_, bf16[40,6,128,128]{3,2,1,0:T(8,128)(2,1)} %bitcast.40, f32[40,128,128]{2,1,0:T(8,128)} %bitcast.49, f32[40,1,128]{2,1,0:T(1,128)} %shard_map.119.state_ref.refs_3_, f32[2,1,128]{2,1,0:T(1,128)} %copy-done.2, f32[40,1,128]{2,1,0:T(1,128)} %bitcast.53, ...), custom_call_target="tpu_custom_call" | custom-call | flops 9175040 | bytes 10485760 | tf_op jit(solution)/shard_map/pallas_call | solution.py:78
  103.0 1.9 %shard_map.124 = f32[2,1,128]{2,1,0:T(1,128)} custom-call(s32[12]{0:T(128)} %slice.57.cols_ref, bf16[2,6,128,128]{3,2,1,0:T(8,128)(2,1)} %slice_bitcast_fusion.c_ref, f32[2,128,128]{2,1,0:T(8,128)} %slice_bitcast_fusion.1.inv_ref, f32[40,1,128]{2,1,0:T(1,128)} %shard_map.122.refs_3_.state_ref, f32[2,1,128]{2,1,0:T(1,128)} %copy-done.3, f32[2,1,128]{2,1,0:T(1,128)} %bitcast.70), custom_call_target="tpu_custom_call" | custom-call | tf_op jit(solution)/shard_map/pallas_call | solution.py:109
  105.4 6.6 %shard_map.123.refs_3_.state_ref = f32[40,1,128]{2,1,0:T(1,128)} custom-call(s32[240]{0:T(256)} %reshape_squeeze.6.refs_0_, bf16[40,6,128,128]{3,2,1,0:T(8,128)(2,1)} %bitcast.41, f32[40,128,128]{2,1,0:T(8,128)} %bitcast.50, f32[40,1,128]{2,1,0:T(1,128)} %shard_map.122.refs_3_.state_ref, f32[2,1,128]{2,1,0:T(1,128)} %copy-done.3, f32[40,1,128]{2,1,0:T(1,128)} %bitcast.54, ...), custom_call_target="tpu_custom_call" | custom-call | flops 9175040 | bytes 10485760 | tf_op jit(solution)/shard_map/pallas_call | solution.py:78
  112.6 1.9 %shard_map.126 = f32[2,1,128]{2,1,0:T(1,128)} custom-call(s32[12]{0:T(128)} %slice.57.cols_ref, bf16[2,6,128,128]{3,2,1,0:T(8,128)(2,1)} %slice_bitcast_fusion.c_ref, f32[2,128,128]{2,1,0:T(8,128)} %slice_bitcast_fusion.1.inv_ref, f32[40,1,128]{2,1,0:T(1,128)} %shard_map.123.refs_3_.state_ref, f32[2,1,128]{2,1,0:T(1,128)} %copy-done.7, f32[2,1,128]{2,1,0:T(1,128)} %bitcast.71), custom_call_target="tpu_custom_call" | custom-call | tf_op jit(solution)/shard_map/pallas_call | solution.py:109
  114.5 2.5 %collective-permute-start.13 = (f32[2,1,128]{2,1,0:T(1,128)}, f32[2,1,128]{2,1,0:T(1,128)S(1)}, u32[]{:S(2)}, u32[]{:S(2)}) collective-permute-start(f32[2,1,128]{2,1,0:T(1,128)} %shard_map.126), channel_id=1, source_target_pairs={{0,1},{1,0},{2,3},{3,2},{4,5},{5,4},{6,7},{7,6},{8,9},{9,8},{10,11... | collective-permute-start | bytes 3080 | tf_op jit(solution)/shard_map/ppermute | solution.py:22
  117.0 6.6 %shard_map.125.refs_3_ = f32[40,1,128]{2,1,0:T(1,128)} custom-call(s32[240]{0:T(256)} %reshape_squeeze.6.refs_0_, bf16[40,6,128,128]{3,2,1,0:T(8,128)(2,1)} %bitcast.42, f32[40,128,128]{2,1,0:T(8,128)} %bitcast.51, f32[40,1,128]{2,1,0:T(1,128)} %shard_map.123.refs_3_.state_ref, f32[2,1,128]{2,1,0:T(1,128)} %copy-done.7, f32[40,1,128]{2,1,0:T(1,128)} %bitcast.55, ...), custom_call_target="tpu_custom_call" | custom-call | flops 9175040 | bytes 10485760 | tf_op jit(solution)/shard_map/pallas_call | solution.py:78
  124.2 6.6 %shard_map.127 = f32[40,1,128]{2,1,0:T(1,128)} custom-call(s32[240]{0:T(256)} %reshape_squeeze.6.refs_0_, bf16[40,6,128,128]{3,2,1,0:T(8,128)(2,1)} %bitcast.43, f32[40,128,128]{2,1,0:T(8,128)} %bitcast.52, f32[40,1,128]{2,1,0:T(1,128)} %shard_map.125.refs_3_, f32[2,1,128]{2,1,0:T(1,128)} %copy-done.9, f32[40,1,128]{2,1,0:T(1,128)} %bitcast.56, ...), custom_call_target="tpu_custom_call" | custom-call | flops 9175040 | bytes 10485760 | tf_op jit(solution)/shard_map/pallas_call | solution.py:78
  131.5 5.1 %collective-permute-start.14 = (f32[1,4,2,128]{3,2,1,0:T(2,128)S(1)}, f32[1,4,2,128]{3,2,1,0:T(2,128)S(1)}, u32[]{:S(2)}, u32[]{:S(2)}) collective-permute-start(f32[1,4,2,128]{3,2,1,0:T(2,128)S(1)} %get-tuple-element.9), channel_id=1, source_target_pairs={{0,16},{2,18},{4,20},{6,22},{8,24},{10,26},{12,28},{14,30},{16,0},... | collective-permute-start | bytes 12296 | tf_op jit(solution)/shard_map/ppermute | solution.py:139
  136.6 1.3 collective-permute-done.14
  137.9 2.9 %collective-permute-start.15 = (f32[2,4,2,128]{3,2,1,0:T(2,128)S(1)}, f32[2,4,2,128]{3,2,1,0:T(2,128)S(1)}, u32[]{:S(2)}, u32[]{:S(2)}) collective-permute-start(f32[2,4,2,128]{3,2,1,0:T(2,128)S(1)} %pad_maximum_fusion.10), channel_id=1, source_target_pairs={{0,64},{2,66},{4,68},{6,70},{8,72},{10,74},{12,76},{14,78},{16,80}... | collective-permute-start | bytes 24584 | tf_op jit(solution)/shard_map/ppermute | solution.py:139
  140.8 1.1 collective-permute-done.15
  141.9 1.0 collective-permute-start.16
  142.9 2.6 %collective-permute-done.16 = f32[4,4,2,128]{3,2,1,0:T(2,128)S(1)} collective-permute-done((f32[4,4,2,128]{3,2,1,0:T(2,128)S(1)}, f32[4,4,2,128]{3,2,1,0:T(2,128)S(1)}, u32[]{:S(2)}, u32[]{:S(2)}) %collective-permute-start.16) | collective-permute-done | bytes 16416 | tf_op jit(solution)/shard_map/ppermute | solution.py:139
  145.9 2.4 %collective-permute-done.17 = f32[8,4,2,128]{3,2,1,0:T(2,128)S(1)} collective-permute-done((f32[8,4,2,128]{3,2,1,0:T(2,128)S(1)}, f32[8,4,2,128]{3,2,1,0:T(2,128)S(1)}, u32[]{:S(2)}, u32[]{:S(2)}) %collective-permute-start.17) | collective-permute-done | bytes 32800 | tf_op jit(solution)/shard_map/ppermute | solution.py:139
  148.4 1.4 collective-permute-start.18
  149.8 1.8 %collective-permute-done.18 = f32[16,4,2,128]{3,2,1,0:T(2,128)S(1)} collective-permute-done((f32[16,4,2,128]{3,2,1,0:T(2,128)S(1)}, f32[16,4,2,128]{3,2,1,0:T(2,128)S(1)}, u32[]{:S(2)}, u32[]{:S(2)}) %collective-permute-start.18) | collective-permute-done | bytes 65568 | tf_op jit(solution)/shard_map/ppermute | solution.py:139
  151.7 1.7 %collective-permute-start.19 = (f32[32,4,2,128]{3,2,1,0:T(2,128)S(1)}, f32[32,4,2,128]{3,2,1,0:T(2,128)S(1)}, u32[]{:S(2)}, u32[]{:S(2)}) collective-permute-start(f32[32,4,2,128]{3,2,1,0:T(2,128)S(1)} %get-tuple-element.14), channel_id=1, source_target_pairs={{0,4},{2,6},{4,0},{6,2},{8,12},{10,14},{12,8},{14,10},{16,20},{18,... | collective-permute-start | bytes 393224 | tf_op jit(solution)/shard_map/ppermute | solution.py:139
  153.4 2.4 %collective-permute-done.19 = f32[32,4,2,128]{3,2,1,0:T(2,128)S(1)} collective-permute-done((f32[32,4,2,128]{3,2,1,0:T(2,128)S(1)}, f32[32,4,2,128]{3,2,1,0:T(2,128)S(1)}, u32[]{:S(2)}, u32[]{:S(2)}) %collective-permute-start.19) | collective-permute-done | bytes 131104 | tf_op jit(solution)/shard_map/ppermute | solution.py:139
  155.8 7.8 %collective-permute-start.20 = (f32[64,4,2,128]{3,2,1,0:T(2,128)S(1)}, f32[64,4,2,128]{3,2,1,0:T(2,128)S(1)}, u32[]{:S(2)}, u32[]{:S(2)}) collective-permute-start(f32[64,4,2,128]{3,2,1,0:T(2,128)S(1)} %get-tuple-element.10), channel_id=1, source_target_pairs={{0,2},{2,0},{4,6},{6,4},{8,10},{10,8},{12,14},{14,12},{16,18},{18,... | collective-permute-start | bytes 786440 | tf_op jit(solution)/shard_map/ppermute | solution.py:139
  163.6 1.2 collective-permute-done.20
  164.8 1.2 gather_fusion.2
  (83 shorter events, 19.6 us)
Async XLA Ops:
  0.6 0.7 copy-start
  5.8 16.0 %collective-permute-start = (f32[2,1,128]{2,1,0:T(1,128)}, f32[2,1,128]{2,1,0:T(1,128)S(1)}, u32[]{:S(2)}, u32[]{:S(2)}) collective-permute-start(f32[2,1,128]{2,1,0:T(1,128)} %shard_map.114), channel_id=1, source_target_pairs={{0,1},{1,0},{2,3},{3,2},{4,5},{5,4},{6,7},{7,6},{8,9},{9,8},{10,11... | collective-permute-start | bytes 3080 | tf_op jit(solution)/shard_map/ppermute | solution.py:22
  21.8 0.6 copy-start.4
  24.3 8.0 %collective-permute-start.1 = (f32[2,1,128]{2,1,0:T(1,128)}, f32[2,1,128]{2,1,0:T(1,128)S(1)}, u32[]{:S(2)}, u32[]{:S(2)}) collective-permute-start(f32[2,1,128]{2,1,0:T(1,128)} %shard_map.116), channel_id=1, source_target_pairs={{0,1},{1,0},{2,3},{3,2},{4,5},{5,4},{6,7},{7,6},{8,9},{9,8},{10,11... | collective-permute-start | bytes 3080 | tf_op jit(solution)/shard_map/ppermute | solution.py:22
  32.2 0.6 copy-start.5
  34.7 9.6 %collective-permute-start.2 = (f32[2,1,128]{2,1,0:T(1,128)}, f32[2,1,128]{2,1,0:T(1,128)S(1)}, u32[]{:S(2)}, u32[]{:S(2)}) collective-permute-start(f32[2,1,128]{2,1,0:T(1,128)} %shard_map.118), channel_id=1, source_target_pairs={{0,1},{1,0},{2,3},{3,2},{4,5},{5,4},{6,7},{7,6},{8,9},{9,8},{10,11... | collective-permute-start | bytes 3080 | tf_op jit(solution)/shard_map/ppermute | solution.py:22
  44.4 7.8 %copy-start.1 = (f32[1,1,4,2,128]{4,3,2,1,0:T(2,128)S(1)}, f32[1,1,4,2,128]{4,3,2,1,0:T(2,128)}, u32[]{:S(2)}) copy-start(f32[1,1,4,2,128]{4,3,2,1,0:T(2,128)} %param.19) | copy-start | bytes 12292
  44.4 37.8 %copy-start.8 = (s32[4,128]{1,0:T(4,128)S(1)}, s32[4,128]{1,0:T(4,128)}, u32[]{:S(2)}) copy-start(s32[4,128]{1,0:T(4,128)} %param.18) | copy-start | bytes 6148
  44.4 0.6 copy-start.6
  54.2 7.9 %collective-permute-start.4 = (f32[1,4,2,128]{3,2,1,0:T(2,128)S(1)}, f32[1,4,2,128]{3,2,1,0:T(2,128)S(1)}, u32[]{:S(2)}, u32[]{:S(2)}) collective-permute-start(f32[1,4,2,128]{3,2,1,0:T(2,128)S(1)} %bitcast.62), channel_id=1, source_target_pairs={{0,16},{2,18},{4,20},{6,22},{8,24},{10,26},{12,28},{14,30},{16,0},... | collective-permute-start | bytes 12296 | tf_op jit(solution)/shard_map/ppermute | solution.py:139
  62.1 4.0 %collective-permute-start.5 = (f32[2,4,2,128]{3,2,1,0:T(2,128)S(1)}, f32[2,4,2,128]{3,2,1,0:T(2,128)S(1)}, u32[]{:S(2)}, u32[]{:S(2)}) collective-permute-start(f32[2,4,2,128]{3,2,1,0:T(2,128)S(1)} %pad_maximum_fusion.9), channel_id=1, source_target_pairs={{0,64},{2,66},{4,68},{6,70},{8,72},{10,74},{12,76},{14,78},{16,80}... | collective-permute-start | bytes 24584 | tf_op jit(solution)/shard_map/ppermute | solution.py:139
  66.1 8.2 %collective-permute-start.6 = (f32[4,4,2,128]{3,2,1,0:T(2,128)S(1)}, f32[4,4,2,128]{3,2,1,0:T(2,128)S(1)}, u32[]{:S(2)}, u32[]{:S(2)}) collective-permute-start(f32[4,4,2,128]{3,2,1,0:T(2,128)S(1)} %pad_maximum_fusion.7), channel_id=1, source_target_pairs={{0,8},{2,10},{4,12},{6,14},{8,0},{10,2},{12,4},{14,6},{16,24},{18,... | collective-permute-start | bytes 49160 | tf_op jit(solution)/shard_map/ppermute | solution.py:139
  67.7 4.1 %collective-permute-start.3 = (f32[2,1,128]{2,1,0:T(1,128)}, f32[2,1,128]{2,1,0:T(1,128)S(1)}, u32[]{:S(2)}, u32[]{:S(2)}) collective-permute-start(f32[2,1,128]{2,1,0:T(1,128)} %shard_map.120), channel_id=1, source_target_pairs={{0,1},{1,0},{2,3},{3,2},{4,5},{5,4},{6,7},{7,6},{8,9},{9,8},{10,11... | collective-permute-start | bytes 3080 | tf_op jit(solution)/shard_map/ppermute | solution.py:22
  71.8 0.6 copy-start.2
  74.3 2.9 %collective-permute-start.7 = (f32[8,4,2,128]{3,2,1,0:T(2,128)S(1)}, f32[8,4,2,128]{3,2,1,0:T(2,128)S(1)}, u32[]{:S(2)}, u32[]{:S(2)}) collective-permute-start(f32[8,4,2,128]{3,2,1,0:T(2,128)S(1)} %pad_maximum_fusion.3), channel_id=1, source_target_pairs={{0,128},{2,130},{4,132},{6,134},{8,136},{10,138},{12,140},{14,142}... | collective-permute-start | bytes 98312 | tf_op jit(solution)/shard_map/ppermute | solution.py:139
  77.2 3.2 %collective-permute-start.8 = (f32[16,4,2,128]{3,2,1,0:T(2,128)S(1)}, f32[16,4,2,128]{3,2,1,0:T(2,128)S(1)}, u32[]{:S(2)}, u32[]{:S(2)}) collective-permute-start(f32[16,4,2,128]{3,2,1,0:T(2,128)S(1)} %pad_maximum_fusion.2), channel_id=1, source_target_pairs={{0,32},{2,34},{4,36},{6,38},{8,40},{10,42},{12,44},{14,46},{16,48}... | collective-permute-start | bytes 196616 | tf_op jit(solution)/shard_map/ppermute | solution.py:139
  80.5 4.1 %collective-permute-start.9 = (f32[32,4,2,128]{3,2,1,0:T(2,128)S(1)}, f32[32,4,2,128]{3,2,1,0:T(2,128)S(1)}, u32[]{:S(2)}, u32[]{:S(2)}) collective-permute-start(f32[32,4,2,128]{3,2,1,0:T(2,128)S(1)} %pad_maximum_fusion.1), channel_id=1, source_target_pairs={{0,4},{2,6},{4,0},{6,2},{8,12},{10,14},{12,8},{14,10},{16,20},{18,... | collective-permute-start | bytes 393224 | tf_op jit(solution)/shard_map/ppermute | solution.py:139
  82.4 20.0 %collective-permute-start.11 = (f32[2,1,128]{2,1,0:T(1,128)}, f32[2,1,128]{2,1,0:T(1,128)S(1)}, u32[]{:S(2)}, u32[]{:S(2)}) collective-permute-start(f32[2,1,128]{2,1,0:T(1,128)} %shard_map.121), channel_id=1, source_target_pairs={{0,1},{1,0},{2,3},{3,2},{4,5},{5,4},{6,7},{7,6},{8,9},{9,8},{10,11... | collective-permute-start | bytes 3080 | tf_op jit(solution)/shard_map/ppermute | solution.py:22
  84.7 9.9 %collective-permute-start.10 = (f32[64,4,2,128]{3,2,1,0:T(2,128)S(1)}, f32[64,4,2,128]{3,2,1,0:T(2,128)S(1)}, u32[]{:S(2)}, u32[]{:S(2)}) collective-permute-start(f32[64,4,2,128]{3,2,1,0:T(2,128)S(1)} %pad_maximum_fusion), channel_id=1, source_target_pairs={{0,2},{2,0},{4,6},{6,4},{8,10},{10,8},{12,14},{14,12},{16,18},{18,... | collective-permute-start | bytes 786440 | tf_op jit(solution)/shard_map/ppermute | solution.py:139
  102.4 0.6 copy-start.3
  104.9 7.1 %collective-permute-start.12 = (f32[2,1,128]{2,1,0:T(1,128)}, f32[2,1,128]{2,1,0:T(1,128)S(1)}, u32[]{:S(2)}, u32[]{:S(2)}) collective-permute-start(f32[2,1,128]{2,1,0:T(1,128)} %shard_map.124), channel_id=1, source_target_pairs={{0,1},{1,0},{2,3},{3,2},{4,5},{5,4},{6,7},{7,6},{8,9},{9,8},{10,11... | collective-permute-start | bytes 3080 | tf_op jit(solution)/shard_map/ppermute | solution.py:22
  112.0 0.6 copy-start.7
  114.5 9.1 %collective-permute-start.13 = (f32[2,1,128]{2,1,0:T(1,128)}, f32[2,1,128]{2,1,0:T(1,128)S(1)}, u32[]{:S(2)}, u32[]{:S(2)}) collective-permute-start(f32[2,1,128]{2,1,0:T(1,128)} %shard_map.126), channel_id=1, source_target_pairs={{0,1},{1,0},{2,3},{3,2},{4,5},{5,4},{6,7},{7,6},{8,9},{9,8},{10,11... | collective-permute-start | bytes 3080 | tf_op jit(solution)/shard_map/ppermute | solution.py:22
  123.6 0.6 copy-start.9
  131.5 6.4 %collective-permute-start.14 = (f32[1,4,2,128]{3,2,1,0:T(2,128)S(1)}, f32[1,4,2,128]{3,2,1,0:T(2,128)S(1)}, u32[]{:S(2)}, u32[]{:S(2)}) collective-permute-start(f32[1,4,2,128]{3,2,1,0:T(2,128)S(1)} %get-tuple-element.9), channel_id=1, source_target_pairs={{0,16},{2,18},{4,20},{6,22},{8,24},{10,26},{12,28},{14,30},{16,0},... | collective-permute-start | bytes 12296 | tf_op jit(solution)/shard_map/ppermute | solution.py:139
  137.9 4.0 %collective-permute-start.15 = (f32[2,4,2,128]{3,2,1,0:T(2,128)S(1)}, f32[2,4,2,128]{3,2,1,0:T(2,128)S(1)}, u32[]{:S(2)}, u32[]{:S(2)}) collective-permute-start(f32[2,4,2,128]{3,2,1,0:T(2,128)S(1)} %pad_maximum_fusion.10), channel_id=1, source_target_pairs={{0,64},{2,66},{4,68},{6,70},{8,72},{10,74},{12,76},{14,78},{16,80}... | collective-permute-start | bytes 24584 | tf_op jit(solution)/shard_map/ppermute | solution.py:139
  141.9 3.6 %collective-permute-start.16 = (f32[4,4,2,128]{3,2,1,0:T(2,128)S(1)}, f32[4,4,2,128]{3,2,1,0:T(2,128)S(1)}, u32[]{:S(2)}, u32[]{:S(2)}) collective-permute-start(f32[4,4,2,128]{3,2,1,0:T(2,128)S(1)} %pad_maximum_fusion.8), channel_id=1, source_target_pairs={{0,8},{2,10},{4,12},{6,14},{8,0},{10,2},{12,4},{14,6},{16,24},{18,... | collective-permute-start | bytes 49160 | tf_op jit(solution)/shard_map/ppermute | solution.py:139
  145.5 2.9 %collective-permute-start.17 = (f32[8,4,2,128]{3,2,1,0:T(2,128)S(1)}, f32[8,4,2,128]{3,2,1,0:T(2,128)S(1)}, u32[]{:S(2)}, u32[]{:S(2)}) collective-permute-start(f32[8,4,2,128]{3,2,1,0:T(2,128)S(1)} %pad_maximum_fusion.4), channel_id=1, source_target_pairs={{0,128},{2,130},{4,132},{6,134},{8,136},{10,138},{12,140},{14,142}... | collective-permute-start | bytes 98312 | tf_op jit(solution)/shard_map/ppermute | solution.py:139
  148.4 3.2 %collective-permute-start.18 = (f32[16,4,2,128]{3,2,1,0:T(2,128)S(1)}, f32[16,4,2,128]{3,2,1,0:T(2,128)S(1)}, u32[]{:S(2)}, u32[]{:S(2)}) collective-permute-start(f32[16,4,2,128]{3,2,1,0:T(2,128)S(1)} %get-tuple-element.18), channel_id=1, source_target_pairs={{0,32},{2,34},{4,36},{6,38},{8,40},{10,42},{12,44},{14,46},{16,48}... | collective-permute-start | bytes 196616 | tf_op jit(solution)/shard_map/ppermute | solution.py:139
  151.7 4.1 %collective-permute-start.19 = (f32[32,4,2,128]{3,2,1,0:T(2,128)S(1)}, f32[32,4,2,128]{3,2,1,0:T(2,128)S(1)}, u32[]{:S(2)}, u32[]{:S(2)}) collective-permute-start(f32[32,4,2,128]{3,2,1,0:T(2,128)S(1)} %get-tuple-element.14), channel_id=1, source_target_pairs={{0,4},{2,6},{4,0},{6,2},{8,12},{10,14},{12,8},{14,10},{16,20},{18,... | collective-permute-start | bytes 393224 | tf_op jit(solution)/shard_map/ppermute | solution.py:139
  155.8 8.9 %collective-permute-start.20 = (f32[64,4,2,128]{3,2,1,0:T(2,128)S(1)}, f32[64,4,2,128]{3,2,1,0:T(2,128)S(1)}, u32[]{:S(2)}, u32[]{:S(2)}) collective-permute-start(f32[64,4,2,128]{3,2,1,0:T(2,128)S(1)} %get-tuple-element.10), channel_id=1, source_target_pairs={{0,2},{2,0},{4,6},{6,4},{8,10},{10,8},{12,14},{14,12},{16,18},{18,... | collective-permute-start | bytes 786440 | tf_op jit(solution)/shard_map/ppermute | solution.py:139

commit v5 on v3

--- a/solution.py
+++ b/solution.py
@@ -24,7 +24,7 @@
 
 def sweep_kernel(*refs, coupled_terms, first, blocks):
     if coupled_terms:
-        cols_ref, c_ref, inv_ref, state_ref, ghost_ref, f_ref, p_ref, o_ref = refs
+        cols_ref, p_ref, c_ref, inv_ref, state_ref, ghost_ref, f_ref, o_ref = refs
     else:
         inv_ref, f_ref, o_ref = refs
     rows = inv_ref.shape[0]
@@ -36,14 +36,14 @@
             row = base + r
             acc = None
             for b in range(bands):
-                col = cols_ref[row * bands + b]
+                col = cols_ref[row, b]
                 own = state_ref[jnp.minimum(col, blocks - 1)]
                 other = ghost_ref[jnp.maximum(col - blocks, 0)]
                 xb = jnp.where(col >= blocks, other, own)
                 term = c_ref[r, b].astype(jnp.float32) * xb
                 acc = term if acc is None else acc + term
             y = y - jnp.sum(acc.T, axis=0, keepdims=True)
-            y = y - p_ref[r] * state_ref[row]
+            y = y - p_ref[row] * state_ref[row]
         o_ref[r] = jnp.sum((inv_ref[r] * y).T, axis=0, keepdims=True)
 
 
@@ -56,18 +56,17 @@
         prefetch = 0
         bands = 0
     else:
-        cols, tile, state, ghost, prows = coupling
+        cols, prows, tile, state, ghost = coupling
         bands = tile.shape[1]
-        operands = [cols, tile, inv, state, ghost, forcing, prows]
+        operands = [cols, prows, tile, inv, state, ghost, forcing]
         specs = [
             pl.BlockSpec((rows, bands, width, width), lambda g, *_: (g + first, 0, 0, 0)),
             pl.BlockSpec((rows, width, width), at),
             pl.BlockSpec(state.shape, lambda g, *_: (0, 0, 0)),
             pl.BlockSpec(ghost.shape, lambda g, *_: (0, 0, 0)),
             pl.BlockSpec((rows, 1, width), at),
-            pl.BlockSpec((rows, 1, width), at),
         ]
-        prefetch = 1
+        prefetch = 2
     done = count * rows
     grid_spec = pltpu.PrefetchScalarGridSpec(
         num_scalar_prefetch=prefetch,
@@ -148,13 +147,12 @@
     partners = lax.dynamic_index_in_dim(matching, lax.axis_index("sub"), axis=1, keepdims=False)
     robin_data = lambda_in[0, 0]
 
-    flat_columns = columns.reshape(-1)
-    prows = jnp.concatenate([p_face, jnp.zeros((blocks - iface,), jnp.float32)])[:, None, None] * jnp.ones((1, 1, width), jnp.float32)
+    prows = jnp.where(jnp.arange(blocks) < iface, p_block, 0.0)
 
     def sweep_rows(state, ghost, forcing, rows, first, count):
         if state is None:
             return block_sweep(inverse, forcing, rows, first, count)
-        coupling = (flat_columns, couple[0, 0], state, ghost, prows)
+        coupling = (columns, prows, couple[0, 0], state, ghost)
         return block_sweep(inverse, forcing, rows, first, count, coupling)
 
     head_forcing = rhs[:, None]

time: 165 us -> 169 us (1.024)
  Pallas kernels: 65.9 us -> 69.9 us
    pallas_call x15, Pallas kernels: 65.9 us -> 69.9 us  [block_sweep(): pl.pallas_call(functools.partial(sweep_kernel, coupled_terms=coupling is...]
  transfers between devices with their start and end apart: 21 -> 21, of which waited for: 14 -> 14; matrix products, arithmetic and copies ran while one was open for 4% -> 4% of each run, Pallas kernels for 23% -> 24%
where the time goes in v5:
time: 169 us; the launch traced here: 168 us
  Pallas kernels  69.9 us (41%)
  starting transfers between devices  54.4 us (32%)
  waiting for transfers between devices  25.5 us (15%)
  local copies, waits for them, and re-layouts  9.68 us (6%)
  other arithmetic  7.4 us (4%)
    pallas_call x15, Pallas kernels, block_sweep(): pl.pallas_call(functools.partial(sweep_kernel, coupled_terms=coupling is...  69.9 us
    ppermute x14, starting transfers between devices, exchange(): held = jnp.concatenate([held, lax.ppermute(held, 'sub', route)], axis=0)  44 us
    ppermute x14, waiting for transfers between devices, exchange(): held = jnp.concatenate([held, lax.ppermute(held, 'sub', route)], axis=0)  21.6 us
    ppermute x7, starting transfers between devices, partner(): return lax.ppermute(block, axis, route)  10.4 us
    unnamed x31, local copies, waits for them, and re-layouts  5.56 us
    ppermute x7, waiting for transfers between devices, partner(): return lax.ppermute(block, axis, route)  3.93 us
  transfers between devices with their start and end apart: 21, of which 14 were waited for; matrix products, arithmetic and copies ran while one was open for 4% of the time, Pallas kernels for 24%

profile of v5, /device:TPU:1, one launch (start us, length us, event | category | flops | bytes accessed | tf_op | source)
XLA Modules:
  0.0 167.6 jit_solution(9309322871854614280)
XLA Ops:
  2.8 1.4 multiply_add_fusion.refs_1_.refs_6_
  4.2 1.6 shard_map.114
  5.8 3.6 %collective-permute-start = (f32[2,1,128]{2,1,0:T(1,128)}, f32[2,1,128]{2,1,0:T(1,128)S(1)}, u32[]{:S(2)}, u32[]{:S(2)}) collective-permute-start(f32[2,1,128]{2,1,0:T(1,128)} %shard_map.114), channel_id=1, source_target_pairs={{0,1},{1,0},{2,3},{3,2},{4,5},{5,4},{6,7},{7,6},{8,9},{9,8},{10,11... | collective-permute-start | bytes 3080 | tf_op jit(solution)/shard_map/ppermute | solution.py:22
  9.4 0.8 bitcast_add_fusion
  12.8 1.4 copy.22
  14.2 2.8 %shard_map.113.refs_4_ = f32[40,1,128]{2,1,0:T(1,128)} custom-call(f32[40,128,128]{2,1,0:T(8,128)} %bitcast.43, f32[40,1,128]{2,1,0:T(1,128)} %bitcast.74), custom_call_target="tpu_custom_call" | custom-call | flops 1310720 | bytes 2621440 | tf_op jit(solution)/shard_map/pallas_call | solution.py:77
  17.5 2.9 %shard_map.116 = f32[2,1,128]{2,1,0:T(1,128)} custom-call(s32[40,6]{1,0:T(8,128)} %bitcast.57, f32[40]{0:T(128)} %compare_select_fusion.3.refs_1_, bf16[40,6,128,128]{3,2,1,0:T(8,128)(2,1)} %bitcast.29, f32[40,128,128]{2,1,0:T(8,128)} %bitcast.44, f32[40,1,128]{2,1,0:T(1,128)} %shard_map.113.refs_4_, f32[2,1,128]{2,1,0:T(1,128)} %copy-done.4, ...), custom_call_target="tpu_custom_call" | custom-call | flops 458752 | bytes 524288 | tf_op jit(solution)/shard_map/pallas_call | solution.py:77
  20.4 6.9 %shard_map.115.refs_4_ = f32[40,1,128]{2,1,0:T(1,128)} custom-call(s32[40,6]{1,0:T(8,128)} %bitcast.58, f32[40]{0:T(128)} %compare_select_fusion.3.refs_1_, bf16[40,6,128,128]{3,2,1,0:T(8,128)(2,1)} %bitcast.30, f32[40,128,128]{2,1,0:T(8,128)} %bitcast.45, f32[40,1,128]{2,1,0:T(1,128)} %shard_map.113.refs_4_, f32[2,1,128]{2,1,0:T(1,128)} %copy-done.4, ...), custom_call_target="tpu_custom_call" | custom-call | flops 9175040 | bytes 10485760 | tf_op jit(solution)/shard_map/pallas_call | solution.py:77
  27.8 2.9 %shard_map.118 = f32[2,1,128]{2,1,0:T(1,128)} custom-call(s32[40,6]{1,0:T(8,128)} %bitcast.59, f32[40]{0:T(128)} %compare_select_fusion.3.refs_1_, bf16[40,6,128,128]{3,2,1,0:T(8,128)(2,1)} %bitcast.31, f32[40,128,128]{2,1,0:T(8,128)} %bitcast.46, f32[40,1,128]{2,1,0:T(1,128)} %shard_map.115.refs_4_, f32[2,1,128]{2,1,0:T(1,128)} %copy-done.5, ...), custom_call_target="tpu_custom_call" | custom-call | flops 458752 | bytes 524288 | tf_op jit(solution)/shard_map/pallas_call | solution.py:77
  30.7 3.0 %collective-permute-start.2 = (f32[2,1,128]{2,1,0:T(1,128)}, f32[2,1,128]{2,1,0:T(1,128)S(1)}, u32[]{:S(2)}, u32[]{:S(2)}) collective-permute-start(f32[2,1,128]{2,1,0:T(1,128)} %shard_map.118), channel_id=1, source_target_pairs={{0,1},{1,0},{2,3},{3,2},{4,5},{5,4},{6,7},{7,6},{8,9},{9,8},{10,11... | collective-permute-start | bytes 3080 | tf_op jit(solution)/shard_map/ppermute | solution.py:22
  33.8 6.9 %shard_map.117.refs_4_ = f32[40,1,128]{2,1,0:T(1,128)} custom-call(s32[40,6]{1,0:T(8,128)} %bitcast.60, f32[40]{0:T(128)} %compare_select_fusion.3.refs_1_, bf16[40,6,128,128]{3,2,1,0:T(8,128)(2,1)} %bitcast.32, f32[40,128,128]{2,1,0:T(8,128)} %bitcast.47, f32[40,1,128]{2,1,0:T(1,128)} %shard_map.115.refs_4_, f32[2,1,128]{2,1,0:T(1,128)} %copy-done.5, ...), custom_call_target="tpu_custom_call" | custom-call | flops 9175040 | bytes 10485760 | tf_op jit(solution)/shard_map/pallas_call | solution.py:77
  41.2 6.9 %shard_map.119.refs_4_ = f32[40,1,128]{2,1,0:T(1,128)} custom-call(s32[40,6]{1,0:T(8,128)} %bitcast.61, f32[40]{0:T(128)} %compare_select_fusion.3.refs_1_, bf16[40,6,128,128]{3,2,1,0:T(8,128)(2,1)} %bitcast.33, f32[40,128,128]{2,1,0:T(8,128)} %bitcast.48, f32[40,1,128]{2,1,0:T(1,128)} %shard_map.117.refs_4_, f32[2,1,128]{2,1,0:T(1,128)} %copy-done.6, ...), custom_call_target="tpu_custom_call" | custom-call | flops 9175040 | bytes 10485760 | tf_op jit(solution)/shard_map/pallas_call | solution.py:77
  48.8 2.9 %shard_map.120 = f32[2,1,128]{2,1,0:T(1,128)} custom-call(s32[40,6]{1,0:T(8,128)} %bitcast.62, f32[40]{0:T(128)} %compare_select_fusion.3.refs_1_, bf16[40,6,128,128]{3,2,1,0:T(8,128)(2,1)} %bitcast.34, f32[40,128,128]{2,1,0:T(8,128)} %bitcast.49, f32[40,1,128]{2,1,0:T(1,128)} %shard_map.117.refs_4_, f32[2,1,128]{2,1,0:T(1,128)} %copy-done.6, ...), custom_call_target="tpu_custom_call" | custom-call | flops 458752 | bytes 524288 | tf_op jit(solution)/shard_map/pallas_call | solution.py:77
  51.8 6.9 %collective-permute-start.4 = (f32[1,4,2,128]{3,2,1,0:T(2,128)S(1)}, f32[1,4,2,128]{3,2,1,0:T(2,128)S(1)}, u32[]{:S(2)}, u32[]{:S(2)}) collective-permute-start(f32[1,4,2,128]{3,2,1,0:T(2,128)S(1)} %bitcast.79), channel_id=1, source_target_pairs={{0,16},{2,18},{4,20},{6,22},{8,24},{10,26},{12,28},{14,30},{16,0},... | collective-permute-start | bytes 12296 | tf_op jit(solution)/shard_map/ppermute | solution.py:111
  58.7 1.0 collective-permute-done.4
  59.7 2.9 %collective-permute-start.5 = (f32[2,4,2,128]{3,2,1,0:T(2,128)S(1)}, f32[2,4,2,128]{3,2,1,0:T(2,128)S(1)}, u32[]{:S(2)}, u32[]{:S(2)}) collective-permute-start(f32[2,4,2,128]{3,2,1,0:T(2,128)S(1)} %pad_maximum_fusion.9), channel_id=1, source_target_pairs={{0,64},{2,66},{4,68},{6,70},{8,72},{10,74},{12,76},{14,78},{16,80}... | collective-permute-start | bytes 24584 | tf_op jit(solution)/shard_map/ppermute | solution.py:111
  62.6 1.1 collective-permute-done.5
  63.7 1.5 collective-permute-start.6
  65.5 3.9 %collective-permute-done.3.refs_5_ = f32[2,1,128]{2,1,0:T(1,128)S(1)} collective-permute-done((f32[2,1,128]{2,1,0:T(1,128)}, f32[2,1,128]{2,1,0:T(1,128)S(1)}, u32[]{:S(2)}, u32[]{:S(2)}) %collective-permute-start.3) | collective-permute-done | bytes 1056 | tf_op jit(solution)/shard_map/ppermute | solution.py:22
  69.9 2.9 %shard_map.121 = f32[2,1,128]{2,1,0:T(1,128)} custom-call(s32[40,6]{1,0:T(8,128)} %bitcast.63, f32[40]{0:T(128)} %compare_select_fusion.3.refs_1_, bf16[40,6,128,128]{3,2,1,0:T(8,128)(2,1)} %bitcast.35, f32[40,128,128]{2,1,0:T(8,128)} %bitcast.50, f32[40,1,128]{2,1,0:T(1,128)} %shard_map.119.refs_4_, f32[2,1,128]{2,1,0:T(1,128)} %copy-done.2, ...), custom_call_target="tpu_custom_call" | custom-call | flops 458752 | bytes 524288 | tf_op jit(solution)/shard_map/pallas_call | solution.py:77
  73.3 2.5 %collective-permute-done.7 = f32[8,4,2,128]{3,2,1,0:T(2,128)S(1)} collective-permute-done((f32[8,4,2,128]{3,2,1,0:T(2,128)S(1)}, f32[8,4,2,128]{3,2,1,0:T(2,128)S(1)}, u32[]{:S(2)}, u32[]{:S(2)}) %collective-permute-start.7) | collective-permute-done | bytes 32800 | tf_op jit(solution)/shard_map/ppermute | solution.py:111
  75.7 1.4 collective-permute-start.8
  77.1 1.8 %collective-permute-done.8 = f32[16,4,2,128]{3,2,1,0:T(2,128)S(1)} collective-permute-done((f32[16,4,2,128]{3,2,1,0:T(2,128)S(1)}, f32[16,4,2,128]{3,2,1,0:T(2,128)S(1)}, u32[]{:S(2)}, u32[]{:S(2)}) %collective-permute-start.8) | collective-permute-done | bytes 65568 | tf_op jit(solution)/shard_map/ppermute | solution.py:111
  79.0 1.7 %collective-permute-start.9 = (f32[32,4,2,128]{3,2,1,0:T(2,128)S(1)}, f32[32,4,2,128]{3,2,1,0:T(2,128)S(1)}, u32[]{:S(2)}, u32[]{:S(2)}) collective-permute-start(f32[32,4,2,128]{3,2,1,0:T(2,128)S(1)} %pad_maximum_fusion.1), channel_id=1, source_target_pairs={{0,4},{2,6},{4,0},{6,2},{8,12},{10,14},{12,8},{14,10},{16,20},{18,... | collective-permute-start | bytes 393224 | tf_op jit(solution)/shard_map/ppermute | solution.py:111
  81.6 1.5 collective-permute-done.9
  83.2 8.8 %collective-permute-start.10 = (f32[64,4,2,128]{3,2,1,0:T(2,128)S(1)}, f32[64,4,2,128]{3,2,1,0:T(2,128)S(1)}, u32[]{:S(2)}, u32[]{:S(2)}) collective-permute-start(f32[64,4,2,128]{3,2,1,0:T(2,128)S(1)} %pad_maximum_fusion), channel_id=1, source_target_pairs={{0,2},{2,0},{4,6},{6,4},{8,10},{10,8},{12,14},{14,12},{16,18},{18,... | collective-permute-start | bytes 786440 | tf_op jit(solution)/shard_map/ppermute | solution.py:111
  92.0 1.1 collective-permute-done.10
  94.4 6.9 %shard_map.122.refs_4_ = f32[40,1,128]{2,1,0:T(1,128)} custom-call(s32[40,6]{1,0:T(8,128)} %bitcast.64, f32[40]{0:T(128)} %compare_select_fusion.3.refs_1_, bf16[40,6,128,128]{3,2,1,0:T(8,128)(2,1)} %bitcast.36, f32[40,128,128]{2,1,0:T(8,128)} %bitcast.51, f32[40,1,128]{2,1,0:T(1,128)} %shard_map.119.refs_4_, f32[2,1,128]{2,1,0:T(1,128)} %copy-done.2, ...), custom_call_target="tpu_custom_call" | custom-call | flops 9175040 | bytes 10485760 | tf_op jit(solution)/shard_map/pallas_call | solution.py:77
  101.8 2.9 %shard_map.124 = f32[2,1,128]{2,1,0:T(1,128)} custom-call(s32[40,6]{1,0:T(8,128)} %bitcast.65, f32[40]{0:T(128)} %compare_select_fusion.3.refs_1_, bf16[40,6,128,128]{3,2,1,0:T(8,128)(2,1)} %bitcast.37, f32[40,128,128]{2,1,0:T(8,128)} %bitcast.52, f32[40,1,128]{2,1,0:T(1,128)} %shard_map.122.refs_4_, f32[2,1,128]{2,1,0:T(1,128)} %copy-done.3, ...), custom_call_target="tpu_custom_call" | custom-call | flops 458752 | bytes 524288 | tf_op jit(solution)/shard_map/pallas_call | solution.py:77
  105.2 6.9 %shard_map.123.refs_4_ = f32[40,1,128]{2,1,0:T(1,128)} custom-call(s32[40,6]{1,0:T(8,128)} %bitcast.66, f32[40]{0:T(128)} %compare_select_fusion.3.refs_1_, bf16[40,6,128,128]{3,2,1,0:T(8,128)(2,1)} %bitcast.38, f32[40,128,128]{2,1,0:T(8,128)} %bitcast.53, f32[40,1,128]{2,1,0:T(1,128)} %shard_map.122.refs_4_, f32[2,1,128]{2,1,0:T(1,128)} %copy-done.3, ...), custom_call_target="tpu_custom_call" | custom-call | flops 9175040 | bytes 10485760 | tf_op jit(solution)/shard_map/pallas_call | solution.py:77
  112.6 2.9 %shard_map.126 = f32[2,1,128]{2,1,0:T(1,128)} custom-call(s32[40,6]{1,0:T(8,128)} %bitcast.67, f32[40]{0:T(128)} %compare_select_fusion.3.refs_1_, bf16[40,6,128,128]{3,2,1,0:T(8,128)(2,1)} %bitcast.39, f32[40,128,128]{2,1,0:T(8,128)} %bitcast.54, f32[40,1,128]{2,1,0:T(1,128)} %shard_map.123.refs_4_, f32[2,1,128]{2,1,0:T(1,128)} %copy-done.7, ...), custom_call_target="tpu_custom_call" | custom-call | flops 458752 | bytes 524288 | tf_op jit(solution)/shard_map/pallas_call | solution.py:77
  115.6 2.5 %collective-permute-start.13 = (f32[2,1,128]{2,1,0:T(1,128)}, f32[2,1,128]{2,1,0:T(1,128)S(1)}, u32[]{:S(2)}, u32[]{:S(2)}) collective-permute-start(f32[2,1,128]{2,1,0:T(1,128)} %shard_map.126), channel_id=1, source_target_pairs={{0,1},{1,0},{2,3},{3,2},{4,5},{5,4},{6,7},{7,6},{8,9},{9,8},{10,11... | collective-permute-start | bytes 3080 | tf_op jit(solution)/shard_map/ppermute | solution.py:22
  118.0 6.9 %shard_map.125.refs_4_ = f32[40,1,128]{2,1,0:T(1,128)} custom-call(s32[40,6]{1,0:T(8,128)} %bitcast.68, f32[40]{0:T(128)} %compare_select_fusion.3.refs_1_, bf16[40,6,128,128]{3,2,1,0:T(8,128)(2,1)} %bitcast.40, f32[40,128,128]{2,1,0:T(8,128)} %bitcast.55, f32[40,1,128]{2,1,0:T(1,128)} %shard_map.123.refs_4_, f32[2,1,128]{2,1,0:T(1,128)} %copy-done.7, ...), custom_call_target="tpu_custom_call" | custom-call | flops 9175040 | bytes 10485760 | tf_op jit(solution)/shard_map/pallas_call | solution.py:77
  125.5 6.9 %shard_map.127 = f32[40,1,128]{2,1,0:T(1,128)} custom-call(s32[40,6]{1,0:T(8,128)} %bitcast.69, f32[40]{0:T(128)} %compare_select_fusion.3.refs_1_, bf16[40,6,128,128]{3,2,1,0:T(8,128)(2,1)} %bitcast.41, f32[40,128,128]{2,1,0:T(8,128)} %bitcast.56, f32[40,1,128]{2,1,0:T(1,128)} %shard_map.125.refs_4_, f32[2,1,128]{2,1,0:T(1,128)} %copy-done.9, ...), custom_call_target="tpu_custom_call" | custom-call | flops 9175040 | bytes 10485760 | tf_op jit(solution)/shard_map/pallas_call | solution.py:77
  133.1 5.2 %collective-permute-start.14 = (f32[1,4,2,128]{3,2,1,0:T(2,128)S(1)}, f32[1,4,2,128]{3,2,1,0:T(2,128)S(1)}, u32[]{:S(2)}, u32[]{:S(2)}) collective-permute-start(f32[1,4,2,128]{3,2,1,0:T(2,128)S(1)} %get-tuple-element.9), channel_id=1, source_target_pairs={{0,16},{2,18},{4,20},{6,22},{8,24},{10,26},{12,28},{14,30},{16,0},... | collective-permute-start | bytes 12296 | tf_op jit(solution)/shard_map/ppermute | solution.py:111
  138.3 1.2 collective-permute-done.14
  139.5 2.9 %collective-permute-start.15 = (f32[2,4,2,128]{3,2,1,0:T(2,128)S(1)}, f32[2,4,2,128]{3,2,1,0:T(2,128)S(1)}, u32[]{:S(2)}, u32[]{:S(2)}) collective-permute-start(f32[2,4,2,128]{3,2,1,0:T(2,128)S(1)} %pad_maximum_fusion.10), channel_id=1, source_target_pairs={{0,64},{2,66},{4,68},{6,70},{8,72},{10,74},{12,76},{14,78},{16,80}... | collective-permute-start | bytes 24584 | tf_op jit(solution)/shard_map/ppermute | solution.py:111
  142.4 1.1 collective-permute-done.15
  143.5 1.0 collective-permute-start.16
  144.5 2.6 %collective-permute-done.16 = f32[4,4,2,128]{3,2,1,0:T(2,128)S(1)} collective-permute-done((f32[4,4,2,128]{3,2,1,0:T(2,128)S(1)}, f32[4,4,2,128]{3,2,1,0:T(2,128)S(1)}, u32[]{:S(2)}, u32[]{:S(2)}) %collective-permute-start.16) | collective-permute-done | bytes 16416 | tf_op jit(solution)/shard_map/ppermute | solution.py:111
  147.5 2.4 %collective-permute-done.17 = f32[8,4,2,128]{3,2,1,0:T(2,128)S(1)} collective-permute-done((f32[8,4,2,128]{3,2,1,0:T(2,128)S(1)}, f32[8,4,2,128]{3,2,1,0:T(2,128)S(1)}, u32[]{:S(2)}, u32[]{:S(2)}) %collective-permute-start.17) | collective-permute-done | bytes 32800 | tf_op jit(solution)/shard_map/ppermute | solution.py:111
  150.0 1.4 collective-permute-start.18
  151.4 1.8 %collective-permute-done.18 = f32[16,4,2,128]{3,2,1,0:T(2,128)S(1)} collective-permute-done((f32[16,4,2,128]{3,2,1,0:T(2,128)S(1)}, f32[16,4,2,128]{3,2,1,0:T(2,128)S(1)}, u32[]{:S(2)}, u32[]{:S(2)}) %collective-permute-start.18) | collective-permute-done | bytes 65568 | tf_op jit(solution)/shard_map/ppermute | solution.py:111
  153.3 1.7 %collective-permute-start.19 = (f32[32,4,2,128]{3,2,1,0:T(2,128)S(1)}, f32[32,4,2,128]{3,2,1,0:T(2,128)S(1)}, u32[]{:S(2)}, u32[]{:S(2)}) collective-permute-start(f32[32,4,2,128]{3,2,1,0:T(2,128)S(1)} %get-tuple-element.14), channel_id=1, source_target_pairs={{0,4},{2,6},{4,0},{6,2},{8,12},{10,14},{12,8},{14,10},{16,20},{18,... | collective-permute-start | bytes 393224 | tf_op jit(solution)/shard_map/ppermute | solution.py:111
  155.0 2.4 %collective-permute-done.19 = f32[32,4,2,128]{3,2,1,0:T(2,128)S(1)} collective-permute-done((f32[32,4,2,128]{3,2,1,0:T(2,128)S(1)}, f32[32,4,2,128]{3,2,1,0:T(2,128)S(1)}, u32[]{:S(2)}, u32[]{:S(2)}) %collective-permute-start.19) | collective-permute-done | bytes 131104 | tf_op jit(solution)/shard_map/ppermute | solution.py:111
  157.5 7.7 %collective-permute-start.20 = (f32[64,4,2,128]{3,2,1,0:T(2,128)S(1)}, f32[64,4,2,128]{3,2,1,0:T(2,128)S(1)}, u32[]{:S(2)}, u32[]{:S(2)}) collective-permute-start(f32[64,4,2,128]{3,2,1,0:T(2,128)S(1)} %get-tuple-element.10), channel_id=1, source_target_pairs={{0,2},{2,0},{4,6},{6,4},{8,10},{10,8},{12,14},{14,12},{16,18},{18,... | collective-permute-start | bytes 786440 | tf_op jit(solution)/shard_map/ppermute | solution.py:111
  165.2 1.2 collective-permute-done.20
  166.4 1.2 gather_fusion.2
  (75 shorter events, 14.5 us)
Async XLA Ops:
  0.6 0.7 copy-start
  5.8 11.1 %collective-permute-start = (f32[2,1,128]{2,1,0:T(1,128)}, f32[2,1,128]{2,1,0:T(1,128)S(1)}, u32[]{:S(2)}, u32[]{:S(2)}) collective-permute-start(f32[2,1,128]{2,1,0:T(1,128)} %shard_map.114), channel_id=1, source_target_pairs={{0,1},{1,0},{2,3},{3,2},{4,5},{5,4},{6,7},{7,6},{8,9},{9,8},{10,11... | collective-permute-start | bytes 3080 | tf_op jit(solution)/shard_map/ppermute | solution.py:22
  16.9 0.6 copy-start.4
  20.4 6.9 %collective-permute-start.1 = (f32[2,1,128]{2,1,0:T(1,128)}, f32[2,1,128]{2,1,0:T(1,128)S(1)}, u32[]{:S(2)}, u32[]{:S(2)}) collective-permute-start(f32[2,1,128]{2,1,0:T(1,128)} %shard_map.116), channel_id=1, source_target_pairs={{0,1},{1,0},{2,3},{3,2},{4,5},{5,4},{6,7},{7,6},{8,9},{9,8},{10,11... | collective-permute-start | bytes 3080 | tf_op jit(solution)/shard_map/ppermute | solution.py:22
  27.3 0.6 copy-start.5
  30.7 9.9 %collective-permute-start.2 = (f32[2,1,128]{2,1,0:T(1,128)}, f32[2,1,128]{2,1,0:T(1,128)S(1)}, u32[]{:S(2)}, u32[]{:S(2)}) collective-permute-start(f32[2,1,128]{2,1,0:T(1,128)} %shard_map.118), channel_id=1, source_target_pairs={{0,1},{1,0},{2,3},{3,2},{4,5},{5,4},{6,7},{7,6},{8,9},{9,8},{10,11... | collective-permute-start | bytes 3080 | tf_op jit(solution)/shard_map/ppermute | solution.py:22
  40.7 8.1 %copy-start.1 = (f32[1,1,4,2,128]{4,3,2,1,0:T(2,128)S(1)}, f32[1,1,4,2,128]{4,3,2,1,0:T(2,128)}, u32[]{:S(2)}) copy-start(f32[1,1,4,2,128]{4,3,2,1,0:T(2,128)} %param.19) | copy-start | bytes 12292
  40.7 0.6 copy-start.6
  51.8 29.0 %copy-start.8 = (s32[4,128]{1,0:T(4,128)S(1)}, s32[4,128]{1,0:T(4,128)}, u32[]{:S(2)}) copy-start(s32[4,128]{1,0:T(4,128)} %param.18) | copy-start | bytes 6148
  51.8 7.9 %collective-permute-start.4 = (f32[1,4,2,128]{3,2,1,0:T(2,128)S(1)}, f32[1,4,2,128]{3,2,1,0:T(2,128)S(1)}, u32[]{:S(2)}, u32[]{:S(2)}) collective-permute-start(f32[1,4,2,128]{3,2,1,0:T(2,128)S(1)} %bitcast.79), channel_id=1, source_target_pairs={{0,16},{2,18},{4,20},{6,22},{8,24},{10,26},{12,28},{14,30},{16,0},... | collective-permute-start | bytes 12296 | tf_op jit(solution)/shard_map/ppermute | solution.py:111
  59.7 4.0 %collective-permute-start.5 = (f32[2,4,2,128]{3,2,1,0:T(2,128)S(1)}, f32[2,4,2,128]{3,2,1,0:T(2,128)S(1)}, u32[]{:S(2)}, u32[]{:S(2)}) collective-permute-start(f32[2,4,2,128]{3,2,1,0:T(2,128)S(1)} %pad_maximum_fusion.9), channel_id=1, source_target_pairs={{0,64},{2,66},{4,68},{6,70},{8,72},{10,74},{12,76},{14,78},{16,80}... | collective-permute-start | bytes 24584 | tf_op jit(solution)/shard_map/ppermute | solution.py:111
  63.7 9.1 %collective-permute-start.6 = (f32[4,4,2,128]{3,2,1,0:T(2,128)S(1)}, f32[4,4,2,128]{3,2,1,0:T(2,128)S(1)}, u32[]{:S(2)}, u32[]{:S(2)}) collective-permute-start(f32[4,4,2,128]{3,2,1,0:T(2,128)S(1)} %pad_maximum_fusion.7), channel_id=1, source_target_pairs={{0,8},{2,10},{4,12},{6,14},{8,0},{10,2},{12,4},{14,6},{16,24},{18,... | collective-permute-start | bytes 49160 | tf_op jit(solution)/shard_map/ppermute | solution.py:111
  65.2 4.1 %collective-permute-start.3 = (f32[2,1,128]{2,1,0:T(1,128)}, f32[2,1,128]{2,1,0:T(1,128)S(1)}, u32[]{:S(2)}, u32[]{:S(2)}) collective-permute-start(f32[2,1,128]{2,1,0:T(1,128)} %shard_map.120), channel_id=1, source_target_pairs={{0,1},{1,0},{2,3},{3,2},{4,5},{5,4},{6,7},{7,6},{8,9},{9,8},{10,11... | collective-permute-start | bytes 3080 | tf_op jit(solution)/shard_map/ppermute | solution.py:22
  69.4 0.6 copy-start.2
  72.9 2.9 %collective-permute-start.7 = (f32[8,4,2,128]{3,2,1,0:T(2,128)S(1)}, f32[8,4,2,128]{3,2,1,0:T(2,128)S(1)}, u32[]{:S(2)}, u32[]{:S(2)}) collective-permute-start(f32[8,4,2,128]{3,2,1,0:T(2,128)S(1)} %pad_maximum_fusion.3), channel_id=1, source_target_pairs={{0,128},{2,130},{4,132},{6,134},{8,136},{10,138},{12,140},{14,142}... | collective-permute-start | bytes 98312 | tf_op jit(solution)/shard_map/ppermute | solution.py:111
  75.7 3.2 %collective-permute-start.8 = (f32[16,4,2,128]{3,2,1,0:T(2,128)S(1)}, f32[16,4,2,128]{3,2,1,0:T(2,128)S(1)}, u32[]{:S(2)}, u32[]{:S(2)}) collective-permute-start(f32[16,4,2,128]{3,2,1,0:T(2,128)S(1)} %pad_maximum_fusion.2), channel_id=1, source_target_pairs={{0,32},{2,34},{4,36},{6,38},{8,40},{10,42},{12,44},{14,46},{16,48}... | collective-permute-start | bytes 196616 | tf_op jit(solution)/shard_map/ppermute | solution.py:111
  79.0 4.1 %collective-permute-start.9 = (f32[32,4,2,128]{3,2,1,0:T(2,128)S(1)}, f32[32,4,2,128]{3,2,1,0:T(2,128)S(1)}, u32[]{:S(2)}, u32[]{:S(2)}) collective-permute-start(f32[32,4,2,128]{3,2,1,0:T(2,128)S(1)} %pad_maximum_fusion.1), channel_id=1, source_target_pairs={{0,4},{2,6},{4,0},{6,2},{8,12},{10,14},{12,8},{14,10},{16,20},{18,... | collective-permute-start | bytes 393224 | tf_op jit(solution)/shard_map/ppermute | solution.py:111
  80.9 20.3 %collective-permute-start.11 = (f32[2,1,128]{2,1,0:T(1,128)}, f32[2,1,128]{2,1,0:T(1,128)S(1)}, u32[]{:S(2)}, u32[]{:S(2)}) collective-permute-start(f32[2,1,128]{2,1,0:T(1,128)} %shard_map.121), channel_id=1, source_target_pairs={{0,1},{1,0},{2,3},{3,2},{4,5},{5,4},{6,7},{7,6},{8,9},{9,8},{10,11... | collective-permute-start | bytes 3080 | tf_op jit(solution)/shard_map/ppermute | solution.py:22
  83.2 9.9 %collective-permute-start.10 = (f32[64,4,2,128]{3,2,1,0:T(2,128)S(1)}, f32[64,4,2,128]{3,2,1,0:T(2,128)S(1)}, u32[]{:S(2)}, u32[]{:S(2)}) collective-permute-start(f32[64,4,2,128]{3,2,1,0:T(2,128)S(1)} %pad_maximum_fusion), channel_id=1, source_target_pairs={{0,2},{2,0},{4,6},{6,4},{8,10},{10,8},{12,14},{14,12},{16,18},{18,... | collective-permute-start | bytes 786440 | tf_op jit(solution)/shard_map/ppermute | solution.py:111
  101.3 0.6 copy-start.3
  104.7 7.3 %collective-permute-start.12 = (f32[2,1,128]{2,1,0:T(1,128)}, f32[2,1,128]{2,1,0:T(1,128)S(1)}, u32[]{:S(2)}, u32[]{:S(2)}) collective-permute-start(f32[2,1,128]{2,1,0:T(1,128)} %shard_map.124), channel_id=1, source_target_pairs={{0,1},{1,0},{2,3},{3,2},{4,5},{5,4},{6,7},{7,6},{8,9},{9,8},{10,11... | collective-permute-start | bytes 3080 | tf_op jit(solution)/shard_map/ppermute | solution.py:22
  112.1 0.6 copy-start.7
  115.6 9.4 %collective-permute-start.13 = (f32[2,1,128]{2,1,0:T(1,128)}, f32[2,1,128]{2,1,0:T(1,128)S(1)}, u32[]{:S(2)}, u32[]{:S(2)}) collective-permute-start(f32[2,1,128]{2,1,0:T(1,128)} %shard_map.126), channel_id=1, source_target_pairs={{0,1},{1,0},{2,3},{3,2},{4,5},{5,4},{6,7},{7,6},{8,9},{9,8},{10,11... | collective-permute-start | bytes 3080 | tf_op jit(solution)/shard_map/ppermute | solution.py:22
  124.9 0.6 copy-start.9
  133.1 6.4 %collective-permute-start.14 = (f32[1,4,2,128]{3,2,1,0:T(2,128)S(1)}, f32[1,4,2,128]{3,2,1,0:T(2,128)S(1)}, u32[]{:S(2)}, u32[]{:S(2)}) collective-permute-start(f32[1,4,2,128]{3,2,1,0:T(2,128)S(1)} %get-tuple-element.9), channel_id=1, source_target_pairs={{0,16},{2,18},{4,20},{6,22},{8,24},{10,26},{12,28},{14,30},{16,0},... | collective-permute-start | bytes 12296 | tf_op jit(solution)/shard_map/ppermute | solution.py:111
  139.5 4.0 %collective-permute-start.15 = (f32[2,4,2,128]{3,2,1,0:T(2,128)S(1)}, f32[2,4,2,128]{3,2,1,0:T(2,128)S(1)}, u32[]{:S(2)}, u32[]{:S(2)}) collective-permute-start(f32[2,4,2,128]{3,2,1,0:T(2,128)S(1)} %pad_maximum_fusion.10), channel_id=1, source_target_pairs={{0,64},{2,66},{4,68},{6,70},{8,72},{10,74},{12,76},{14,78},{16,80}... | collective-permute-start | bytes 24584 | tf_op jit(solution)/shard_map/ppermute | solution.py:111
  143.5 3.6 %collective-permute-start.16 = (f32[4,4,2,128]{3,2,1,0:T(2,128)S(1)}, f32[4,4,2,128]{3,2,1,0:T(2,128)S(1)}, u32[]{:S(2)}, u32[]{:S(2)}) collective-permute-start(f32[4,4,2,128]{3,2,1,0:T(2,128)S(1)} %pad_maximum_fusion.8), channel_id=1, source_target_pairs={{0,8},{2,10},{4,12},{6,14},{8,0},{10,2},{12,4},{14,6},{16,24},{18,... | collective-permute-start | bytes 49160 | tf_op jit(solution)/shard_map/ppermute | solution.py:111
  147.1 2.9 %collective-permute-start.17 = (f32[8,4,2,128]{3,2,1,0:T(2,128)S(1)}, f32[8,4,2,128]{3,2,1,0:T(2,128)S(1)}, u32[]{:S(2)}, u32[]{:S(2)}) collective-permute-start(f32[8,4,2,128]{3,2,1,0:T(2,128)S(1)} %pad_maximum_fusion.4), channel_id=1, source_target_pairs={{0,128},{2,130},{4,132},{6,134},{8,136},{10,138},{12,140},{14,142}... | collective-permute-start | bytes 98312 | tf_op jit(solution)/shard_map/ppermute | solution.py:111
  150.0 3.2 %collective-permute-start.18 = (f32[16,4,2,128]{3,2,1,0:T(2,128)S(1)}, f32[16,4,2,128]{3,2,1,0:T(2,128)S(1)}, u32[]{:S(2)}, u32[]{:S(2)}) collective-permute-start(f32[16,4,2,128]{3,2,1,0:T(2,128)S(1)} %get-tuple-element.18), channel_id=1, source_target_pairs={{0,32},{2,34},{4,36},{6,38},{8,40},{10,42},{12,44},{14,46},{16,48}... | collective-permute-start | bytes 196616 | tf_op jit(solution)/shard_map/ppermute | solution.py:111
  153.3 4.1 %collective-permute-start.19 = (f32[32,4,2,128]{3,2,1,0:T(2,128)S(1)}, f32[32,4,2,128]{3,2,1,0:T(2,128)S(1)}, u32[]{:S(2)}, u32[]{:S(2)}) collective-permute-start(f32[32,4,2,128]{3,2,1,0:T(2,128)S(1)} %get-tuple-element.14), channel_id=1, source_target_pairs={{0,4},{2,6},{4,0},{6,2},{8,12},{10,14},{12,8},{14,10},{16,20},{18,... | collective-permute-start | bytes 393224 | tf_op jit(solution)/shard_map/ppermute | solution.py:111
  157.5 8.9 %collective-permute-start.20 = (f32[64,4,2,128]{3,2,1,0:T(2,128)S(1)}, f32[64,4,2,128]{3,2,1,0:T(2,128)S(1)}, u32[]{:S(2)}, u32[]{:S(2)}) collective-permute-start(f32[64,4,2,128]{3,2,1,0:T(2,128)S(1)} %get-tuple-element.10), channel_id=1, source_target_pairs={{0,2},{2,0},{4,6},{6,4},{8,10},{10,8},{12,14},{14,12},{16,18},{18,... | collective-permute-start | bytes 786440 | tf_op jit(solution)/shard_map/ppermute | solution.py:111

commit v6 on v3

--- a/solution.py
+++ b/solution.py
@@ -93,7 +93,7 @@
     return list(range(bits - 1, -1, -1))
 
 
-def exchange(outgoing, partners, tie=None, midway=None):
+def exchange(outgoing, partners, matching_rows, tie=None, midway=None):
     count = lax.axis_size("sub")
     bits = count.bit_length() - 1
     me = lax.axis_index("sub")
@@ -107,17 +107,28 @@
         return every[partners, jnp.arange(outgoing.shape[0])], extra
     order = doubling_order(bits)
     held = outgoing[None]
-    for step, bit in enumerate(order):
+    for step, bit in enumerate(order[:-1]):
         route = [(low, low ^ (1 << bit)) for low in range(count)]
         held = jnp.concatenate([held, lax.ppermute(held, "sub", route)], axis=0)
         if midway is not None and step == min(2, len(order) - 1):
             extra = midway()
             held, extra = lax.optimization_barrier((held, extra))
-    flipped = partners ^ me
-    entry = jnp.zeros_like(partners)
-    for step, bit in enumerate(order):
-        entry = entry | (((flipped >> bit) & 1) << step)
-    return held[entry, jnp.arange(outgoing.shape[0])], extra
+    last = order[-1]
+    colours = jnp.arange(outgoing.shape[0])
+
+    def located(targets):
+        flipped = targets ^ me
+        entry = jnp.zeros_like(targets)
+        for step, bit in enumerate(order[:-1]):
+            entry = entry | (((flipped >> bit) & 1) << step)
+        return held[entry, colours], ((flipped >> last) & 1) == 0
+
+    wanted = lax.dynamic_index_in_dim(matching_rows, me ^ (1 << last), axis=1, keepdims=False)
+    offer, have = located(wanted)
+    route = [(low, low ^ (1 << last)) for low in range(count)]
+    passed = lax.ppermute(jnp.where(have[:, None, None], offer, 0.0), "sub", route)
+    own, mine = located(partners)
+    return jnp.where(mine[:, None, None], own, passed), extra
 
 
 def per_device(
@@ -182,9 +193,9 @@
         )
         if outer < OUTER - 1 and blocks - G >= iface:
             ahead = lambda state=state, ghost=ghost: sweep_rows(state, ghost, head_forcing, G, (blocks - G) // G, 1)
-            robin_data, pending = exchange(outgoing, partners, tie=top, midway=ahead)
+            robin_data, pending = exchange(outgoing, partners, matching, tie=top, midway=ahead)
         else:
-            robin_data, _ = exchange(outgoing, partners)
+            robin_data, _ = exchange(outgoing, partners, matching)
     return (state[:, 0][None, None], robin_data[None, None])
 
 

time: 165 us -> 164 us (level)
  waiting for transfers between devices: 25.5 us -> 23 us
    ppermute x0 -> x2, starting transfers between devices: none -> 16.4 us  [exchange(): lax.ppermute(jnp.where(have[:, None, None], offer, 0.0), 'sub', route)]
    ppermute x14 -> x12, starting transfers between devices: 43.9 us -> 28.3 us  [exchange(): held = jnp.concatenate([held, lax.ppermute(held, 'sub', route)], axis=0)]
    ppermute x14 -> x12, waiting for transfers between devices: 21.6 us -> 18.8 us  [exchange(): held = jnp.concatenate([held, lax.ppermute(held, 'sub', route)], axis=0)]
    unnamed x31 -> x29, local copies, waits for them, and re-layouts: 4.3 us -> 4.38 us
  transfers between devices with their start and end apart: 21 -> 21, of which waited for: 14 -> 13; matrix products, arithmetic and copies ran while one was open for 4% -> 5% of each run, Pallas kernels for 23% -> 23%
where the time goes in v6:
time: 164 us; the launch traced here: 163 us
  Pallas kernels  65.8 us (40%)
  starting transfers between devices  54.7 us (33%)
  waiting for transfers between devices  23 us (14%)
  local copies, waits for them, and re-layouts  10.4 us (6%)
  other arithmetic  8.54 us (5%)
    pallas_call x15, Pallas kernels, block_sweep(): pl.pallas_call(functools.partial(sweep_kernel, coupled_terms=coupling is...  65.8 us
    ppermute x12, starting transfers between devices, exchange(): held = jnp.concatenate([held, lax.ppermute(held, 'sub', route)], axis=0)  28.3 us
    ppermute x12, waiting for transfers between devices, exchange(): held = jnp.concatenate([held, lax.ppermute(held, 'sub', route)], axis=0)  18.8 us
    ppermute x2, starting transfers between devices, exchange(): lax.ppermute(jnp.where(have[:, None, None], offer, 0.0), 'sub', route)  16.4 us
    ppermute x7, starting transfers between devices, partner(): return lax.ppermute(block, axis, route)  10 us
    unnamed x29, local copies, waits for them, and re-layouts  4.38 us
    ppermute x7, waiting for transfers between devices, partner(): return lax.ppermute(block, axis, route)  3.93 us
  transfers between devices with their start and end apart: 21, of which 13 were waited for; matrix products, arithmetic and copies ran while one was open for 5% of the time, Pallas kernels for 23%

profile of v6, /device:TPU:1, one launch (start us, length us, event | category | flops | bytes accessed | tf_op | source)
XLA Modules:
  0.0 163.3 jit_solution(16698576215107098866)
XLA Ops:
  1.4 0.8 gather_fusion
  2.8 1.4 multiply_add_fusion.refs_1_.refs_5_
  4.2 1.6 shard_map.114
  5.8 3.6 %collective-permute-start = (f32[2,1,128]{2,1,0:T(1,128)}, f32[2,1,128]{2,1,0:T(1,128)S(1)}, u32[]{:S(2)}, u32[]{:S(2)}) collective-permute-start(f32[2,1,128]{2,1,0:T(1,128)} %shard_map.114), channel_id=1, source_target_pairs={{0,1},{1,0},{2,3},{3,2},{4,5},{5,4},{6,7},{7,6},{8,9},{9,8},{10,11... | collective-permute-start | bytes 3080 | tf_op jit(solution)/shard_map/ppermute | solution.py:22
  9.4 0.8 bitcast_add_fusion
  10.9 0.8 select_reduce_fusion
  12.9 0.8 copy.21
  14.4 2.8 %shard_map.113.refs_3_ = f32[40,1,128]{2,1,0:T(1,128)} custom-call(f32[40,128,128]{2,1,0:T(8,128)} %bitcast.45, f32[40,1,128]{2,1,0:T(1,128)} %bitcast.63), custom_call_target="tpu_custom_call" | custom-call | flops 1310720 | bytes 2621440 | tf_op jit(solution)/shard_map/pallas_call | solution.py:78
  17.9 2.6 %shard_map.116 = f32[2,1,128]{2,1,0:T(1,128)} custom-call(s32[240]{0:T(256)} %reshape_squeeze.6.refs_0_, bf16[40,6,128,128]{3,2,1,0:T(8,128)(2,1)} %bitcast.31, f32[40,128,128]{2,1,0:T(8,128)} %bitcast.46, f32[40,1,128]{2,1,0:T(1,128)} %shard_map.113.refs_3_, f32[2,1,128]{2,1,0:T(1,128)} %copy-done.5, f32[40,1,128]{2,1,0:T(1,128)} %multiply_add_fusion.refs_1_.refs_5_, ...), custom_call_target="tpu_custom_call" | custom-call | flops 458752 | bytes 524288 | tf_op jit(solution)/shard_map/pallas_call | solution.py:78
  20.4 6.6 %shard_map.115.refs_3_ = f32[40,1,128]{2,1,0:T(1,128)} custom-call(s32[240]{0:T(256)} %reshape_squeeze.6.refs_0_, bf16[40,6,128,128]{3,2,1,0:T(8,128)(2,1)} %bitcast.32, f32[40,128,128]{2,1,0:T(8,128)} %bitcast.47, f32[40,1,128]{2,1,0:T(1,128)} %shard_map.113.refs_3_, f32[2,1,128]{2,1,0:T(1,128)} %copy-done.5, f32[40,1,128]{2,1,0:T(1,128)} %bitcast.64, ...), custom_call_target="tpu_custom_call" | custom-call | flops 9175040 | bytes 10485760 | tf_op jit(solution)/shard_map/pallas_call | solution.py:78
  27.6 2.6 %shard_map.118 = f32[2,1,128]{2,1,0:T(1,128)} custom-call(s32[240]{0:T(256)} %reshape_squeeze.6.refs_0_, bf16[40,6,128,128]{3,2,1,0:T(8,128)(2,1)} %bitcast.33, f32[40,128,128]{2,1,0:T(8,128)} %bitcast.48, f32[40,1,128]{2,1,0:T(1,128)} %shard_map.115.refs_3_, f32[2,1,128]{2,1,0:T(1,128)} %copy-done.6, f32[40,1,128]{2,1,0:T(1,128)} %multiply_add_fusion.refs_1_.refs_5_, ...), custom_call_target="tpu_custom_call" | custom-call | flops 458752 | bytes 524288 | tf_op jit(solution)/shard_map/pallas_call | solution.py:78
  30.2 3.0 %collective-permute-start.2 = (f32[2,1,128]{2,1,0:T(1,128)}, f32[2,1,128]{2,1,0:T(1,128)S(1)}, u32[]{:S(2)}, u32[]{:S(2)}) collective-permute-start(f32[2,1,128]{2,1,0:T(1,128)} %shard_map.118), channel_id=1, source_target_pairs={{0,1},{1,0},{2,3},{3,2},{4,5},{5,4},{6,7},{7,6},{8,9},{9,8},{10,11... | collective-permute-start | bytes 3080 | tf_op jit(solution)/shard_map/ppermute | solution.py:22
  33.2 6.6 %shard_map.117.refs_3_ = f32[40,1,128]{2,1,0:T(1,128)} custom-call(s32[240]{0:T(256)} %reshape_squeeze.6.refs_0_, bf16[40,6,128,128]{3,2,1,0:T(8,128)(2,1)} %bitcast.34, f32[40,128,128]{2,1,0:T(8,128)} %bitcast.49, f32[40,1,128]{2,1,0:T(1,128)} %shard_map.115.refs_3_, f32[2,1,128]{2,1,0:T(1,128)} %copy-done.6, f32[40,1,128]{2,1,0:T(1,128)} %bitcast.65, ...), custom_call_target="tpu_custom_call" | custom-call | flops 9175040 | bytes 10485760 | tf_op jit(solution)/shard_map/pallas_call | solution.py:78
  40.3 6.6 %shard_map.119.refs_3_ = f32[40,1,128]{2,1,0:T(1,128)} custom-call(s32[240]{0:T(256)} %reshape_squeeze.6.refs_0_, bf16[40,6,128,128]{3,2,1,0:T(8,128)(2,1)} %bitcast.35, f32[40,128,128]{2,1,0:T(8,128)} %bitcast.50, f32[40,1,128]{2,1,0:T(1,128)} %shard_map.117.refs_3_, f32[2,1,128]{2,1,0:T(1,128)} %copy-done.7, f32[40,1,128]{2,1,0:T(1,128)} %bitcast.66, ...), custom_call_target="tpu_custom_call" | custom-call | flops 9175040 | bytes 10485760 | tf_op jit(solution)/shard_map/pallas_call | solution.py:78
  47.7 2.6 %shard_map.120 = f32[2,1,128]{2,1,0:T(1,128)} custom-call(s32[240]{0:T(256)} %reshape_squeeze.6.refs_0_, bf16[40,6,128,128]{3,2,1,0:T(8,128)(2,1)} %bitcast.36, f32[40,128,128]{2,1,0:T(8,128)} %bitcast.51, f32[40,1,128]{2,1,0:T(1,128)} %shard_map.117.refs_3_, f32[2,1,128]{2,1,0:T(1,128)} %copy-done.7, f32[40,1,128]{2,1,0:T(1,128)} %multiply_add_fusion.refs_1_.refs_5_, ...), custom_call_target="tpu_custom_call" | custom-call | flops 458752 | bytes 524288 | tf_op jit(solution)/shard_map/pallas_call | solution.py:78
  50.3 6.9 %collective-permute-start.4 = (f32[1,4,2,128]{3,2,1,0:T(2,128)S(1)}, f32[1,4,2,128]{3,2,1,0:T(2,128)S(1)}, u32[]{:S(2)}, u32[]{:S(2)}) collective-permute-start(f32[1,4,2,128]{3,2,1,0:T(2,128)S(1)} %bitcast.68), channel_id=1, source_target_pairs={{0,16},{2,18},{4,20},{6,22},{8,24},{10,26},{12,28},{14,30},{16,0},... | collective-permute-start | bytes 12296 | tf_op jit(solution)/shard_map/ppermute | solution.py:112
  57.2 1.0 collective-permute-done.4
  58.2 2.9 %collective-permute-start.5 = (f32[2,4,2,128]{3,2,1,0:T(2,128)S(1)}, f32[2,4,2,128]{3,2,1,0:T(2,128)S(1)}, u32[]{:S(2)}, u32[]{:S(2)}) collective-permute-start(f32[2,4,2,128]{3,2,1,0:T(2,128)S(1)} %pad_maximum_fusion.8), channel_id=1, source_target_pairs={{0,64},{2,66},{4,68},{6,70},{8,72},{10,74},{12,76},{14,78},{16,80}... | collective-permute-start | bytes 24584 | tf_op jit(solution)/shard_map/ppermute | solution.py:112
  61.1 1.1 collective-permute-done.5
  62.2 1.5 collective-permute-start.6
  64.0 3.9 %collective-permute-done.3.refs_4_ = f32[2,1,128]{2,1,0:T(1,128)S(1)} collective-permute-done((f32[2,1,128]{2,1,0:T(1,128)}, f32[2,1,128]{2,1,0:T(1,128)S(1)}, u32[]{:S(2)}, u32[]{:S(2)}) %collective-permute-start.3) | collective-permute-done | bytes 1056 | tf_op jit(solution)/shard_map/ppermute | solution.py:22
  68.5 2.6 %shard_map.121 = f32[2,1,128]{2,1,0:T(1,128)} custom-call(s32[240]{0:T(256)} %reshape_squeeze.6.refs_0_, bf16[40,6,128,128]{3,2,1,0:T(8,128)(2,1)} %bitcast.37, f32[40,128,128]{2,1,0:T(8,128)} %bitcast.52, f32[40,1,128]{2,1,0:T(1,128)} %shard_map.119.refs_3_, f32[2,1,128]{2,1,0:T(1,128)} %copy-done.3, f32[40,1,128]{2,1,0:T(1,128)} %multiply_add_fusion.refs_1_.refs_5_, ...), custom_call_target="tpu_custom_call" | custom-call | flops 458752 | bytes 524288 | tf_op jit(solution)/shard_map/pallas_call | solution.py:78
  71.9 2.0 %collective-permute-done.7 = f32[8,4,2,128]{3,2,1,0:T(2,128)S(1)} collective-permute-done((f32[8,4,2,128]{3,2,1,0:T(2,128)S(1)}, f32[8,4,2,128]{3,2,1,0:T(2,128)S(1)}, u32[]{:S(2)}, u32[]{:S(2)}) %collective-permute-start.7) | collective-permute-done | bytes 32800 | tf_op jit(solution)/shard_map/ppermute | solution.py:112
  74.0 1.4 collective-permute-start.8
  75.3 1.8 %collective-permute-done.8 = f32[16,4,2,128]{3,2,1,0:T(2,128)S(1)} collective-permute-done((f32[16,4,2,128]{3,2,1,0:T(2,128)S(1)}, f32[16,4,2,128]{3,2,1,0:T(2,128)S(1)}, u32[]{:S(2)}, u32[]{:S(2)}) %collective-permute-start.8) | collective-permute-done | bytes 65568 | tf_op jit(solution)/shard_map/ppermute | solution.py:112
  77.2 1.7 %collective-permute-start.9 = (f32[32,4,2,128]{3,2,1,0:T(2,128)S(1)}, f32[32,4,2,128]{3,2,1,0:T(2,128)S(1)}, u32[]{:S(2)}, u32[]{:S(2)}) collective-permute-start(f32[32,4,2,128]{3,2,1,0:T(2,128)S(1)} %pad_maximum_fusion), channel_id=1, source_target_pairs={{0,4},{2,6},{4,0},{6,2},{8,12},{10,14},{12,8},{14,10},{16,20},{18,... | collective-permute-start | bytes 393224 | tf_op jit(solution)/shard_map/ppermute | solution.py:112
  79.0 2.3 %collective-permute-done.9 = f32[32,4,2,128]{3,2,1,0:T(2,128)S(1)} collective-permute-done((f32[32,4,2,128]{3,2,1,0:T(2,128)S(1)}, f32[32,4,2,128]{3,2,1,0:T(2,128)S(1)}, u32[]{:S(2)}, u32[]{:S(2)}) %collective-permute-start.9) | collective-permute-done | bytes 131104 | tf_op jit(solution)/shard_map/ppermute | solution.py:112
  82.0 8.5 %collective-permute-start.10 = (f32[4,2,128]{2,1,0:T(2,128)S(1)}, f32[4,2,128]{2,1,0:T(2,128)S(1)}, u32[]{:S(2)}, u32[]{:S(2)}) collective-permute-start(f32[4,2,128]{2,1,0:T(2,128)S(1)} %broadcast_select_fusion.1), channel_id=1, source_target_pairs={{0,2},{2,0},{4,6},{6,4},{8,10},{10,8},{12,14},{14,12},{16,18},{18,... | collective-permute-start | bytes 12296 | tf_op jit(solution)/shard_map/ppermute | solution.py:129
  92.1 6.6 %shard_map.122.refs_3_ = f32[40,1,128]{2,1,0:T(1,128)} custom-call(s32[240]{0:T(256)} %reshape_squeeze.6.refs_0_, bf16[40,6,128,128]{3,2,1,0:T(8,128)(2,1)} %bitcast.38, f32[40,128,128]{2,1,0:T(8,128)} %bitcast.53, f32[40,1,128]{2,1,0:T(1,128)} %shard_map.119.refs_3_, f32[2,1,128]{2,1,0:T(1,128)} %copy-done.3, f32[40,1,128]{2,1,0:T(1,128)} %bitcast.59, ...), custom_call_target="tpu_custom_call" | custom-call | flops 9175040 | bytes 10485760 | tf_op jit(solution)/shard_map/pallas_call | solution.py:78
  99.2 2.6 %shard_map.124 = f32[2,1,128]{2,1,0:T(1,128)} custom-call(s32[240]{0:T(256)} %reshape_squeeze.6.refs_0_, bf16[40,6,128,128]{3,2,1,0:T(8,128)(2,1)} %bitcast.39, f32[40,128,128]{2,1,0:T(8,128)} %bitcast.54, f32[40,1,128]{2,1,0:T(1,128)} %shard_map.122.refs_3_, f32[2,1,128]{2,1,0:T(1,128)} %copy-done.4, f32[40,1,128]{2,1,0:T(1,128)} %multiply_add_fusion.refs_1_.refs_5_, ...), custom_call_target="tpu_custom_call" | custom-call | flops 458752 | bytes 524288 | tf_op jit(solution)/shard_map/pallas_call | solution.py:78
  101.8 2.7 %collective-permute-start.12 = (f32[2,1,128]{2,1,0:T(1,128)}, f32[2,1,128]{2,1,0:T(1,128)S(1)}, u32[]{:S(2)}, u32[]{:S(2)}) collective-permute-start(f32[2,1,128]{2,1,0:T(1,128)} %shard_map.124), channel_id=1, source_target_pairs={{0,1},{1,0},{2,3},{3,2},{4,5},{5,4},{6,7},{7,6},{8,9},{9,8},{10,11... | collective-permute-start | bytes 3080 | tf_op jit(solution)/shard_map/ppermute | solution.py:22
  104.5 6.6 %shard_map.123.refs_3_ = f32[40,1,128]{2,1,0:T(1,128)} custom-call(s32[240]{0:T(256)} %reshape_squeeze.6.refs_0_, bf16[40,6,128,128]{3,2,1,0:T(8,128)(2,1)} %bitcast.40, f32[40,128,128]{2,1,0:T(8,128)} %bitcast.55, f32[40,1,128]{2,1,0:T(1,128)} %shard_map.122.refs_3_, f32[2,1,128]{2,1,0:T(1,128)} %copy-done.4, f32[40,1,128]{2,1,0:T(1,128)} %bitcast.60, ...), custom_call_target="tpu_custom_call" | custom-call | flops 9175040 | bytes 10485760 | tf_op jit(solution)/shard_map/pallas_call | solution.py:78
  111.6 2.6 %shard_map.126 = f32[2,1,128]{2,1,0:T(1,128)} custom-call(s32[240]{0:T(256)} %reshape_squeeze.6.refs_0_, bf16[40,6,128,128]{3,2,1,0:T(8,128)(2,1)} %bitcast.41, f32[40,128,128]{2,1,0:T(8,128)} %bitcast.56, f32[40,1,128]{2,1,0:T(1,128)} %shard_map.123.refs_3_, f32[2,1,128]{2,1,0:T(1,128)} %copy-done.8, f32[40,1,128]{2,1,0:T(1,128)} %multiply_add_fusion.refs_1_.refs_5_, ...), custom_call_target="tpu_custom_call" | custom-call | flops 458752 | bytes 524288 | tf_op jit(solution)/shard_map/pallas_call | solution.py:78
  114.5 6.6 %shard_map.125.refs_3_ = f32[40,1,128]{2,1,0:T(1,128)} custom-call(s32[240]{0:T(256)} %reshape_squeeze.6.refs_0_, bf16[40,6,128,128]{3,2,1,0:T(8,128)(2,1)} %bitcast.42, f32[40,128,128]{2,1,0:T(8,128)} %bitcast.57, f32[40,1,128]{2,1,0:T(1,128)} %shard_map.123.refs_3_, f32[2,1,128]{2,1,0:T(1,128)} %copy-done.8, f32[40,1,128]{2,1,0:T(1,128)} %bitcast.61, ...), custom_call_target="tpu_custom_call" | custom-call | flops 9175040 | bytes 10485760 | tf_op jit(solution)/shard_map/pallas_call | solution.py:78
  121.7 6.6 %shard_map.127 = f32[40,1,128]{2,1,0:T(1,128)} custom-call(s32[240]{0:T(256)} %reshape_squeeze.6.refs_0_, bf16[40,6,128,128]{3,2,1,0:T(8,128)(2,1)} %bitcast.43, f32[40,128,128]{2,1,0:T(8,128)} %bitcast.58, f32[40,1,128]{2,1,0:T(1,128)} %shard_map.125.refs_3_, f32[2,1,128]{2,1,0:T(1,128)} %copy-done.9, f32[40,1,128]{2,1,0:T(1,128)} %bitcast.62, ...), custom_call_target="tpu_custom_call" | custom-call | flops 9175040 | bytes 10485760 | tf_op jit(solution)/shard_map/pallas_call | solution.py:78
  129.0 5.1 %collective-permute-start.14 = (f32[1,4,2,128]{3,2,1,0:T(2,128)S(1)}, f32[1,4,2,128]{3,2,1,0:T(2,128)S(1)}, u32[]{:S(2)}, u32[]{:S(2)}) collective-permute-start(f32[1,4,2,128]{3,2,1,0:T(2,128)S(1)} %get-tuple-element.13), channel_id=1, source_target_pairs={{0,16},{2,18},{4,20},{6,22},{8,24},{10,26},{12,28},{14,30},{16,0},... | collective-permute-start | bytes 12296 | tf_op jit(solution)/shard_map/ppermute | solution.py:112
  134.2 1.3 collective-permute-done.14
  135.4 2.9 %collective-permute-start.15 = (f32[2,4,2,128]{3,2,1,0:T(2,128)S(1)}, f32[2,4,2,128]{3,2,1,0:T(2,128)S(1)}, u32[]{:S(2)}, u32[]{:S(2)}) collective-permute-start(f32[2,4,2,128]{3,2,1,0:T(2,128)S(1)} %pad_maximum_fusion.9), channel_id=1, source_target_pairs={{0,64},{2,66},{4,68},{6,70},{8,72},{10,74},{12,76},{14,78},{16,80}... | collective-permute-start | bytes 24584 | tf_op jit(solution)/shard_map/ppermute | solution.py:112
  138.3 1.1 collective-permute-done.15
  139.4 1.1 collective-permute-start.16
  140.6 2.4 %collective-permute-done.16 = f32[4,4,2,128]{3,2,1,0:T(2,128)S(1)} collective-permute-done((f32[4,4,2,128]{3,2,1,0:T(2,128)S(1)}, f32[4,4,2,128]{3,2,1,0:T(2,128)S(1)}, u32[]{:S(2)}, u32[]{:S(2)}) %collective-permute-start.16) | collective-permute-done | bytes 16416 | tf_op jit(solution)/shard_map/ppermute | solution.py:112
  143.0 1.2 collective-permute-start.17
  144.3 1.6 collective-permute-done.17
  145.9 1.4 collective-permute-start.18
  147.3 1.8 %collective-permute-done.18 = f32[16,4,2,128]{3,2,1,0:T(2,128)S(1)} collective-permute-done((f32[16,4,2,128]{3,2,1,0:T(2,128)S(1)}, f32[16,4,2,128]{3,2,1,0:T(2,128)S(1)}, u32[]{:S(2)}, u32[]{:S(2)}) %collective-permute-start.18) | collective-permute-done | bytes 65568 | tf_op jit(solution)/shard_map/ppermute | solution.py:112
  149.2 1.7 %collective-permute-start.19 = (f32[32,4,2,128]{3,2,1,0:T(2,128)S(1)}, f32[32,4,2,128]{3,2,1,0:T(2,128)S(1)}, u32[]{:S(2)}, u32[]{:S(2)}) collective-permute-start(f32[32,4,2,128]{3,2,1,0:T(2,128)S(1)} %get-tuple-element.14), channel_id=1, source_target_pairs={{0,4},{2,6},{4,0},{6,2},{8,12},{10,14},{12,8},{14,10},{16,20},{18,... | collective-permute-start | bytes 393224 | tf_op jit(solution)/shard_map/ppermute | solution.py:112
  150.9 2.4 %collective-permute-done.19 = f32[32,4,2,128]{3,2,1,0:T(2,128)S(1)} collective-permute-done((f32[32,4,2,128]{3,2,1,0:T(2,128)S(1)}, f32[32,4,2,128]{3,2,1,0:T(2,128)S(1)}, u32[]{:S(2)}, u32[]{:S(2)}) %collective-permute-start.19) | collective-permute-done | bytes 131104 | tf_op jit(solution)/shard_map/ppermute | solution.py:112
  153.9 7.9 %collective-permute-start.20 = (f32[4,2,128]{2,1,0:T(2,128)S(1)}, f32[4,2,128]{2,1,0:T(2,128)S(1)}, u32[]{:S(2)}, u32[]{:S(2)}) collective-permute-start(f32[4,2,128]{2,1,0:T(2,128)S(1)} %broadcast_select_fusion), channel_id=1, source_target_pairs={{0,2},{2,0},{4,6},{6,4},{8,10},{10,8},{12,14},{14,12},{16,18},{18,... | collective-permute-start | bytes 12296 | tf_op jit(solution)/shard_map/ppermute | solution.py:129
  (81 shorter events, 15.9 us)
Async XLA Ops:
  0.6 0.7 copy-start
  5.8 11.3 %collective-permute-start = (f32[2,1,128]{2,1,0:T(1,128)}, f32[2,1,128]{2,1,0:T(1,128)S(1)}, u32[]{:S(2)}, u32[]{:S(2)}) collective-permute-start(f32[2,1,128]{2,1,0:T(1,128)} %shard_map.114), channel_id=1, source_target_pairs={{0,1},{1,0},{2,3},{3,2},{4,5},{5,4},{6,7},{7,6},{8,9},{9,8},{10,11... | collective-permute-start | bytes 3080 | tf_op jit(solution)/shard_map/ppermute | solution.py:22
  17.1 0.7 copy-start.5
  20.4 6.6 %collective-permute-start.1 = (f32[2,1,128]{2,1,0:T(1,128)}, f32[2,1,128]{2,1,0:T(1,128)S(1)}, u32[]{:S(2)}, u32[]{:S(2)}) collective-permute-start(f32[2,1,128]{2,1,0:T(1,128)} %shard_map.116), channel_id=1, source_target_pairs={{0,1},{1,0},{2,3},{3,2},{4,5},{5,4},{6,7},{7,6},{8,9},{9,8},{10,11... | collective-permute-start | bytes 3080 | tf_op jit(solution)/shard_map/ppermute | solution.py:22
  27.0 0.6 copy-start.6
  30.2 9.6 %collective-permute-start.2 = (f32[2,1,128]{2,1,0:T(1,128)}, f32[2,1,128]{2,1,0:T(1,128)S(1)}, u32[]{:S(2)}, u32[]{:S(2)}) collective-permute-start(f32[2,1,128]{2,1,0:T(1,128)} %shard_map.118), channel_id=1, source_target_pairs={{0,1},{1,0},{2,3},{3,2},{4,5},{5,4},{6,7},{7,6},{8,9},{9,8},{10,11... | collective-permute-start | bytes 3080 | tf_op jit(solution)/shard_map/ppermute | solution.py:22
  39.8 7.8 %copy-start.2 = (f32[1,1,4,2,128]{4,3,2,1,0:T(2,128)S(1)}, f32[1,1,4,2,128]{4,3,2,1,0:T(2,128)}, u32[]{:S(2)}) copy-start(f32[1,1,4,2,128]{4,3,2,1,0:T(2,128)} %param.19) | copy-start | bytes 12292
  39.8 0.6 copy-start.7
  50.3 21.2 %copy-start.1 = (s32[4,128]{1,0:T(4,128)S(1)}, s32[4,128]{1,0:T(4,128)}, u32[]{:S(2)}) copy-start(s32[4,128]{1,0:T(4,128)} %param.18) | copy-start | bytes 6148
  50.3 7.9 %collective-permute-start.4 = (f32[1,4,2,128]{3,2,1,0:T(2,128)S(1)}, f32[1,4,2,128]{3,2,1,0:T(2,128)S(1)}, u32[]{:S(2)}, u32[]{:S(2)}) collective-permute-start(f32[1,4,2,128]{3,2,1,0:T(2,128)S(1)} %bitcast.68), channel_id=1, source_target_pairs={{0,16},{2,18},{4,20},{6,22},{8,24},{10,26},{12,28},{14,30},{16,0},... | collective-permute-start | bytes 12296 | tf_op jit(solution)/shard_map/ppermute | solution.py:112
  58.2 4.0 %collective-permute-start.5 = (f32[2,4,2,128]{3,2,1,0:T(2,128)S(1)}, f32[2,4,2,128]{3,2,1,0:T(2,128)S(1)}, u32[]{:S(2)}, u32[]{:S(2)}) collective-permute-start(f32[2,4,2,128]{3,2,1,0:T(2,128)S(1)} %pad_maximum_fusion.8), channel_id=1, source_target_pairs={{0,64},{2,66},{4,68},{6,70},{8,72},{10,74},{12,76},{14,78},{16,80}... | collective-permute-start | bytes 24584 | tf_op jit(solution)/shard_map/ppermute | solution.py:112
  62.2 8.9 %collective-permute-start.6 = (f32[4,4,2,128]{3,2,1,0:T(2,128)S(1)}, f32[4,4,2,128]{3,2,1,0:T(2,128)S(1)}, u32[]{:S(2)}, u32[]{:S(2)}) collective-permute-start(f32[4,4,2,128]{3,2,1,0:T(2,128)S(1)} %pad_maximum_fusion.6), channel_id=1, source_target_pairs={{0,8},{2,10},{4,12},{6,14},{8,0},{10,2},{12,4},{14,6},{16,24},{18,... | collective-permute-start | bytes 49160 | tf_op jit(solution)/shard_map/ppermute | solution.py:112
  63.7 4.1 %collective-permute-start.3 = (f32[2,1,128]{2,1,0:T(1,128)}, f32[2,1,128]{2,1,0:T(1,128)S(1)}, u32[]{:S(2)}, u32[]{:S(2)}) collective-permute-start(f32[2,1,128]{2,1,0:T(1,128)} %shard_map.120), channel_id=1, source_target_pairs={{0,1},{1,0},{2,3},{3,2},{4,5},{5,4},{6,7},{7,6},{8,9},{9,8},{10,11... | collective-permute-start | bytes 3080 | tf_op jit(solution)/shard_map/ppermute | solution.py:22
  67.9 0.6 copy-start.3
  71.1 2.9 %collective-permute-start.7 = (f32[8,4,2,128]{3,2,1,0:T(2,128)S(1)}, f32[8,4,2,128]{3,2,1,0:T(2,128)S(1)}, u32[]{:S(2)}, u32[]{:S(2)}) collective-permute-start(f32[8,4,2,128]{3,2,1,0:T(2,128)S(1)} %pad_maximum_fusion.2), channel_id=1, source_target_pairs={{0,128},{2,130},{4,132},{6,134},{8,136},{10,138},{12,140},{14,142}... | collective-permute-start | bytes 98312 | tf_op jit(solution)/shard_map/ppermute | solution.py:112
  74.0 3.2 %collective-permute-start.8 = (f32[16,4,2,128]{3,2,1,0:T(2,128)S(1)}, f32[16,4,2,128]{3,2,1,0:T(2,128)S(1)}, u32[]{:S(2)}, u32[]{:S(2)}) collective-permute-start(f32[16,4,2,128]{3,2,1,0:T(2,128)S(1)} %pad_maximum_fusion.1), channel_id=1, source_target_pairs={{0,32},{2,34},{4,36},{6,38},{8,40},{10,42},{12,44},{14,46},{16,48}... | collective-permute-start | bytes 196616 | tf_op jit(solution)/shard_map/ppermute | solution.py:112
  77.2 4.1 %collective-permute-start.9 = (f32[32,4,2,128]{3,2,1,0:T(2,128)S(1)}, f32[32,4,2,128]{3,2,1,0:T(2,128)S(1)}, u32[]{:S(2)}, u32[]{:S(2)}) collective-permute-start(f32[32,4,2,128]{3,2,1,0:T(2,128)S(1)} %pad_maximum_fusion), channel_id=1, source_target_pairs={{0,4},{2,6},{4,0},{6,2},{8,12},{10,14},{12,8},{14,10},{16,20},{18,... | collective-permute-start | bytes 393224 | tf_op jit(solution)/shard_map/ppermute | solution.py:112
  82.0 9.4 %collective-permute-start.10 = (f32[4,2,128]{2,1,0:T(2,128)S(1)}, f32[4,2,128]{2,1,0:T(2,128)S(1)}, u32[]{:S(2)}, u32[]{:S(2)}) collective-permute-start(f32[4,2,128]{2,1,0:T(2,128)S(1)} %broadcast_select_fusion.1), channel_id=1, source_target_pairs={{0,2},{2,0},{4,6},{6,4},{8,10},{10,8},{12,14},{14,12},{16,18},{18,... | collective-permute-start | bytes 12296 | tf_op jit(solution)/shard_map/ppermute | solution.py:129
  90.5 8.1 %collective-permute-start.11 = (f32[2,1,128]{2,1,0:T(1,128)}, f32[2,1,128]{2,1,0:T(1,128)S(1)}, u32[]{:S(2)}, u32[]{:S(2)}) collective-permute-start(f32[2,1,128]{2,1,0:T(1,128)} %shard_map.121), channel_id=1, source_target_pairs={{0,1},{1,0},{2,3},{3,2},{4,5},{5,4},{6,7},{7,6},{8,9},{9,8},{10,11... | collective-permute-start | bytes 3080 | tf_op jit(solution)/shard_map/ppermute | solution.py:22
  98.6 0.6 copy-start.4
  101.8 9.2 %collective-permute-start.12 = (f32[2,1,128]{2,1,0:T(1,128)}, f32[2,1,128]{2,1,0:T(1,128)S(1)}, u32[]{:S(2)}, u32[]{:S(2)}) collective-permute-start(f32[2,1,128]{2,1,0:T(1,128)} %shard_map.124), channel_id=1, source_target_pairs={{0,1},{1,0},{2,3},{3,2},{4,5},{5,4},{6,7},{7,6},{8,9},{9,8},{10,11... | collective-permute-start | bytes 3080 | tf_op jit(solution)/shard_map/ppermute | solution.py:22
  111.0 0.6 copy-start.8
  114.2 6.9 %collective-permute-start.13 = (f32[2,1,128]{2,1,0:T(1,128)}, f32[2,1,128]{2,1,0:T(1,128)S(1)}, u32[]{:S(2)}, u32[]{:S(2)}) collective-permute-start(f32[2,1,128]{2,1,0:T(1,128)} %shard_map.126), channel_id=1, source_target_pairs={{0,1},{1,0},{2,3},{3,2},{4,5},{5,4},{6,7},{7,6},{8,9},{9,8},{10,11... | collective-permute-start | bytes 3080 | tf_op jit(solution)/shard_map/ppermute | solution.py:22
  121.1 0.6 copy-start.9
  129.0 6.4 %collective-permute-start.14 = (f32[1,4,2,128]{3,2,1,0:T(2,128)S(1)}, f32[1,4,2,128]{3,2,1,0:T(2,128)S(1)}, u32[]{:S(2)}, u32[]{:S(2)}) collective-permute-start(f32[1,4,2,128]{3,2,1,0:T(2,128)S(1)} %get-tuple-element.13), channel_id=1, source_target_pairs={{0,16},{2,18},{4,20},{6,22},{8,24},{10,26},{12,28},{14,30},{16,0},... | collective-permute-start | bytes 12296 | tf_op jit(solution)/shard_map/ppermute | solution.py:112
  135.4 4.0 %collective-permute-start.15 = (f32[2,4,2,128]{3,2,1,0:T(2,128)S(1)}, f32[2,4,2,128]{3,2,1,0:T(2,128)S(1)}, u32[]{:S(2)}, u32[]{:S(2)}) collective-permute-start(f32[2,4,2,128]{3,2,1,0:T(2,128)S(1)} %pad_maximum_fusion.9), channel_id=1, source_target_pairs={{0,64},{2,66},{4,68},{6,70},{8,72},{10,74},{12,76},{14,78},{16,80}... | collective-permute-start | bytes 24584 | tf_op jit(solution)/shard_map/ppermute | solution.py:112
  139.4 3.6 %collective-permute-start.16 = (f32[4,4,2,128]{3,2,1,0:T(2,128)S(1)}, f32[4,4,2,128]{3,2,1,0:T(2,128)S(1)}, u32[]{:S(2)}, u32[]{:S(2)}) collective-permute-start(f32[4,4,2,128]{3,2,1,0:T(2,128)S(1)} %pad_maximum_fusion.7), channel_id=1, source_target_pairs={{0,8},{2,10},{4,12},{6,14},{8,0},{10,2},{12,4},{14,6},{16,24},{18,... | collective-permute-start | bytes 49160 | tf_op jit(solution)/shard_map/ppermute | solution.py:112
  143.0 2.9 %collective-permute-start.17 = (f32[8,4,2,128]{3,2,1,0:T(2,128)S(1)}, f32[8,4,2,128]{3,2,1,0:T(2,128)S(1)}, u32[]{:S(2)}, u32[]{:S(2)}) collective-permute-start(f32[8,4,2,128]{3,2,1,0:T(2,128)S(1)} %pad_maximum_fusion.3), channel_id=1, source_target_pairs={{0,128},{2,130},{4,132},{6,134},{8,136},{10,138},{12,140},{14,142}... | collective-permute-start | bytes 98312 | tf_op jit(solution)/shard_map/ppermute | solution.py:112
  145.9 3.2 %collective-permute-start.18 = (f32[16,4,2,128]{3,2,1,0:T(2,128)S(1)}, f32[16,4,2,128]{3,2,1,0:T(2,128)S(1)}, u32[]{:S(2)}, u32[]{:S(2)}) collective-permute-start(f32[16,4,2,128]{3,2,1,0:T(2,128)S(1)} %get-tuple-element.18), channel_id=1, source_target_pairs={{0,32},{2,34},{4,36},{6,38},{8,40},{10,42},{12,44},{14,46},{16,48}... | collective-permute-start | bytes 196616 | tf_op jit(solution)/shard_map/ppermute | solution.py:112
  149.2 4.1 %collective-permute-start.19 = (f32[32,4,2,128]{3,2,1,0:T(2,128)S(1)}, f32[32,4,2,128]{3,2,1,0:T(2,128)S(1)}, u32[]{:S(2)}, u32[]{:S(2)}) collective-permute-start(f32[32,4,2,128]{3,2,1,0:T(2,128)S(1)} %get-tuple-element.14), channel_id=1, source_target_pairs={{0,4},{2,6},{4,0},{6,2},{8,12},{10,14},{12,8},{14,10},{16,20},{18,... | collective-permute-start | bytes 393224 | tf_op jit(solution)/shard_map/ppermute | solution.py:112
  153.9 8.7 %collective-permute-start.20 = (f32[4,2,128]{2,1,0:T(2,128)S(1)}, f32[4,2,128]{2,1,0:T(2,128)S(1)}, u32[]{:S(2)}, u32[]{:S(2)}) collective-permute-start(f32[4,2,128]{2,1,0:T(2,128)S(1)} %broadcast_select_fusion), channel_id=1, source_target_pairs={{0,2},{2,0},{4,6},{6,4},{8,10},{10,8},{12,14},{14,12},{16,18},{18,... | collective-permute-start | bytes 12296 | tf_op jit(solution)/shard_map/ppermute | solution.py:129

commit v7 on v3

--- a/solution.py
+++ b/solution.py
@@ -89,7 +89,7 @@
 
 def doubling_order(bits):
     if bits == 7:
-        return [3, 5, 2, 6, 4, 1, 0]
+        return [0, 1, 4, 6, 2, 5, 3]
     return list(range(bits - 1, -1, -1))
 
 

time: 165 us -> 174 us (1.055)
  the two profiles are of different devices: /device:TPU:1 before, /device:TPU:64 now
where the time goes in v7:
time: 174 us; the launch traced here: 173 us
  Pallas kernels  65.9 us (38%)
  waiting for transfers between devices  53.3 us (31%)
  starting transfers between devices  36 us (21%)
  local copies, waits for them, and re-layouts  9.8 us (6%)
  other arithmetic  7.52 us (4%)
    pallas_call x15, Pallas kernels, block_sweep(): pl.pallas_call(functools.partial(sweep_kernel, coupled_terms=coupling is...  65.9 us
    ppermute x14, waiting for transfers between devices, exchange(): held = jnp.concatenate([held, lax.ppermute(held, 'sub', route)], axis=0)  48.5 us
    ppermute x14, starting transfers between devices, exchange(): held = jnp.concatenate([held, lax.ppermute(held, 'sub', route)], axis=0)  24.7 us
    ppermute x7, starting transfers between devices, partner(): return lax.ppermute(block, axis, route)  11.2 us
    ppermute x7, waiting for transfers between devices, partner(): return lax.ppermute(block, axis, route)  4.79 us
    unnamed x31, local copies, waits for them, and re-layouts  4.3 us
  transfers between devices with their start and end apart: 21, of which 14 were waited for; matrix products, arithmetic and copies ran while one was open for 4% of the time, Pallas kernels for 22%

profile of v7, /device:TPU:64, one launch (start us, length us, event | category | flops | bytes accessed | tf_op | source)
XLA Modules:
  0.0 173.3 jit_solution(11965709959580707353)
XLA Ops:
  1.4 0.8 gather_fusion
  2.8 1.4 multiply_add_fusion.refs_1_.refs_5_
  4.2 1.6 shard_map.114
  5.8 3.0 %collective-permute-start = (f32[2,1,128]{2,1,0:T(1,128)}, f32[2,1,128]{2,1,0:T(1,128)S(1)}, u32[]{:S(2)}, u32[]{:S(2)}) collective-permute-start(f32[2,1,128]{2,1,0:T(1,128)} %shard_map.114), channel_id=1, source_target_pairs={{0,1},{1,0},{2,3},{3,2},{4,5},{5,4},{6,7},{7,6},{8,9},{9,8},{10,11... | collective-permute-start | bytes 3080 | tf_op jit(solution)/shard_map/ppermute | solution.py:22
  8.9 0.8 bitcast_add_fusion
  9.7 0.7 slice_add_fusion.1
  10.4 0.8 select_reduce_fusion
  12.4 0.8 copy.21
  13.8 2.8 %shard_map.113.refs_3_ = f32[40,1,128]{2,1,0:T(1,128)} custom-call(f32[40,128,128]{2,1,0:T(8,128)} %bitcast.44, f32[40,1,128]{2,1,0:T(1,128)} %bitcast.62), custom_call_target="tpu_custom_call" | custom-call | flops 1310720 | bytes 2621440 | tf_op jit(solution)/shard_map/pallas_call | solution.py:78
  16.6 0.7 mul.72.refs_6_
  17.3 2.6 %shard_map.116 = f32[2,1,128]{2,1,0:T(1,128)} custom-call(s32[240]{0:T(256)} %reshape_squeeze.6.refs_0_, bf16[40,6,128,128]{3,2,1,0:T(8,128)(2,1)} %bitcast.30, f32[40,128,128]{2,1,0:T(8,128)} %bitcast.45, f32[40,1,128]{2,1,0:T(1,128)} %shard_map.113.refs_3_, f32[2,1,128]{2,1,0:T(1,128)} %copy-done.4, f32[40,1,128]{2,1,0:T(1,128)} %multiply_add_fusion.refs_1_.refs_5_, ...), custom_call_target="tpu_custom_call" | custom-call | flops 458752 | bytes 524288 | tf_op jit(solution)/shard_map/pallas_call | solution.py:78
  20.4 6.6 %shard_map.115.refs_3_ = f32[40,1,128]{2,1,0:T(1,128)} custom-call(s32[240]{0:T(256)} %reshape_squeeze.6.refs_0_, bf16[40,6,128,128]{3,2,1,0:T(8,128)(2,1)} %bitcast.31, f32[40,128,128]{2,1,0:T(8,128)} %bitcast.46, f32[40,1,128]{2,1,0:T(1,128)} %shard_map.113.refs_3_, f32[2,1,128]{2,1,0:T(1,128)} %copy-done.4, f32[40,1,128]{2,1,0:T(1,128)} %bitcast.63, ...), custom_call_target="tpu_custom_call" | custom-call | flops 9175040 | bytes 10485760 | tf_op jit(solution)/shard_map/pallas_call | solution.py:78
  27.5 2.6 %shard_map.118 = f32[2,1,128]{2,1,0:T(1,128)} custom-call(s32[240]{0:T(256)} %reshape_squeeze.6.refs_0_, bf16[40,6,128,128]{3,2,1,0:T(8,128)(2,1)} %bitcast.32, f32[40,128,128]{2,1,0:T(8,128)} %bitcast.47, f32[40,1,128]{2,1,0:T(1,128)} %shard_map.115.refs_3_, f32[2,1,128]{2,1,0:T(1,128)} %copy-done.5, f32[40,1,128]{2,1,0:T(1,128)} %multiply_add_fusion.refs_1_.refs_5_, ...), custom_call_target="tpu_custom_call" | custom-call | flops 458752 | bytes 524288 | tf_op jit(solution)/shard_map/pallas_call | solution.py:78
  30.1 3.0 %collective-permute-start.2 = (f32[2,1,128]{2,1,0:T(1,128)}, f32[2,1,128]{2,1,0:T(1,128)S(1)}, u32[]{:S(2)}, u32[]{:S(2)}) collective-permute-start(f32[2,1,128]{2,1,0:T(1,128)} %shard_map.118), channel_id=1, source_target_pairs={{0,1},{1,0},{2,3},{3,2},{4,5},{5,4},{6,7},{7,6},{8,9},{9,8},{10,11... | collective-permute-start | bytes 3080 | tf_op jit(solution)/shard_map/ppermute | solution.py:22
  33.2 6.6 %shard_map.117.refs_3_ = f32[40,1,128]{2,1,0:T(1,128)} custom-call(s32[240]{0:T(256)} %reshape_squeeze.6.refs_0_, bf16[40,6,128,128]{3,2,1,0:T(8,128)(2,1)} %bitcast.33, f32[40,128,128]{2,1,0:T(8,128)} %bitcast.48, f32[40,1,128]{2,1,0:T(1,128)} %shard_map.115.refs_3_, f32[2,1,128]{2,1,0:T(1,128)} %copy-done.5, f32[40,1,128]{2,1,0:T(1,128)} %bitcast.64, ...), custom_call_target="tpu_custom_call" | custom-call | flops 9175040 | bytes 10485760 | tf_op jit(solution)/shard_map/pallas_call | solution.py:78
  40.3 6.6 %shard_map.119.refs_3_ = f32[40,1,128]{2,1,0:T(1,128)} custom-call(s32[240]{0:T(256)} %reshape_squeeze.6.refs_0_, bf16[40,6,128,128]{3,2,1,0:T(8,128)(2,1)} %bitcast.34, f32[40,128,128]{2,1,0:T(8,128)} %bitcast.49, f32[40,1,128]{2,1,0:T(1,128)} %shard_map.117.refs_3_, f32[2,1,128]{2,1,0:T(1,128)} %copy-done.6, f32[40,1,128]{2,1,0:T(1,128)} %bitcast.65, ...), custom_call_target="tpu_custom_call" | custom-call | flops 9175040 | bytes 10485760 | tf_op jit(solution)/shard_map/pallas_call | solution.py:78
  47.7 2.6 %shard_map.120 = f32[2,1,128]{2,1,0:T(1,128)} custom-call(s32[240]{0:T(256)} %reshape_squeeze.6.refs_0_, bf16[40,6,128,128]{3,2,1,0:T(8,128)(2,1)} %bitcast.35, f32[40,128,128]{2,1,0:T(8,128)} %bitcast.50, f32[40,1,128]{2,1,0:T(1,128)} %shard_map.117.refs_3_, f32[2,1,128]{2,1,0:T(1,128)} %copy-done.6, f32[40,1,128]{2,1,0:T(1,128)} %multiply_add_fusion.refs_1_.refs_5_, ...), custom_call_target="tpu_custom_call" | custom-call | flops 458752 | bytes 524288 | tf_op jit(solution)/shard_map/pallas_call | solution.py:78
  50.3 1.2 collective-permute-done.4
  51.4 1.9 %collective-permute-start.5 = (f32[2,4,2,128]{3,2,1,0:T(2,128)S(1)}, f32[2,4,2,128]{3,2,1,0:T(2,128)S(1)}, u32[]{:S(2)}, u32[]{:S(2)}) collective-permute-start(f32[2,4,2,128]{3,2,1,0:T(2,128)S(1)} %pad_maximum_fusion.9), channel_id=1, source_target_pairs={{0,4},{2,6},{4,0},{6,2},{8,12},{10,14},{12,8},{14,10},{16,20},{18,... | collective-permute-start | bytes 24584 | tf_op jit(solution)/shard_map/ppermute | solution.py:112
  53.4 1.7 collective-permute-done.5
  55.1 1.7 collective-permute-start.6
  57.3 4.8 %collective-permute-done.3.refs_4_ = f32[2,1,128]{2,1,0:T(1,128)S(1)} collective-permute-done((f32[2,1,128]{2,1,0:T(1,128)}, f32[2,1,128]{2,1,0:T(1,128)S(1)}, u32[]{:S(2)}, u32[]{:S(2)}) %collective-permute-start.3) | collective-permute-done | bytes 1056 | tf_op jit(solution)/shard_map/ppermute | solution.py:22
  62.6 2.6 %shard_map.121 = f32[2,1,128]{2,1,0:T(1,128)} custom-call(s32[240]{0:T(256)} %reshape_squeeze.6.refs_0_, bf16[40,6,128,128]{3,2,1,0:T(8,128)(2,1)} %bitcast.36, f32[40,128,128]{2,1,0:T(8,128)} %bitcast.51, f32[40,1,128]{2,1,0:T(1,128)} %shard_map.119.refs_3_, f32[2,1,128]{2,1,0:T(1,128)} %copy-done.2, f32[40,1,128]{2,1,0:T(1,128)} %multiply_add_fusion.refs_1_.refs_5_, ...), custom_call_target="tpu_custom_call" | custom-call | flops 458752 | bytes 524288 | tf_op jit(solution)/shard_map/pallas_call | solution.py:78
  65.9 3.3 %collective-permute-done.7 = f32[8,4,2,128]{3,2,1,0:T(2,128)S(1)} collective-permute-done((f32[8,4,2,128]{3,2,1,0:T(2,128)S(1)}, f32[8,4,2,128]{3,2,1,0:T(2,128)S(1)}, u32[]{:S(2)}, u32[]{:S(2)}) %collective-permute-start.7) | collective-permute-done | bytes 32800 | tf_op jit(solution)/shard_map/ppermute | solution.py:112
  69.3 5.2 %collective-permute-done.8 = f32[16,4,2,128]{3,2,1,0:T(2,128)S(1)} collective-permute-done((f32[16,4,2,128]{3,2,1,0:T(2,128)S(1)}, f32[16,4,2,128]{3,2,1,0:T(2,128)S(1)}, u32[]{:S(2)}, u32[]{:S(2)}) %collective-permute-start.8) | collective-permute-done | bytes 65568 | tf_op jit(solution)/shard_map/ppermute | solution.py:112
  74.6 3.0 %collective-permute-start.9 = (f32[32,4,2,128]{3,2,1,0:T(2,128)S(1)}, f32[32,4,2,128]{3,2,1,0:T(2,128)S(1)}, u32[]{:S(2)}, u32[]{:S(2)}) collective-permute-start(f32[32,4,2,128]{3,2,1,0:T(2,128)S(1)} %pad_maximum_fusion.1), channel_id=1, source_target_pairs={{0,64},{2,66},{4,68},{6,70},{8,72},{10,74},{12,76},{14,78},{16,80}... | collective-permute-start | bytes 393224 | tf_op jit(solution)/shard_map/ppermute | solution.py:112
  78.4 2.7 %collective-permute-done.9 = f32[32,4,2,128]{3,2,1,0:T(2,128)S(1)} collective-permute-done((f32[32,4,2,128]{3,2,1,0:T(2,128)S(1)}, f32[32,4,2,128]{3,2,1,0:T(2,128)S(1)}, u32[]{:S(2)}, u32[]{:S(2)}) %collective-permute-start.9) | collective-permute-done | bytes 131104 | tf_op jit(solution)/shard_map/ppermute | solution.py:112
  81.2 5.8 %collective-permute-start.10 = (f32[64,4,2,128]{3,2,1,0:T(2,128)S(1)}, f32[64,4,2,128]{3,2,1,0:T(2,128)S(1)}, u32[]{:S(2)}, u32[]{:S(2)}) collective-permute-start(f32[64,4,2,128]{3,2,1,0:T(2,128)S(1)} %pad_maximum_fusion), channel_id=1, source_target_pairs={{0,16},{2,18},{4,20},{6,22},{8,24},{10,26},{12,28},{14,30},{16,0},... | collective-permute-start | bytes 786440 | tf_op jit(solution)/shard_map/ppermute | solution.py:112
  87.0 7.7 %collective-permute-done.10 = f32[64,4,2,128]{3,2,1,0:T(2,128)S(1)} collective-permute-done((f32[64,4,2,128]{3,2,1,0:T(2,128)S(1)}, f32[64,4,2,128]{3,2,1,0:T(2,128)S(1)}, u32[]{:S(2)}, u32[]{:S(2)}) %collective-permute-start.10) | collective-permute-done | bytes 262176 | tf_op jit(solution)/shard_map/ppermute | solution.py:112
  95.9 6.6 %shard_map.122.refs_3_ = f32[40,1,128]{2,1,0:T(1,128)} custom-call(s32[240]{0:T(256)} %reshape_squeeze.6.refs_0_, bf16[40,6,128,128]{3,2,1,0:T(8,128)(2,1)} %bitcast.37, f32[40,128,128]{2,1,0:T(8,128)} %bitcast.52, f32[40,1,128]{2,1,0:T(1,128)} %shard_map.119.refs_3_, f32[2,1,128]{2,1,0:T(1,128)} %copy-done.2, f32[40,1,128]{2,1,0:T(1,128)} %bitcast.58, ...), custom_call_target="tpu_custom_call" | custom-call | flops 9175040 | bytes 10485760 | tf_op jit(solution)/shard_map/pallas_call | solution.py:78
  103.0 2.6 %shard_map.124 = f32[2,1,128]{2,1,0:T(1,128)} custom-call(s32[240]{0:T(256)} %reshape_squeeze.6.refs_0_, bf16[40,6,128,128]{3,2,1,0:T(8,128)(2,1)} %bitcast.38, f32[40,128,128]{2,1,0:T(8,128)} %bitcast.53, f32[40,1,128]{2,1,0:T(1,128)} %shard_map.122.refs_3_, f32[2,1,128]{2,1,0:T(1,128)} %copy-done.3, f32[40,1,128]{2,1,0:T(1,128)} %multiply_add_fusion.refs_1_.refs_5_, ...), custom_call_target="tpu_custom_call" | custom-call | flops 458752 | bytes 524288 | tf_op jit(solution)/shard_map/pallas_call | solution.py:78
  106.2 6.6 %shard_map.123.refs_3_ = f32[40,1,128]{2,1,0:T(1,128)} custom-call(s32[240]{0:T(256)} %reshape_squeeze.6.refs_0_, bf16[40,6,128,128]{3,2,1,0:T(8,128)(2,1)} %bitcast.39, f32[40,128,128]{2,1,0:T(8,128)} %bitcast.54, f32[40,1,128]{2,1,0:T(1,128)} %shard_map.122.refs_3_, f32[2,1,128]{2,1,0:T(1,128)} %copy-done.3, f32[40,1,128]{2,1,0:T(1,128)} %bitcast.59, ...), custom_call_target="tpu_custom_call" | custom-call | flops 9175040 | bytes 10485760 | tf_op jit(solution)/shard_map/pallas_call | solution.py:78
  113.3 2.6 %shard_map.126 = f32[2,1,128]{2,1,0:T(1,128)} custom-call(s32[240]{0:T(256)} %reshape_squeeze.6.refs_0_, bf16[40,6,128,128]{3,2,1,0:T(8,128)(2,1)} %bitcast.40, f32[40,128,128]{2,1,0:T(8,128)} %bitcast.55, f32[40,1,128]{2,1,0:T(1,128)} %shard_map.123.refs_3_, f32[2,1,128]{2,1,0:T(1,128)} %copy-done.7, f32[40,1,128]{2,1,0:T(1,128)} %multiply_add_fusion.refs_1_.refs_5_, ...), custom_call_target="tpu_custom_call" | custom-call | flops 458752 | bytes 524288 | tf_op jit(solution)/shard_map/pallas_call | solution.py:78
  115.9 2.9 %collective-permute-start.13 = (f32[2,1,128]{2,1,0:T(1,128)}, f32[2,1,128]{2,1,0:T(1,128)S(1)}, u32[]{:S(2)}, u32[]{:S(2)}) collective-permute-start(f32[2,1,128]{2,1,0:T(1,128)} %shard_map.126), channel_id=1, source_target_pairs={{0,1},{1,0},{2,3},{3,2},{4,5},{5,4},{6,7},{7,6},{8,9},{9,8},{10,11... | collective-permute-start | bytes 3080 | tf_op jit(solution)/shard_map/ppermute | solution.py:22
  118.9 6.6 %shard_map.125.refs_3_ = f32[40,1,128]{2,1,0:T(1,128)} custom-call(s32[240]{0:T(256)} %reshape_squeeze.6.refs_0_, bf16[40,6,128,128]{3,2,1,0:T(8,128)(2,1)} %bitcast.41, f32[40,128,128]{2,1,0:T(8,128)} %bitcast.56, f32[40,1,128]{2,1,0:T(1,128)} %shard_map.123.refs_3_, f32[2,1,128]{2,1,0:T(1,128)} %copy-done.7, f32[40,1,128]{2,1,0:T(1,128)} %bitcast.60, ...), custom_call_target="tpu_custom_call" | custom-call | flops 9175040 | bytes 10485760 | tf_op jit(solution)/shard_map/pallas_call | solution.py:78
  126.0 6.6 %shard_map.127 = f32[40,1,128]{2,1,0:T(1,128)} custom-call(s32[240]{0:T(256)} %reshape_squeeze.6.refs_0_, bf16[40,6,128,128]{3,2,1,0:T(8,128)(2,1)} %bitcast.42, f32[40,128,128]{2,1,0:T(8,128)} %bitcast.57, f32[40,1,128]{2,1,0:T(1,128)} %shard_map.125.refs_3_, f32[2,1,128]{2,1,0:T(1,128)} %copy-done.9, f32[40,1,128]{2,1,0:T(1,128)} %bitcast.61, ...), custom_call_target="tpu_custom_call" | custom-call | flops 9175040 | bytes 10485760 | tf_op jit(solution)/shard_map/pallas_call | solution.py:78
  133.4 1.1 collective-permute-done.14
  134.5 1.9 %collective-permute-start.15 = (f32[2,4,2,128]{3,2,1,0:T(2,128)S(1)}, f32[2,4,2,128]{3,2,1,0:T(2,128)S(1)}, u32[]{:S(2)}, u32[]{:S(2)}) collective-permute-start(f32[2,4,2,128]{3,2,1,0:T(2,128)S(1)} %pad_maximum_fusion.10), channel_id=1, source_target_pairs={{0,4},{2,6},{4,0},{6,2},{8,12},{10,14},{12,8},{14,10},{16,20},{18,... | collective-permute-start | bytes 24584 | tf_op jit(solution)/shard_map/ppermute | solution.py:112
  136.4 1.7 collective-permute-done.15
  138.7 3.3 %collective-permute-done.16 = f32[4,4,2,128]{3,2,1,0:T(2,128)S(1)} collective-permute-done((f32[4,4,2,128]{3,2,1,0:T(2,128)S(1)}, f32[4,4,2,128]{3,2,1,0:T(2,128)S(1)}, u32[]{:S(2)}, u32[]{:S(2)}) %collective-permute-start.16) | collective-permute-done | bytes 16416 | tf_op jit(solution)/shard_map/ppermute | solution.py:112
  142.7 3.3 %collective-permute-done.17 = f32[8,4,2,128]{3,2,1,0:T(2,128)S(1)} collective-permute-done((f32[8,4,2,128]{3,2,1,0:T(2,128)S(1)}, f32[8,4,2,128]{3,2,1,0:T(2,128)S(1)}, u32[]{:S(2)}, u32[]{:S(2)}) %collective-permute-start.17) | collective-permute-done | bytes 32800 | tf_op jit(solution)/shard_map/ppermute | solution.py:112
  146.1 1.7 collective-permute-start.18
  147.7 3.6 %collective-permute-done.18 = f32[16,4,2,128]{3,2,1,0:T(2,128)S(1)} collective-permute-done((f32[16,4,2,128]{3,2,1,0:T(2,128)S(1)}, f32[16,4,2,128]{3,2,1,0:T(2,128)S(1)}, u32[]{:S(2)}, u32[]{:S(2)}) %collective-permute-start.18) | collective-permute-done | bytes 65568 | tf_op jit(solution)/shard_map/ppermute | solution.py:112
  151.4 3.0 %collective-permute-start.19 = (f32[32,4,2,128]{3,2,1,0:T(2,128)S(1)}, f32[32,4,2,128]{3,2,1,0:T(2,128)S(1)}, u32[]{:S(2)}, u32[]{:S(2)}) collective-permute-start(f32[32,4,2,128]{3,2,1,0:T(2,128)S(1)} %get-tuple-element.14), channel_id=1, source_target_pairs={{0,64},{2,66},{4,68},{6,70},{8,72},{10,74},{12,76},{14,78},{16,80}... | collective-permute-start | bytes 393224 | tf_op jit(solution)/shard_map/ppermute | solution.py:112
  154.4 3.6 %collective-permute-done.19 = f32[32,4,2,128]{3,2,1,0:T(2,128)S(1)} collective-permute-done((f32[32,4,2,128]{3,2,1,0:T(2,128)S(1)}, f32[32,4,2,128]{3,2,1,0:T(2,128)S(1)}, u32[]{:S(2)}, u32[]{:S(2)}) %collective-permute-start.19) | collective-permute-done | bytes 131104 | tf_op jit(solution)/shard_map/ppermute | solution.py:112
  158.1 3.9 %collective-permute-start.20 = (f32[64,4,2,128]{3,2,1,0:T(2,128)S(1)}, f32[64,4,2,128]{3,2,1,0:T(2,128)S(1)}, u32[]{:S(2)}, u32[]{:S(2)}) collective-permute-start(f32[64,4,2,128]{3,2,1,0:T(2,128)S(1)} %get-tuple-element.10), channel_id=1, source_target_pairs={{0,16},{2,18},{4,20},{6,22},{8,24},{10,26},{12,28},{14,30},{16,0},... | collective-permute-start | bytes 786440 | tf_op jit(solution)/shard_map/ppermute | solution.py:112
  161.9 10.1 %collective-permute-done.20 = f32[64,4,2,128]{3,2,1,0:T(2,128)S(1)} collective-permute-done((f32[64,4,2,128]{3,2,1,0:T(2,128)S(1)}, f32[64,4,2,128]{3,2,1,0:T(2,128)S(1)}, u32[]{:S(2)}, u32[]{:S(2)}) %collective-permute-start.20) | collective-permute-done | bytes 262176 | tf_op jit(solution)/shard_map/ppermute | solution.py:112
  172.1 1.2 gather_fusion.2
  (77 shorter events, 14.5 us)
Async XLA Ops:
  0.6 0.7 copy-start
  5.8 10.8 %collective-permute-start = (f32[2,1,128]{2,1,0:T(1,128)}, f32[2,1,128]{2,1,0:T(1,128)S(1)}, u32[]{:S(2)}, u32[]{:S(2)}) collective-permute-start(f32[2,1,128]{2,1,0:T(1,128)} %shard_map.114), channel_id=1, source_target_pairs={{0,1},{1,0},{2,3},{3,2},{4,5},{5,4},{6,7},{7,6},{8,9},{9,8},{10,11... | collective-permute-start | bytes 3080 | tf_op jit(solution)/shard_map/ppermute | solution.py:22
  16.6 0.7 copy-start.4
  19.9 7.1 %collective-permute-start.1 = (f32[2,1,128]{2,1,0:T(1,128)}, f32[2,1,128]{2,1,0:T(1,128)S(1)}, u32[]{:S(2)}, u32[]{:S(2)}) collective-permute-start(f32[2,1,128]{2,1,0:T(1,128)} %shard_map.116), channel_id=1, source_target_pairs={{0,1},{1,0},{2,3},{3,2},{4,5},{5,4},{6,7},{7,6},{8,9},{9,8},{10,11... | collective-permute-start | bytes 3080 | tf_op jit(solution)/shard_map/ppermute | solution.py:22
  27.0 0.5 copy-start.5
  30.1 9.7 %collective-permute-start.2 = (f32[2,1,128]{2,1,0:T(1,128)}, f32[2,1,128]{2,1,0:T(1,128)S(1)}, u32[]{:S(2)}, u32[]{:S(2)}) collective-permute-start(f32[2,1,128]{2,1,0:T(1,128)} %shard_map.118), channel_id=1, source_target_pairs={{0,1},{1,0},{2,3},{3,2},{4,5},{5,4},{6,7},{7,6},{8,9},{9,8},{10,11... | collective-permute-start | bytes 3080 | tf_op jit(solution)/shard_map/ppermute | solution.py:22
  39.8 7.8 %copy-start.1 = (f32[1,1,4,2,128]{4,3,2,1,0:T(2,128)S(1)}, f32[1,1,4,2,128]{4,3,2,1,0:T(2,128)}, u32[]{:S(2)}) copy-start(f32[1,1,4,2,128]{4,3,2,1,0:T(2,128)} %param.19) | copy-start | bytes 12292
  39.8 0.6 copy-start.6
  50.3 27.3 %copy-start.8 = (s32[4,128]{1,0:T(4,128)S(1)}, s32[4,128]{1,0:T(4,128)}, u32[]{:S(2)}) copy-start(s32[4,128]{1,0:T(4,128)} %param.18) | copy-start | bytes 6148
  50.3 1.2 collective-permute-start.4
  51.4 3.7 %collective-permute-start.5 = (f32[2,4,2,128]{3,2,1,0:T(2,128)S(1)}, f32[2,4,2,128]{3,2,1,0:T(2,128)S(1)}, u32[]{:S(2)}, u32[]{:S(2)}) collective-permute-start(f32[2,4,2,128]{3,2,1,0:T(2,128)S(1)} %pad_maximum_fusion.9), channel_id=1, source_target_pairs={{0,4},{2,6},{4,0},{6,2},{8,12},{10,14},{12,8},{14,10},{16,20},{18,... | collective-permute-start | bytes 24584 | tf_op jit(solution)/shard_map/ppermute | solution.py:112
  55.1 10.1 %collective-permute-start.6 = (f32[4,4,2,128]{3,2,1,0:T(2,128)S(1)}, f32[4,4,2,128]{3,2,1,0:T(2,128)S(1)}, u32[]{:S(2)}, u32[]{:S(2)}) collective-permute-start(f32[4,4,2,128]{3,2,1,0:T(2,128)S(1)} %pad_maximum_fusion.7), channel_id=1, source_target_pairs={{0,32},{2,34},{4,36},{6,38},{8,40},{10,42},{12,44},{14,46},{16,48}... | collective-permute-start | bytes 49160 | tf_op jit(solution)/shard_map/ppermute | solution.py:112
  56.7 5.3 %collective-permute-start.3 = (f32[2,1,128]{2,1,0:T(1,128)}, f32[2,1,128]{2,1,0:T(1,128)S(1)}, u32[]{:S(2)}, u32[]{:S(2)}) collective-permute-start(f32[2,1,128]{2,1,0:T(1,128)} %shard_map.120), channel_id=1, source_target_pairs={{0,1},{1,0},{2,3},{3,2},{4,5},{5,4},{6,7},{7,6},{8,9},{9,8},{10,11... | collective-permute-start | bytes 3080 | tf_op jit(solution)/shard_map/ppermute | solution.py:22
  62.0 0.5 copy-start.2
  65.2 4.0 %collective-permute-start.7 = (f32[8,4,2,128]{3,2,1,0:T(2,128)S(1)}, f32[8,4,2,128]{3,2,1,0:T(2,128)S(1)}, u32[]{:S(2)}, u32[]{:S(2)}) collective-permute-start(f32[8,4,2,128]{3,2,1,0:T(2,128)S(1)} %pad_maximum_fusion.3), channel_id=1, source_target_pairs={{0,128},{2,130},{4,132},{6,134},{8,136},{10,138},{12,140},{14,142}... | collective-permute-start | bytes 98312 | tf_op jit(solution)/shard_map/ppermute | solution.py:112
  69.2 5.3 %collective-permute-start.8 = (f32[16,4,2,128]{3,2,1,0:T(2,128)S(1)}, f32[16,4,2,128]{3,2,1,0:T(2,128)S(1)}, u32[]{:S(2)}, u32[]{:S(2)}) collective-permute-start(f32[16,4,2,128]{3,2,1,0:T(2,128)S(1)} %pad_maximum_fusion.2), channel_id=1, source_target_pairs={{0,8},{2,10},{4,12},{6,14},{8,0},{10,2},{12,4},{14,6},{16,24},{18,... | collective-permute-start | bytes 196616 | tf_op jit(solution)/shard_map/ppermute | solution.py:112
  74.6 6.6 %collective-permute-start.9 = (f32[32,4,2,128]{3,2,1,0:T(2,128)S(1)}, f32[32,4,2,128]{3,2,1,0:T(2,128)S(1)}, u32[]{:S(2)}, u32[]{:S(2)}) collective-permute-start(f32[32,4,2,128]{3,2,1,0:T(2,128)S(1)} %pad_maximum_fusion.1), channel_id=1, source_target_pairs={{0,64},{2,66},{4,68},{6,70},{8,72},{10,74},{12,76},{14,78},{16,80}... | collective-permute-start | bytes 393224 | tf_op jit(solution)/shard_map/ppermute | solution.py:112
  77.8 24.7 %collective-permute-start.11 = (f32[2,1,128]{2,1,0:T(1,128)}, f32[2,1,128]{2,1,0:T(1,128)S(1)}, u32[]{:S(2)}, u32[]{:S(2)}) collective-permute-start(f32[2,1,128]{2,1,0:T(1,128)} %shard_map.121), channel_id=1, source_target_pairs={{0,1},{1,0},{2,3},{3,2},{4,5},{5,4},{6,7},{7,6},{8,9},{9,8},{10,11... | collective-permute-start | bytes 3080 | tf_op jit(solution)/shard_map/ppermute | solution.py:22
  81.2 13.5 %collective-permute-start.10 = (f32[64,4,2,128]{3,2,1,0:T(2,128)S(1)}, f32[64,4,2,128]{3,2,1,0:T(2,128)S(1)}, u32[]{:S(2)}, u32[]{:S(2)}) collective-permute-start(f32[64,4,2,128]{3,2,1,0:T(2,128)S(1)} %pad_maximum_fusion), channel_id=1, source_target_pairs={{0,16},{2,18},{4,20},{6,22},{8,24},{10,26},{12,28},{14,30},{16,0},... | collective-permute-start | bytes 786440 | tf_op jit(solution)/shard_map/ppermute | solution.py:112
  102.5 0.5 copy-start.3
  105.6 7.1 %collective-permute-start.12 = (f32[2,1,128]{2,1,0:T(1,128)}, f32[2,1,128]{2,1,0:T(1,128)S(1)}, u32[]{:S(2)}, u32[]{:S(2)}) collective-permute-start(f32[2,1,128]{2,1,0:T(1,128)} %shard_map.124), channel_id=1, source_target_pairs={{0,1},{1,0},{2,3},{3,2},{4,5},{5,4},{6,7},{7,6},{8,9},{9,8},{10,11... | collective-permute-start | bytes 3080 | tf_op jit(solution)/shard_map/ppermute | solution.py:22
  112.8 0.6 copy-start.7
  115.9 9.5 %collective-permute-start.13 = (f32[2,1,128]{2,1,0:T(1,128)}, f32[2,1,128]{2,1,0:T(1,128)S(1)}, u32[]{:S(2)}, u32[]{:S(2)}) collective-permute-start(f32[2,1,128]{2,1,0:T(1,128)} %shard_map.126), channel_id=1, source_target_pairs={{0,1},{1,0},{2,3},{3,2},{4,5},{5,4},{6,7},{7,6},{8,9},{9,8},{10,11... | collective-permute-start | bytes 3080 | tf_op jit(solution)/shard_map/ppermute | solution.py:22
  125.5 0.5 copy-start.9
  133.3 1.2 collective-permute-start.14
  134.5 3.7 %collective-permute-start.15 = (f32[2,4,2,128]{3,2,1,0:T(2,128)S(1)}, f32[2,4,2,128]{3,2,1,0:T(2,128)S(1)}, u32[]{:S(2)}, u32[]{:S(2)}) collective-permute-start(f32[2,4,2,128]{3,2,1,0:T(2,128)S(1)} %pad_maximum_fusion.10), channel_id=1, source_target_pairs={{0,4},{2,6},{4,0},{6,2},{8,12},{10,14},{12,8},{14,10},{16,20},{18,... | collective-permute-start | bytes 24584 | tf_op jit(solution)/shard_map/ppermute | solution.py:112
  138.2 3.8 %collective-permute-start.16 = (f32[4,4,2,128]{3,2,1,0:T(2,128)S(1)}, f32[4,4,2,128]{3,2,1,0:T(2,128)S(1)}, u32[]{:S(2)}, u32[]{:S(2)}) collective-permute-start(f32[4,4,2,128]{3,2,1,0:T(2,128)S(1)} %pad_maximum_fusion.8), channel_id=1, source_target_pairs={{0,32},{2,34},{4,36},{6,38},{8,40},{10,42},{12,44},{14,46},{16,48}... | collective-permute-start | bytes 49160 | tf_op jit(solution)/shard_map/ppermute | solution.py:112
  142.0 4.0 %collective-permute-start.17 = (f32[8,4,2,128]{3,2,1,0:T(2,128)S(1)}, f32[8,4,2,128]{3,2,1,0:T(2,128)S(1)}, u32[]{:S(2)}, u32[]{:S(2)}) collective-permute-start(f32[8,4,2,128]{3,2,1,0:T(2,128)S(1)} %pad_maximum_fusion.4), channel_id=1, source_target_pairs={{0,128},{2,130},{4,132},{6,134},{8,136},{10,138},{12,140},{14,142}... | collective-permute-start | bytes 98312 | tf_op jit(solution)/shard_map/ppermute | solution.py:112
  146.1 5.3 %collective-permute-start.18 = (f32[16,4,2,128]{3,2,1,0:T(2,128)S(1)}, f32[16,4,2,128]{3,2,1,0:T(2,128)S(1)}, u32[]{:S(2)}, u32[]{:S(2)}) collective-permute-start(f32[16,4,2,128]{3,2,1,0:T(2,128)S(1)} %get-tuple-element.18), channel_id=1, source_target_pairs={{0,8},{2,10},{4,12},{6,14},{8,0},{10,2},{12,4},{14,6},{16,24},{18,... | collective-permute-start | bytes 196616 | tf_op jit(solution)/shard_map/ppermute | solution.py:112
  151.4 6.6 %collective-permute-start.19 = (f32[32,4,2,128]{3,2,1,0:T(2,128)S(1)}, f32[32,4,2,128]{3,2,1,0:T(2,128)S(1)}, u32[]{:S(2)}, u32[]{:S(2)}) collective-permute-start(f32[32,4,2,128]{3,2,1,0:T(2,128)S(1)} %get-tuple-element.14), channel_id=1, source_target_pairs={{0,64},{2,66},{4,68},{6,70},{8,72},{10,74},{12,76},{14,78},{16,80}... | collective-permute-start | bytes 393224 | tf_op jit(solution)/shard_map/ppermute | solution.py:112
  158.1 14.0 %collective-permute-start.20 = (f32[64,4,2,128]{3,2,1,0:T(2,128)S(1)}, f32[64,4,2,128]{3,2,1,0:T(2,128)S(1)}, u32[]{:S(2)}, u32[]{:S(2)}) collective-permute-start(f32[64,4,2,128]{3,2,1,0:T(2,128)S(1)} %get-tuple-element.10), channel_id=1, source_target_pairs={{0,16},{2,18},{4,20},{6,22},{8,24},{10,26},{12,28},{14,30},{16,0},... | collective-permute-start | bytes 786440 | tf_op jit(solution)/shard_map/ppermute | solution.py:112

commit v8 on v3

--- a/solution.py
+++ b/solution.py
@@ -171,7 +171,8 @@
             else:
                 top = sweep_rows(state, ghost, head_source(forcing), G, (blocks - G) // G, 1)
             sent = partner(top, "depth", 0)
-            state = sweep_rows(state, ghost, forcing, body_rows, 0, blocks // body_rows)
+            size = blocks if state is None else body_rows
+            state = sweep_rows(state, ghost, forcing, size, 0, blocks // size)
             ghost = sent
         state2 = state[:, 0]
         outgoing = (

time: 165 us -> 165 us (level)
  no operation moved by 1% of the time
where the time goes in v8:
time: 165 us; the launch traced here: 164 us
  Pallas kernels  66.2 us (40%)
  starting transfers between devices  54.4 us (33%)
  waiting for transfers between devices  25.3 us (15%)
  local copies, waits for them, and re-layouts  9.8 us (6%)
  other arithmetic  7.52 us (5%)
    pallas_call x15, Pallas kernels, block_sweep(): pl.pallas_call(functools.partial(sweep_kernel, coupled_terms=coupling is...  66.2 us
    ppermute x14, starting transfers between devices, exchange(): held = jnp.concatenate([held, lax.ppermute(held, 'sub', route)], axis=0)  43.8 us
    ppermute x14, waiting for transfers between devices, exchange(): held = jnp.concatenate([held, lax.ppermute(held, 'sub', route)], axis=0)  21.4 us
    ppermute x7, starting transfers between devices, partner(): return lax.ppermute(block, axis, route)  10.6 us
    unnamed x31, local copies, waits for them, and re-layouts  4.3 us
    ppermute x7, waiting for transfers between devices, partner(): return lax.ppermute(block, axis, route)  3.92 us
  transfers between devices with their start and end apart: 21, of which 14 were waited for; matrix products, arithmetic and copies ran while one was open for 4% of the time, Pallas kernels for 23%

profile of v8, /device:TPU:1, one launch (start us, length us, event | category | flops | bytes accessed | tf_op | source)
XLA Modules:
  0.0 164.0 jit_solution(17488929463833400381)
XLA Ops:
  2.8 1.4 multiply_add_fusion.refs_1_.refs_5_
  4.2 1.6 shard_map.114
  5.8 3.6 %collective-permute-start = (f32[2,1,128]{2,1,0:T(1,128)}, f32[2,1,128]{2,1,0:T(1,128)S(1)}, u32[]{:S(2)}, u32[]{:S(2)}) collective-permute-start(f32[2,1,128]{2,1,0:T(1,128)} %shard_map.114), channel_id=1, source_target_pairs={{0,1},{1,0},{2,3},{3,2},{4,5},{5,4},{6,7},{7,6},{8,9},{9,8},{10,11... | collective-permute-start | bytes 3080 | tf_op jit(solution)/shard_map/ppermute | solution.py:22
  9.4 0.8 bitcast_add_fusion
  14.4 3.1 %shard_map.113.refs_3_ = f32[40,1,128]{2,1,0:T(1,128)} custom-call(f32[40,128,128]{2,1,0:T(8,128)} %bitcast.44, f32[40,1,128]{2,1,0:T(1,128)} %bitcast.62), custom_call_target="tpu_custom_call" | custom-call | flops 1310720 | bytes 2621440 | tf_op jit(solution)/shard_map/pallas_call | solution.py:78
  18.2 2.6 %shard_map.116 = f32[2,1,128]{2,1,0:T(1,128)} custom-call(s32[240]{0:T(256)} %reshape_squeeze.6.refs_0_, bf16[40,6,128,128]{3,2,1,0:T(8,128)(2,1)} %bitcast.30, f32[40,128,128]{2,1,0:T(8,128)} %bitcast.45, f32[40,1,128]{2,1,0:T(1,128)} %shard_map.113.refs_3_, f32[2,1,128]{2,1,0:T(1,128)} %copy-done.4, f32[40,1,128]{2,1,0:T(1,128)} %multiply_add_fusion.refs_1_.refs_5_, ...), custom_call_target="tpu_custom_call" | custom-call | flops 458752 | bytes 524288 | tf_op jit(solution)/shard_map/pallas_call | solution.py:78
  20.8 6.6 %shard_map.115.refs_3_ = f32[40,1,128]{2,1,0:T(1,128)} custom-call(s32[240]{0:T(256)} %reshape_squeeze.6.refs_0_, bf16[40,6,128,128]{3,2,1,0:T(8,128)(2,1)} %bitcast.31, f32[40,128,128]{2,1,0:T(8,128)} %bitcast.46, f32[40,1,128]{2,1,0:T(1,128)} %shard_map.113.refs_3_, f32[2,1,128]{2,1,0:T(1,128)} %copy-done.4, f32[40,1,128]{2,1,0:T(1,128)} %bitcast.63, ...), custom_call_target="tpu_custom_call" | custom-call | flops 9175040 | bytes 10485760 | tf_op jit(solution)/shard_map/pallas_call | solution.py:78
  27.9 2.6 %shard_map.118 = f32[2,1,128]{2,1,0:T(1,128)} custom-call(s32[240]{0:T(256)} %reshape_squeeze.6.refs_0_, bf16[40,6,128,128]{3,2,1,0:T(8,128)(2,1)} %bitcast.32, f32[40,128,128]{2,1,0:T(8,128)} %bitcast.47, f32[40,1,128]{2,1,0:T(1,128)} %shard_map.115.refs_3_, f32[2,1,128]{2,1,0:T(1,128)} %copy-done.5, f32[40,1,128]{2,1,0:T(1,128)} %multiply_add_fusion.refs_1_.refs_5_, ...), custom_call_target="tpu_custom_call" | custom-call | flops 458752 | bytes 524288 | tf_op jit(solution)/shard_map/pallas_call | solution.py:78
  30.4 3.0 %collective-permute-start.2 = (f32[2,1,128]{2,1,0:T(1,128)}, f32[2,1,128]{2,1,0:T(1,128)S(1)}, u32[]{:S(2)}, u32[]{:S(2)}) collective-permute-start(f32[2,1,128]{2,1,0:T(1,128)} %shard_map.118), channel_id=1, source_target_pairs={{0,1},{1,0},{2,3},{3,2},{4,5},{5,4},{6,7},{7,6},{8,9},{9,8},{10,11... | collective-permute-start | bytes 3080 | tf_op jit(solution)/shard_map/ppermute | solution.py:22
  33.5 6.6 %shard_map.117.refs_3_ = f32[40,1,128]{2,1,0:T(1,128)} custom-call(s32[240]{0:T(256)} %reshape_squeeze.6.refs_0_, bf16[40,6,128,128]{3,2,1,0:T(8,128)(2,1)} %bitcast.33, f32[40,128,128]{2,1,0:T(8,128)} %bitcast.48, f32[40,1,128]{2,1,0:T(1,128)} %shard_map.115.refs_3_, f32[2,1,128]{2,1,0:T(1,128)} %copy-done.5, f32[40,1,128]{2,1,0:T(1,128)} %bitcast.64, ...), custom_call_target="tpu_custom_call" | custom-call | flops 9175040 | bytes 10485760 | tf_op jit(solution)/shard_map/pallas_call | solution.py:78
  40.6 6.6 %shard_map.119.refs_3_ = f32[40,1,128]{2,1,0:T(1,128)} custom-call(s32[240]{0:T(256)} %reshape_squeeze.6.refs_0_, bf16[40,6,128,128]{3,2,1,0:T(8,128)(2,1)} %bitcast.34, f32[40,128,128]{2,1,0:T(8,128)} %bitcast.49, f32[40,1,128]{2,1,0:T(1,128)} %shard_map.117.refs_3_, f32[2,1,128]{2,1,0:T(1,128)} %copy-done.6, f32[40,1,128]{2,1,0:T(1,128)} %bitcast.65, ...), custom_call_target="tpu_custom_call" | custom-call | flops 9175040 | bytes 10485760 | tf_op jit(solution)/shard_map/pallas_call | solution.py:78
  48.0 2.6 %shard_map.120 = f32[2,1,128]{2,1,0:T(1,128)} custom-call(s32[240]{0:T(256)} %reshape_squeeze.6.refs_0_, bf16[40,6,128,128]{3,2,1,0:T(8,128)(2,1)} %bitcast.35, f32[40,128,128]{2,1,0:T(8,128)} %bitcast.50, f32[40,1,128]{2,1,0:T(1,128)} %shard_map.117.refs_3_, f32[2,1,128]{2,1,0:T(1,128)} %copy-done.6, f32[40,1,128]{2,1,0:T(1,128)} %multiply_add_fusion.refs_1_.refs_5_, ...), custom_call_target="tpu_custom_call" | custom-call | flops 458752 | bytes 524288 | tf_op jit(solution)/shard_map/pallas_call | solution.py:78
  50.6 6.9 %collective-permute-start.4 = (f32[1,4,2,128]{3,2,1,0:T(2,128)S(1)}, f32[1,4,2,128]{3,2,1,0:T(2,128)S(1)}, u32[]{:S(2)}, u32[]{:S(2)}) collective-permute-start(f32[1,4,2,128]{3,2,1,0:T(2,128)S(1)} %bitcast.67), channel_id=1, source_target_pairs={{0,16},{2,18},{4,20},{6,22},{8,24},{10,26},{12,28},{14,30},{16,0},... | collective-permute-start | bytes 12296 | tf_op jit(solution)/shard_map/ppermute | solution.py:112
  57.5 1.0 collective-permute-done.4
  58.5 2.9 %collective-permute-start.5 = (f32[2,4,2,128]{3,2,1,0:T(2,128)S(1)}, f32[2,4,2,128]{3,2,1,0:T(2,128)S(1)}, u32[]{:S(2)}, u32[]{:S(2)}) collective-permute-start(f32[2,4,2,128]{3,2,1,0:T(2,128)S(1)} %pad_maximum_fusion.9), channel_id=1, source_target_pairs={{0,64},{2,66},{4,68},{6,70},{8,72},{10,74},{12,76},{14,78},{16,80}... | collective-permute-start | bytes 24584 | tf_op jit(solution)/shard_map/ppermute | solution.py:112
  61.4 1.1 collective-permute-done.5
  62.5 1.5 collective-permute-start.6
  64.3 3.9 %collective-permute-done.3.refs_4_ = f32[2,1,128]{2,1,0:T(1,128)S(1)} collective-permute-done((f32[2,1,128]{2,1,0:T(1,128)}, f32[2,1,128]{2,1,0:T(1,128)S(1)}, u32[]{:S(2)}, u32[]{:S(2)}) %collective-permute-start.3) | collective-permute-done | bytes 1056 | tf_op jit(solution)/shard_map/ppermute | solution.py:22
  68.7 2.6 %shard_map.121 = f32[2,1,128]{2,1,0:T(1,128)} custom-call(s32[240]{0:T(256)} %reshape_squeeze.6.refs_0_, bf16[40,6,128,128]{3,2,1,0:T(8,128)(2,1)} %bitcast.36, f32[40,128,128]{2,1,0:T(8,128)} %bitcast.51, f32[40,1,128]{2,1,0:T(1,128)} %shard_map.119.refs_3_, f32[2,1,128]{2,1,0:T(1,128)} %copy-done.2, f32[40,1,128]{2,1,0:T(1,128)} %multiply_add_fusion.refs_1_.refs_5_, ...), custom_call_target="tpu_custom_call" | custom-call | flops 458752 | bytes 524288 | tf_op jit(solution)/shard_map/pallas_call | solution.py:78
  71.7 2.5 %collective-permute-done.7 = f32[8,4,2,128]{3,2,1,0:T(2,128)S(1)} collective-permute-done((f32[8,4,2,128]{3,2,1,0:T(2,128)S(1)}, f32[8,4,2,128]{3,2,1,0:T(2,128)S(1)}, u32[]{:S(2)}, u32[]{:S(2)}) %collective-permute-start.7) | collective-permute-done | bytes 32800 | tf_op jit(solution)/shard_map/ppermute | solution.py:112
  74.2 1.4 collective-permute-start.8
  75.6 1.8 %collective-permute-done.8 = f32[16,4,2,128]{3,2,1,0:T(2,128)S(1)} collective-permute-done((f32[16,4,2,128]{3,2,1,0:T(2,128)S(1)}, f32[16,4,2,128]{3,2,1,0:T(2,128)S(1)}, u32[]{:S(2)}, u32[]{:S(2)}) %collective-permute-start.8) | collective-permute-done | bytes 65568 | tf_op jit(solution)/shard_map/ppermute | solution.py:112
  77.5 1.7 %collective-permute-start.9 = (f32[32,4,2,128]{3,2,1,0:T(2,128)S(1)}, f32[32,4,2,128]{3,2,1,0:T(2,128)S(1)}, u32[]{:S(2)}, u32[]{:S(2)}) collective-permute-start(f32[32,4,2,128]{3,2,1,0:T(2,128)S(1)} %pad_maximum_fusion.1), channel_id=1, source_target_pairs={{0,4},{2,6},{4,0},{6,2},{8,12},{10,14},{12,8},{14,10},{16,20},{18,... | collective-permute-start | bytes 393224 | tf_op jit(solution)/shard_map/ppermute | solution.py:112
  79.4 0.8 collective-permute-start.11
  80.3 1.3 collective-permute-done.9
  81.7 8.6 %collective-permute-start.10 = (f32[64,4,2,128]{3,2,1,0:T(2,128)S(1)}, f32[64,4,2,128]{3,2,1,0:T(2,128)S(1)}, u32[]{:S(2)}, u32[]{:S(2)}) collective-permute-start(f32[64,4,2,128]{3,2,1,0:T(2,128)S(1)} %pad_maximum_fusion), channel_id=1, source_target_pairs={{0,2},{2,0},{4,6},{6,4},{8,10},{10,8},{12,14},{14,12},{16,18},{18,... | collective-permute-start | bytes 786440 | tf_op jit(solution)/shard_map/ppermute | solution.py:112
  90.3 1.1 collective-permute-done.10
  92.7 6.6 %shard_map.122.refs_3_ = f32[40,1,128]{2,1,0:T(1,128)} custom-call(s32[240]{0:T(256)} %reshape_squeeze.6.refs_0_, bf16[40,6,128,128]{3,2,1,0:T(8,128)(2,1)} %bitcast.37, f32[40,128,128]{2,1,0:T(8,128)} %bitcast.52, f32[40,1,128]{2,1,0:T(1,128)} %shard_map.119.refs_3_, f32[2,1,128]{2,1,0:T(1,128)} %copy-done.2, f32[40,1,128]{2,1,0:T(1,128)} %bitcast.58, ...), custom_call_target="tpu_custom_call" | custom-call | flops 9175040 | bytes 10485760 | tf_op jit(solution)/shard_map/pallas_call | solution.py:78
  99.8 2.6 %shard_map.124 = f32[2,1,128]{2,1,0:T(1,128)} custom-call(s32[240]{0:T(256)} %reshape_squeeze.6.refs_0_, bf16[40,6,128,128]{3,2,1,0:T(8,128)(2,1)} %bitcast.38, f32[40,128,128]{2,1,0:T(8,128)} %bitcast.53, f32[40,1,128]{2,1,0:T(1,128)} %shard_map.122.refs_3_, f32[2,1,128]{2,1,0:T(1,128)} %copy-done.3, f32[40,1,128]{2,1,0:T(1,128)} %multiply_add_fusion.refs_1_.refs_5_, ...), custom_call_target="tpu_custom_call" | custom-call | flops 458752 | bytes 524288 | tf_op jit(solution)/shard_map/pallas_call | solution.py:78
  103.0 6.6 %shard_map.123.refs_3_ = f32[40,1,128]{2,1,0:T(1,128)} custom-call(s32[240]{0:T(256)} %reshape_squeeze.6.refs_0_, bf16[40,6,128,128]{3,2,1,0:T(8,128)(2,1)} %bitcast.39, f32[40,128,128]{2,1,0:T(8,128)} %bitcast.54, f32[40,1,128]{2,1,0:T(1,128)} %shard_map.122.refs_3_, f32[2,1,128]{2,1,0:T(1,128)} %copy-done.3, f32[40,1,128]{2,1,0:T(1,128)} %bitcast.59, ...), custom_call_target="tpu_custom_call" | custom-call | flops 9175040 | bytes 10485760 | tf_op jit(solution)/shard_map/pallas_call | solution.py:78
  110.2 2.6 %shard_map.126 = f32[2,1,128]{2,1,0:T(1,128)} custom-call(s32[240]{0:T(256)} %reshape_squeeze.6.refs_0_, bf16[40,6,128,128]{3,2,1,0:T(8,128)(2,1)} %bitcast.40, f32[40,128,128]{2,1,0:T(8,128)} %bitcast.55, f32[40,1,128]{2,1,0:T(1,128)} %shard_map.123.refs_3_, f32[2,1,128]{2,1,0:T(1,128)} %copy-done.7, f32[40,1,128]{2,1,0:T(1,128)} %multiply_add_fusion.refs_1_.refs_5_, ...), custom_call_target="tpu_custom_call" | custom-call | flops 458752 | bytes 524288 | tf_op jit(solution)/shard_map/pallas_call | solution.py:78
  112.7 2.3 %collective-permute-start.13 = (f32[2,1,128]{2,1,0:T(1,128)}, f32[2,1,128]{2,1,0:T(1,128)S(1)}, u32[]{:S(2)}, u32[]{:S(2)}) collective-permute-start(f32[2,1,128]{2,1,0:T(1,128)} %shard_map.126), channel_id=1, source_target_pairs={{0,1},{1,0},{2,3},{3,2},{4,5},{5,4},{6,7},{7,6},{8,9},{9,8},{10,11... | collective-permute-start | bytes 3080 | tf_op jit(solution)/shard_map/ppermute | solution.py:22
  115.1 6.6 %shard_map.125.refs_3_ = f32[40,1,128]{2,1,0:T(1,128)} custom-call(s32[240]{0:T(256)} %reshape_squeeze.6.refs_0_, bf16[40,6,128,128]{3,2,1,0:T(8,128)(2,1)} %bitcast.41, f32[40,128,128]{2,1,0:T(8,128)} %bitcast.56, f32[40,1,128]{2,1,0:T(1,128)} %shard_map.123.refs_3_, f32[2,1,128]{2,1,0:T(1,128)} %copy-done.7, f32[40,1,128]{2,1,0:T(1,128)} %bitcast.60, ...), custom_call_target="tpu_custom_call" | custom-call | flops 9175040 | bytes 10485760 | tf_op jit(solution)/shard_map/pallas_call | solution.py:78
  122.2 6.6 %shard_map.127 = f32[40,1,128]{2,1,0:T(1,128)} custom-call(s32[240]{0:T(256)} %reshape_squeeze.6.refs_0_, bf16[40,6,128,128]{3,2,1,0:T(8,128)(2,1)} %bitcast.42, f32[40,128,128]{2,1,0:T(8,128)} %bitcast.57, f32[40,1,128]{2,1,0:T(1,128)} %shard_map.125.refs_3_, f32[2,1,128]{2,1,0:T(1,128)} %copy-done.9, f32[40,1,128]{2,1,0:T(1,128)} %bitcast.61, ...), custom_call_target="tpu_custom_call" | custom-call | flops 9175040 | bytes 10485760 | tf_op jit(solution)/shard_map/pallas_call | solution.py:78
  129.5 5.1 %collective-permute-start.14 = (f32[1,4,2,128]{3,2,1,0:T(2,128)S(1)}, f32[1,4,2,128]{3,2,1,0:T(2,128)S(1)}, u32[]{:S(2)}, u32[]{:S(2)}) collective-permute-start(f32[1,4,2,128]{3,2,1,0:T(2,128)S(1)} %get-tuple-element.9), channel_id=1, source_target_pairs={{0,16},{2,18},{4,20},{6,22},{8,24},{10,26},{12,28},{14,30},{16,0},... | collective-permute-start | bytes 12296 | tf_op jit(solution)/shard_map/ppermute | solution.py:112
  134.6 1.2 collective-permute-done.14
  135.9 2.9 %collective-permute-start.15 = (f32[2,4,2,128]{3,2,1,0:T(2,128)S(1)}, f32[2,4,2,128]{3,2,1,0:T(2,128)S(1)}, u32[]{:S(2)}, u32[]{:S(2)}) collective-permute-start(f32[2,4,2,128]{3,2,1,0:T(2,128)S(1)} %pad_maximum_fusion.10), channel_id=1, source_target_pairs={{0,64},{2,66},{4,68},{6,70},{8,72},{10,74},{12,76},{14,78},{16,80}... | collective-permute-start | bytes 24584 | tf_op jit(solution)/shard_map/ppermute | solution.py:112
  138.8 1.1 collective-permute-done.15
  139.9 1.0 collective-permute-start.16
  140.9 2.6 %collective-permute-done.16 = f32[4,4,2,128]{3,2,1,0:T(2,128)S(1)} collective-permute-done((f32[4,4,2,128]{3,2,1,0:T(2,128)S(1)}, f32[4,4,2,128]{3,2,1,0:T(2,128)S(1)}, u32[]{:S(2)}, u32[]{:S(2)}) %collective-permute-start.16) | collective-permute-done | bytes 16416 | tf_op jit(solution)/shard_map/ppermute | solution.py:112
  143.9 2.4 %collective-permute-done.17 = f32[8,4,2,128]{3,2,1,0:T(2,128)S(1)} collective-permute-done((f32[8,4,2,128]{3,2,1,0:T(2,128)S(1)}, f32[8,4,2,128]{3,2,1,0:T(2,128)S(1)}, u32[]{:S(2)}, u32[]{:S(2)}) %collective-permute-start.17) | collective-permute-done | bytes 32800 | tf_op jit(solution)/shard_map/ppermute | solution.py:112
  146.4 1.4 collective-permute-start.18
  147.8 1.8 %collective-permute-done.18 = f32[16,4,2,128]{3,2,1,0:T(2,128)S(1)} collective-permute-done((f32[16,4,2,128]{3,2,1,0:T(2,128)S(1)}, f32[16,4,2,128]{3,2,1,0:T(2,128)S(1)}, u32[]{:S(2)}, u32[]{:S(2)}) %collective-permute-start.18) | collective-permute-done | bytes 65568 | tf_op jit(solution)/shard_map/ppermute | solution.py:112
  149.7 1.7 %collective-permute-start.19 = (f32[32,4,2,128]{3,2,1,0:T(2,128)S(1)}, f32[32,4,2,128]{3,2,1,0:T(2,128)S(1)}, u32[]{:S(2)}, u32[]{:S(2)}) collective-permute-start(f32[32,4,2,128]{3,2,1,0:T(2,128)S(1)} %get-tuple-element.14), channel_id=1, source_target_pairs={{0,4},{2,6},{4,0},{6,2},{8,12},{10,14},{12,8},{14,10},{16,20},{18,... | collective-permute-start | bytes 393224 | tf_op jit(solution)/shard_map/ppermute | solution.py:112
  151.4 2.4 %collective-permute-done.19 = f32[32,4,2,128]{3,2,1,0:T(2,128)S(1)} collective-permute-done((f32[32,4,2,128]{3,2,1,0:T(2,128)S(1)}, f32[32,4,2,128]{3,2,1,0:T(2,128)S(1)}, u32[]{:S(2)}, u32[]{:S(2)}) %collective-permute-start.19) | collective-permute-done | bytes 131104 | tf_op jit(solution)/shard_map/ppermute | solution.py:112
  153.9 7.7 %collective-permute-start.20 = (f32[64,4,2,128]{3,2,1,0:T(2,128)S(1)}, f32[64,4,2,128]{3,2,1,0:T(2,128)S(1)}, u32[]{:S(2)}, u32[]{:S(2)}) collective-permute-start(f32[64,4,2,128]{3,2,1,0:T(2,128)S(1)} %get-tuple-element.10), channel_id=1, source_target_pairs={{0,2},{2,0},{4,6},{6,4},{8,10},{10,8},{12,14},{14,12},{16,18},{18,... | collective-permute-start | bytes 786440 | tf_op jit(solution)/shard_map/ppermute | solution.py:112
  161.6 1.2 collective-permute-done.20
  162.8 1.2 gather_fusion.2
  (77 shorter events, 15.6 us)
Async XLA Ops:
  0.6 0.7 copy-start
  5.8 11.6 %collective-permute-start = (f32[2,1,128]{2,1,0:T(1,128)}, f32[2,1,128]{2,1,0:T(1,128)S(1)}, u32[]{:S(2)}, u32[]{:S(2)}) collective-permute-start(f32[2,1,128]{2,1,0:T(1,128)} %shard_map.114), channel_id=1, source_target_pairs={{0,1},{1,0},{2,3},{3,2},{4,5},{5,4},{6,7},{7,6},{8,9},{9,8},{10,11... | collective-permute-start | bytes 3080 | tf_op jit(solution)/shard_map/ppermute | solution.py:22
  17.5 0.7 copy-start.4
  20.8 6.6 %collective-permute-start.1 = (f32[2,1,128]{2,1,0:T(1,128)}, f32[2,1,128]{2,1,0:T(1,128)S(1)}, u32[]{:S(2)}, u32[]{:S(2)}) collective-permute-start(f32[2,1,128]{2,1,0:T(1,128)} %shard_map.116), channel_id=1, source_target_pairs={{0,1},{1,0},{2,3},{3,2},{4,5},{5,4},{6,7},{7,6},{8,9},{9,8},{10,11... | collective-permute-start | bytes 3080 | tf_op jit(solution)/shard_map/ppermute | solution.py:22
  27.3 0.5 copy-start.5
  30.4 9.6 %collective-permute-start.2 = (f32[2,1,128]{2,1,0:T(1,128)}, f32[2,1,128]{2,1,0:T(1,128)S(1)}, u32[]{:S(2)}, u32[]{:S(2)}) collective-permute-start(f32[2,1,128]{2,1,0:T(1,128)} %shard_map.118), channel_id=1, source_target_pairs={{0,1},{1,0},{2,3},{3,2},{4,5},{5,4},{6,7},{7,6},{8,9},{9,8},{10,11... | collective-permute-start | bytes 3080 | tf_op jit(solution)/shard_map/ppermute | solution.py:22
  40.1 7.8 %copy-start.1 = (f32[1,1,4,2,128]{4,3,2,1,0:T(2,128)S(1)}, f32[1,1,4,2,128]{4,3,2,1,0:T(2,128)}, u32[]{:S(2)}) copy-start(f32[1,1,4,2,128]{4,3,2,1,0:T(2,128)} %param.19) | copy-start | bytes 12292
  40.1 0.6 copy-start.6
  50.6 28.7 %copy-start.8 = (s32[4,128]{1,0:T(4,128)S(1)}, s32[4,128]{1,0:T(4,128)}, u32[]{:S(2)}) copy-start(s32[4,128]{1,0:T(4,128)} %param.18) | copy-start | bytes 6148
  50.6 7.9 %collective-permute-start.4 = (f32[1,4,2,128]{3,2,1,0:T(2,128)S(1)}, f32[1,4,2,128]{3,2,1,0:T(2,128)S(1)}, u32[]{:S(2)}, u32[]{:S(2)}) collective-permute-start(f32[1,4,2,128]{3,2,1,0:T(2,128)S(1)} %bitcast.67), channel_id=1, source_target_pairs={{0,16},{2,18},{4,20},{6,22},{8,24},{10,26},{12,28},{14,30},{16,0},... | collective-permute-start | bytes 12296 | tf_op jit(solution)/shard_map/ppermute | solution.py:112
  58.5 4.0 %collective-permute-start.5 = (f32[2,4,2,128]{3,2,1,0:T(2,128)S(1)}, f32[2,4,2,128]{3,2,1,0:T(2,128)S(1)}, u32[]{:S(2)}, u32[]{:S(2)}) collective-permute-start(f32[2,4,2,128]{3,2,1,0:T(2,128)S(1)} %pad_maximum_fusion.9), channel_id=1, source_target_pairs={{0,64},{2,66},{4,68},{6,70},{8,72},{10,74},{12,76},{14,78},{16,80}... | collective-permute-start | bytes 24584 | tf_op jit(solution)/shard_map/ppermute | solution.py:112
  62.5 8.8 %collective-permute-start.6 = (f32[4,4,2,128]{3,2,1,0:T(2,128)S(1)}, f32[4,4,2,128]{3,2,1,0:T(2,128)S(1)}, u32[]{:S(2)}, u32[]{:S(2)}) collective-permute-start(f32[4,4,2,128]{3,2,1,0:T(2,128)S(1)} %pad_maximum_fusion.7), channel_id=1, source_target_pairs={{0,8},{2,10},{4,12},{6,14},{8,0},{10,2},{12,4},{14,6},{16,24},{18,... | collective-permute-start | bytes 49160 | tf_op jit(solution)/shard_map/ppermute | solution.py:112
  64.0 4.1 %collective-permute-start.3 = (f32[2,1,128]{2,1,0:T(1,128)}, f32[2,1,128]{2,1,0:T(1,128)S(1)}, u32[]{:S(2)}, u32[]{:S(2)}) collective-permute-start(f32[2,1,128]{2,1,0:T(1,128)} %shard_map.120), channel_id=1, source_target_pairs={{0,1},{1,0},{2,3},{3,2},{4,5},{5,4},{6,7},{7,6},{8,9},{9,8},{10,11... | collective-permute-start | bytes 3080 | tf_op jit(solution)/shard_map/ppermute | solution.py:22
  68.2 0.5 copy-start.2
  71.3 2.9 %collective-permute-start.7 = (f32[8,4,2,128]{3,2,1,0:T(2,128)S(1)}, f32[8,4,2,128]{3,2,1,0:T(2,128)S(1)}, u32[]{:S(2)}, u32[]{:S(2)}) collective-permute-start(f32[8,4,2,128]{3,2,1,0:T(2,128)S(1)} %pad_maximum_fusion.3), channel_id=1, source_target_pairs={{0,128},{2,130},{4,132},{6,134},{8,136},{10,138},{12,140},{14,142}... | collective-permute-start | bytes 98312 | tf_op jit(solution)/shard_map/ppermute | solution.py:112
  74.2 3.2 %collective-permute-start.8 = (f32[16,4,2,128]{3,2,1,0:T(2,128)S(1)}, f32[16,4,2,128]{3,2,1,0:T(2,128)S(1)}, u32[]{:S(2)}, u32[]{:S(2)}) collective-permute-start(f32[16,4,2,128]{3,2,1,0:T(2,128)S(1)} %pad_maximum_fusion.2), channel_id=1, source_target_pairs={{0,32},{2,34},{4,36},{6,38},{8,40},{10,42},{12,44},{14,46},{16,48}... | collective-permute-start | bytes 196616 | tf_op jit(solution)/shard_map/ppermute | solution.py:112
  77.5 4.1 %collective-permute-start.9 = (f32[32,4,2,128]{3,2,1,0:T(2,128)S(1)}, f32[32,4,2,128]{3,2,1,0:T(2,128)S(1)}, u32[]{:S(2)}, u32[]{:S(2)}) collective-permute-start(f32[32,4,2,128]{3,2,1,0:T(2,128)S(1)} %pad_maximum_fusion.1), channel_id=1, source_target_pairs={{0,4},{2,6},{4,0},{6,2},{8,12},{10,14},{12,8},{14,10},{16,20},{18,... | collective-permute-start | bytes 393224 | tf_op jit(solution)/shard_map/ppermute | solution.py:112
  79.4 19.8 %collective-permute-start.11 = (f32[2,1,128]{2,1,0:T(1,128)}, f32[2,1,128]{2,1,0:T(1,128)S(1)}, u32[]{:S(2)}, u32[]{:S(2)}) collective-permute-start(f32[2,1,128]{2,1,0:T(1,128)} %shard_map.121), channel_id=1, source_target_pairs={{0,1},{1,0},{2,3},{3,2},{4,5},{5,4},{6,7},{7,6},{8,9},{9,8},{10,11... | collective-permute-start | bytes 3080 | tf_op jit(solution)/shard_map/ppermute | solution.py:22
  81.7 9.8 %collective-permute-start.10 = (f32[64,4,2,128]{3,2,1,0:T(2,128)S(1)}, f32[64,4,2,128]{3,2,1,0:T(2,128)S(1)}, u32[]{:S(2)}, u32[]{:S(2)}) collective-permute-start(f32[64,4,2,128]{3,2,1,0:T(2,128)S(1)} %pad_maximum_fusion), channel_id=1, source_target_pairs={{0,2},{2,0},{4,6},{6,4},{8,10},{10,8},{12,14},{14,12},{16,18},{18,... | collective-permute-start | bytes 786440 | tf_op jit(solution)/shard_map/ppermute | solution.py:112
  99.2 0.5 copy-start.3
  102.4 7.2 %collective-permute-start.12 = (f32[2,1,128]{2,1,0:T(1,128)}, f32[2,1,128]{2,1,0:T(1,128)S(1)}, u32[]{:S(2)}, u32[]{:S(2)}) collective-permute-start(f32[2,1,128]{2,1,0:T(1,128)} %shard_map.124), channel_id=1, source_target_pairs={{0,1},{1,0},{2,3},{3,2},{4,5},{5,4},{6,7},{7,6},{8,9},{9,8},{10,11... | collective-permute-start | bytes 3080 | tf_op jit(solution)/shard_map/ppermute | solution.py:22
  109.6 0.6 copy-start.7
  112.7 8.9 %collective-permute-start.13 = (f32[2,1,128]{2,1,0:T(1,128)}, f32[2,1,128]{2,1,0:T(1,128)S(1)}, u32[]{:S(2)}, u32[]{:S(2)}) collective-permute-start(f32[2,1,128]{2,1,0:T(1,128)} %shard_map.126), channel_id=1, source_target_pairs={{0,1},{1,0},{2,3},{3,2},{4,5},{5,4},{6,7},{7,6},{8,9},{9,8},{10,11... | collective-permute-start | bytes 3080 | tf_op jit(solution)/shard_map/ppermute | solution.py:22
  121.6 0.5 copy-start.9
  129.5 6.4 %collective-permute-start.14 = (f32[1,4,2,128]{3,2,1,0:T(2,128)S(1)}, f32[1,4,2,128]{3,2,1,0:T(2,128)S(1)}, u32[]{:S(2)}, u32[]{:S(2)}) collective-permute-start(f32[1,4,2,128]{3,2,1,0:T(2,128)S(1)} %get-tuple-element.9), channel_id=1, source_target_pairs={{0,16},{2,18},{4,20},{6,22},{8,24},{10,26},{12,28},{14,30},{16,0},... | collective-permute-start | bytes 12296 | tf_op jit(solution)/shard_map/ppermute | solution.py:112
  135.9 4.0 %collective-permute-start.15 = (f32[2,4,2,128]{3,2,1,0:T(2,128)S(1)}, f32[2,4,2,128]{3,2,1,0:T(2,128)S(1)}, u32[]{:S(2)}, u32[]{:S(2)}) collective-permute-start(f32[2,4,2,128]{3,2,1,0:T(2,128)S(1)} %pad_maximum_fusion.10), channel_id=1, source_target_pairs={{0,64},{2,66},{4,68},{6,70},{8,72},{10,74},{12,76},{14,78},{16,80}... | collective-permute-start | bytes 24584 | tf_op jit(solution)/shard_map/ppermute | solution.py:112
  139.9 3.6 %collective-permute-start.16 = (f32[4,4,2,128]{3,2,1,0:T(2,128)S(1)}, f32[4,4,2,128]{3,2,1,0:T(2,128)S(1)}, u32[]{:S(2)}, u32[]{:S(2)}) collective-permute-start(f32[4,4,2,128]{3,2,1,0:T(2,128)S(1)} %pad_maximum_fusion.8), channel_id=1, source_target_pairs={{0,8},{2,10},{4,12},{6,14},{8,0},{10,2},{12,4},{14,6},{16,24},{18,... | collective-permute-start | bytes 49160 | tf_op jit(solution)/shard_map/ppermute | solution.py:112
  143.5 2.9 %collective-permute-start.17 = (f32[8,4,2,128]{3,2,1,0:T(2,128)S(1)}, f32[8,4,2,128]{3,2,1,0:T(2,128)S(1)}, u32[]{:S(2)}, u32[]{:S(2)}) collective-permute-start(f32[8,4,2,128]{3,2,1,0:T(2,128)S(1)} %pad_maximum_fusion.4), channel_id=1, source_target_pairs={{0,128},{2,130},{4,132},{6,134},{8,136},{10,138},{12,140},{14,142}... | collective-permute-start | bytes 98312 | tf_op jit(solution)/shard_map/ppermute | solution.py:112
  146.4 3.2 %collective-permute-start.18 = (f32[16,4,2,128]{3,2,1,0:T(2,128)S(1)}, f32[16,4,2,128]{3,2,1,0:T(2,128)S(1)}, u32[]{:S(2)}, u32[]{:S(2)}) collective-permute-start(f32[16,4,2,128]{3,2,1,0:T(2,128)S(1)} %get-tuple-element.18), channel_id=1, source_target_pairs={{0,32},{2,34},{4,36},{6,38},{8,40},{10,42},{12,44},{14,46},{16,48}... | collective-permute-start | bytes 196616 | tf_op jit(solution)/shard_map/ppermute | solution.py:112
  149.7 4.1 %collective-permute-start.19 = (f32[32,4,2,128]{3,2,1,0:T(2,128)S(1)}, f32[32,4,2,128]{3,2,1,0:T(2,128)S(1)}, u32[]{:S(2)}, u32[]{:S(2)}) collective-permute-start(f32[32,4,2,128]{3,2,1,0:T(2,128)S(1)} %get-tuple-element.14), channel_id=1, source_target_pairs={{0,4},{2,6},{4,0},{6,2},{8,12},{10,14},{12,8},{14,10},{16,20},{18,... | collective-permute-start | bytes 393224 | tf_op jit(solution)/shard_map/ppermute | solution.py:112
  153.9 8.9 %collective-permute-start.20 = (f32[64,4,2,128]{3,2,1,0:T(2,128)S(1)}, f32[64,4,2,128]{3,2,1,0:T(2,128)S(1)}, u32[]{:S(2)}, u32[]{:S(2)}) collective-permute-start(f32[64,4,2,128]{3,2,1,0:T(2,128)S(1)} %get-tuple-element.10), channel_id=1, source_target_pairs={{0,2},{2,0},{4,6},{6,4},{8,10},{10,8},{12,14},{14,12},{16,18},{18,... | collective-permute-start | bytes 786440 | tf_op jit(solution)/shard_map/ppermute | solution.py:112
